TPU v7x, 256 devices: a whole 4x4x8 slice. The times are simulated.
256 devices in a mesh: rows: 64 (over y, z, core), freq: 4 (over x).
Axes of the slice: x: 4, y: 4, z: 8, core: 2. Of those that a mesh axis runs over, the one named last changes fastest.
Arguments:
- snapshots: bfloat16 [1048576, 512], P('rows', 'freq'), may hold values from -60 to 60
- block_cols: int32 [8192, 3], P('rows'), may hold values from 0 to 8191, as said below
- mass_blocks: bfloat16 [8192, 3, 128, 128], P('rows'), may hold values from -2 to 2
- start_group: float32 [512, 32], P('freq'), may hold values from -6 to 6
- start_merge: float32 [64, 32], replicated, may hold values from -6 to 6
Outputs:
- modes: float32 [32, 1048576], P(None, ('rows', 'freq'))
Inputs may be any that keep to these rules, and one draw needn't show every extreme that they name: block_cols[b, 0] is b; the other entries lie within 2 of b, differ from b, and may repeat near the ends.
All inputs are finite; a program needn't handle non-finite values.
Results may differ from a plain program's by a relative error of at most 0.0003.
Values may be sent and summed in bfloat16 or wider, within the bound.
No kernel may reach another device: no remote copies, remote signals or barrier semaphores. Data moves between devices by JAX's collectives and lax.ppermute only.
A program may use at most 128 MiB of HBM per device.

v0:
```python
import jax
import jax.numpy as jnp
from jax import lax
from jax.sharding import PartitionSpec as P
from jax.experimental import pallas as pl
from jax.experimental.pallas import tpu as pltpu

HB = 2
POWER = 2


HIGHEST = lax.Precision.HIGHEST


def extended_2(block, sides, width):
    for axis, dim in sides:
        count = lax.axis_size(axis)
        forward = [(i, i + 1) for i in range(count - 1)]
        backward = [(target, source) for source, target in forward]
        low = lax.ppermute(
            lax.slice_in_dim(block, block.shape[dim] - width, None, axis=dim), axis, forward
        )
        high = lax.ppermute(lax.slice_in_dim(block, 0, width, axis=dim), axis, backward)
        block = jnp.concatenate([low, block, high], axis=dim)
    return block


ROWS_PER_STEP = 16


def mass_kernel(index_ref, low_ref, own_ref, high_ref, mass_ref, out_ref, gram_ref):
    step = pl.program_id(0)
    size = mass_ref.shape[2]
    halo = low_ref.shape[0] // size
    own_tiles = own_ref.shape[0] // size
    rows_here = mass_ref.shape[0]
    kb = mass_ref.shape[1]

    @pl.when(step == 0)
    def _():
        gram_ref[...] = jnp.zeros(gram_ref.shape, gram_ref.dtype)

    for row in range(rows_here):
        block = step * rows_here + row
        total = jnp.zeros((size, out_ref.shape[1]), jnp.float32)
        for k in range(kb):
            tile_id = index_ref[block * kb + k]
            own_at = jnp.clip(tile_id - halo, 0, own_tiles - 1)
            low_at = jnp.clip(tile_id, 0, halo - 1)
            high_at = jnp.clip(tile_id - halo - own_tiles, 0, halo - 1)
            own_tile = own_ref[pl.ds(pl.multiple_of(own_at * size, size), size), :]
            low_tile = low_ref[pl.ds(pl.multiple_of(low_at * size, size), size), :]
            high_tile = high_ref[pl.ds(pl.multiple_of(high_at * size, size), size), :]
            tile = jnp.where(
                tile_id < halo, low_tile, jnp.where(tile_id >= halo + own_tiles, high_tile, own_tile)
            )
            total = total + jnp.dot(mass_ref[row, k], tile, preferred_element_type=jnp.float32)
        out_ref[row * size : (row + 1) * size, :] = total

    chunk = out_ref[...]
    high_part = chunk.astype(jnp.bfloat16)
    low_part = (chunk - high_part.astype(jnp.float32)).astype(jnp.bfloat16)
    dims = (((0,), (0,)), ((), ()))
    main = lax.dot_general(high_part, high_part, dims, preferred_element_type=jnp.float32)
    cross = lax.dot_general(high_part, low_part, dims, preferred_element_type=jnp.float32)
    gram_ref[...] += main + (cross + cross.T)


def apply_mass(low, own, high, mass_blocks, tile_index):
    blocks, kb, size, _ = mass_blocks.shape
    cols = own.shape[1]
    per = ROWS_PER_STEP
    grid_spec = pltpu.PrefetchScalarGridSpec(
        num_scalar_prefetch=1,
        grid=(blocks // per,),
        in_specs=[
            pl.BlockSpec(low.shape, lambda i, idx: (0, 0)),
            pl.BlockSpec(own.shape, lambda i, idx: (0, 0)),
            pl.BlockSpec(high.shape, lambda i, idx: (0, 0)),
            pl.BlockSpec((per, kb, size, size), lambda i, idx: (i, 0, 0, 0)),
        ],
        out_specs=[
            pl.BlockSpec((per * size, cols), lambda i, idx: (i, 0)),
            pl.BlockSpec((cols, cols), lambda i, idx: (0, 0)),
        ],
    )
    return pl.pallas_call(
        mass_kernel,
        grid_spec=grid_spec,
        out_shape=[
            jax.ShapeDtypeStruct((blocks * size, cols), jnp.float32),
            jax.ShapeDtypeStruct((cols, cols), jnp.float32),
        ],
        compiler_params=pltpu.CompilerParams(dimension_semantics=("arbitrary",)),
    )(tile_index.reshape(-1), low, own, high, mass_blocks)


def butterfly_sum(x, axes):
    for axis in axes:
        count = lax.axis_size(axis)
        step = 1
        while step < count:
            pairs = [(i, i ^ step) for i in range(count)]
            x = x + lax.ppermute(x, axis, pairs)
            step *= 2
    return x


def orthonormal(columns_block):
    inner_gram = jnp.dot(columns_block.T, columns_block, precision=HIGHEST)
    lower_factor = jnp.linalg.cholesky(inner_gram)
    return lax.linalg.triangular_solve(
        lower_factor, columns_block, left_side=False, lower=True, transpose_a=True
    )


def subspace(gram_matrix, start_block):
    current = start_block
    for repeat in range(POWER):
        current = orthonormal(jnp.dot(gram_matrix, current, precision=HIGHEST))
    return current


def coefficient_tree(full_gram, start_merge, rank_size, freq_count):
    pairs = freq_count // 2
    width = 2 * rank_size
    blocks = jnp.stack(
        [full_gram[p * width : (p + 1) * width, p * width : (p + 1) * width] for p in range(pairs)]
    )
    pair_weights = jax.vmap(subspace, in_axes=(0, None))(blocks, start_merge)
    zero = jnp.zeros((width, rank_size), jnp.float32)
    coefficients = []
    for p in range(pairs):
        parts = [zero] * pairs
        parts[p] = pair_weights[p]
        coefficients.append(jnp.concatenate(parts, axis=0))
    while len(coefficients) > 1:
        merged = []
        for position in range(0, len(coefficients), 2):
            joined = jnp.concatenate([coefficients[position], coefficients[position + 1]], axis=1)
            pair_gram = jnp.dot(
                joined.T, jnp.dot(full_gram, joined, precision=HIGHEST), precision=HIGHEST
            )
            merged.append(jnp.dot(joined, subspace(pair_gram, start_merge), precision=HIGHEST))
        coefficients = merged
    return coefficients[0]


def shards(snapshots, block_cols, mass_blocks, start_group, start_merge):
    block_size = mass_blocks.shape[2]
    local_blocks = block_cols.shape[0]
    local_cols = snapshots.shape[1]
    total_rows = lax.axis_size("rows") * snapshots.shape[0]
    width = HB * block_size
    count = lax.axis_size("rows")
    forward = [(i, i + 1) for i in range(count - 1)]
    backward = [(target, source) for source, target in forward]
    low = lax.ppermute(snapshots[snapshots.shape[0] - width :], "rows", forward)
    high = lax.ppermute(snapshots[:width], "rows", backward)
    local_index = block_cols - lax.axis_index("rows") * local_blocks + HB
    weighted, local_gram = apply_mass(low, snapshots, high, mass_blocks, local_index)
    group_gram = butterfly_sum(local_gram, ("rows",)) / total_rows
    weights = subspace(group_gram, start_group)
    modes = lax.dot_general(weights, weighted, (((0,), (1,)), ((), ())), precision=HIGHEST)
    rank_size = modes.shape[0]
    freq_count = lax.axis_size("freq")
    group = lax.axis_index("freq")
    share = modes.shape[1] // freq_count
    received = [lax.dynamic_slice_in_dim(modes, group * share, share, 1)]
    for shift in range(1, freq_count):
        piece = lax.dynamic_slice_in_dim(modes, ((group + shift) % freq_count) * share, share, 1)
        pairs = [(i, (i + shift) % freq_count) for i in range(freq_count)]
        received.append(lax.ppermute(piece, "freq", pairs))
    stacked = jnp.concatenate(received, axis=0)
    source = (group - jnp.arange(freq_count)) % freq_count
    local_full = jnp.dot(stacked, stacked.T, precision=HIGHEST)
    blocked = local_full.reshape(freq_count, rank_size, freq_count, rank_size)
    blocked = jnp.take(jnp.take(blocked, source, axis=0), source, axis=2)
    full_gram = butterfly_sum(
        blocked.reshape(freq_count * rank_size, freq_count * rank_size), ("rows", "freq")
    ) / total_rows
    combined = coefficient_tree(full_gram, start_merge, rank_size, freq_count)
    shifted = jnp.take(combined.reshape(freq_count, rank_size, rank_size), source, axis=0)
    result = jnp.dot(shifted.reshape(freq_count * rank_size, rank_size).T, stacked, precision=HIGHEST)
    return result


def solution(mesh):
    in_specs = (
        P("rows", "freq"),
        P("rows", None),
        P("rows", None, None, None),
        P("freq", None),
        P(),
    )
    out_specs = P(None, ("rows", "freq"))
    return jax.shard_map(shards, mesh=mesh, in_specs=in_specs, out_specs=out_specs, check_vma=False)
```

profile of v0, /device:TPU:32, one launch (start us, length us, event | category | flops | bytes accessed | tf_op | source)
XLA Modules:
  0.0 199.1 jit_solution(11878958236142302705)
XLA Ops:
  2.8 3.6 %collective-permute-start.1 = (bf16[256,128]{1,0:T(8,128)(2,1)S(1)}, bf16[256,128]{1,0:T(8,128)(2,1)S(1)}, u32[]{:S(2)}, u32[]{:S(2)}) collective-permute-start(bf16[256,128]{1,0:T(8,128)(2,1)S(1)} %get-tuple-element.14), channel_id=1, source_target_pairs={{4,0},{8,4},{12,8},{16,12},{20,16},{24,20},{28,24},{32,28},{36,32}... | collective-permute-start | bytes 196616 | tf_op jit(solution)/shard_map/ppermute | solution.py:159
  9.3 14.6 %shard_map.55 = (f32[16384,128]{1,0:T(8,128)}, f32[128,128]{1,0:T(8,128)}) custom-call(s32[384]{0:T(512)} %reshape.98.index_ref, bf16[256,128]{1,0:T(8,128)(2,1)} %copy-done.1, bf16[16384,128]{1,0:T(8,128)(2,1)} %own_ref.1, bf16[256,128]{1,0:T(8,128)(2,1)} %copy-done.2, bf16[128,3,128,128]{3,2,1,0:T(8,128)(2,1)} %mass_ref.1), custom_call_target="tpu_custom_call" | custom-call | tf_op jit(solution)/shard_map/pallas_call | solution.py:87
  27.8 4.2 %collective-permute-done.3 = f32[128,128]{1,0:T(8,128)S(1)} collective-permute-done((f32[128,128]{1,0:T(8,128)S(1)}, f32[128,128]{1,0:T(8,128)S(1)}, u32[]{:S(2)}, u32[]{:S(2)}) %collective-permute-start.3) | collective-permute-done | bytes 65568 | tf_op jit(solution)/shard_map/ppermute | solution.py:104
  32.1 5.8 %collective-permute-start.4 = (f32[128,128]{1,0:T(8,128)S(1)}, f32[128,128]{1,0:T(8,128)S(1)}, u32[]{:S(2)}, u32[]{:S(2)}) collective-permute-start(f32[128,128]{1,0:T(8,128)S(1)} %add.141), channel_id=1, source_target_pairs={{0,16},{4,20},{8,24},{12,28},{16,0},{20,4},{24,8},{28,12},{32,48},... | collective-permute-start | bytes 196616 | tf_op jit(solution)/shard_map/ppermute | solution.py:104
  42.9 5.7 %collective-permute-done.5 = f32[128,128]{1,0:T(8,128)S(1)} collective-permute-done((f32[128,128]{1,0:T(8,128)S(1)}, f32[128,128]{1,0:T(8,128)S(1)}, u32[]{:S(2)}, u32[]{:S(2)}) %collective-permute-start.5) | collective-permute-done | bytes 65568 | tf_op jit(solution)/shard_map/ppermute | solution.py:104
  52.9 3.7 %collective-permute-start.7 = (f32[128,128]{1,0:T(8,128)S(1)}, f32[128,128]{1,0:T(8,128)S(1)}, u32[]{:S(2)}, u32[]{:S(2)}) collective-permute-start(f32[128,128]{1,0:T(8,128)S(1)} %add.144), channel_id=1, source_target_pairs={{0,128},{4,132},{8,136},{12,140},{16,144},{20,148},{24,152},{28,15... | collective-permute-start | bytes 196616 | tf_op jit(solution)/shard_map/ppermute | solution.py:104
  59.3 2.9 %cholesky.117 = f32[32,32]{1,0:T(8,128)S(1)} custom-call(f32[32,32]{1,0:T(8,128)S(1)} %fusion.22), custom_call_target="Cholesky" | custom-call | tf_op jit(solution)/shard_map/jit(cholesky)/cholesky | solution.py:111
  66.7 2.9 %cholesky.128 = f32[32,32]{1,0:T(8,128)S(1)} custom-call(f32[32,32]{1,0:T(8,128)S(1)} %fusion.20), custom_call_target="Cholesky" | custom-call | tf_op jit(solution)/shard_map/jit(cholesky)/cholesky | solution.py:111
  73.7 10.7 %fusion.51 = f32[32,16384]{1,0:T(8,128)S(1)} fusion(f32[128,32]{0,1:T(8,128)S(1)} %convolution_bitcast_fusion.4, f32[16384,128]{1,0:T(8,128)} %get-tuple-element.12), kind=kOutput, calls=%fused_computation.113 | convolution fusion | flops 805306368 | bytes 10502144 | tf_op jit(solution)/shard_map/dot_general | solution.py:164
  89.9 15.3 %collective-permute-done.10 = f32[32,4096]{1,0:T(8,128)S(1)} collective-permute-done((f32[32,4096]{1,0:T(8,128)S(1)}, f32[32,4096]{1,0:T(8,128)S(1)}, u32[]{:S(2)}, u32[]{:S(2)}) %collective-permute-start.10) | collective-permute-done | bytes 524320 | tf_op jit(solution)/shard_map/ppermute | solution.py:173
  105.2 3.4 %collective-permute-done.8 = f32[32,4096]{1,0:T(8,128)S(1)} collective-permute-done((f32[32,4096]{1,0:T(8,128)S(1)}, f32[32,4096]{1,0:T(8,128)S(1)}, u32[]{:S(2)}, u32[]{:S(2)}) %collective-permute-start.8) | collective-permute-done | bytes 524320 | tf_op jit(solution)/shard_map/ppermute | solution.py:173
  108.6 3.0 %fusion.1 = f32[128,128]{1,0:T(8,128)S(1)} fusion(f32[32,4096]{1,0:T(8,128)S(1)} %collective-permute-done.10, f32[32,4096]{1,0:T(8,128)} %collective-permute-done.9, f32[32,4096]{1,0:T(8,128)S(1)} %collective-permute-done.8, f32[32,4096]{1,0:T(8,128)S(1)} %get-tuple-element.16), kind=kOutput, calls=%fused_computation.5 | convolution fusion | flops 806879232 | bytes 2162688 | tf_op jit(solution)/shard_map/dot_general | solution.py:176
  115.5 3.6 %collective-permute-done.12 = f32[128,128]{1,0:T(8,128)S(1)} collective-permute-done((f32[128,128]{1,0:T(8,128)S(1)}, f32[128,128]{1,0:T(8,128)S(1)}, u32[]{:S(2)}, u32[]{:S(2)}) %collective-permute-start.12) | collective-permute-done | bytes 65568 | tf_op jit(solution)/shard_map/ppermute | solution.py:104
  119.1 5.3 %collective-permute-start.13 = (f32[128,128]{1,0:T(8,128)S(1)}, f32[128,128]{1,0:T(8,128)S(1)}, u32[]{:S(2)}, u32[]{:S(2)}) collective-permute-start(f32[128,128]{1,0:T(8,128)S(1)} %add.159), channel_id=1, source_target_pairs={{0,16},{4,20},{8,24},{12,28},{16,0},{20,4},{24,8},{28,12},{32,48},... | collective-permute-start | bytes 196616 | tf_op jit(solution)/shard_map/ppermute | solution.py:104
  126.8 8.8 %collective-permute-done.14 = f32[128,128]{1,0:T(8,128)S(1)} collective-permute-done((f32[128,128]{1,0:T(8,128)S(1)}, f32[128,128]{1,0:T(8,128)S(1)}, u32[]{:S(2)}, u32[]{:S(2)}) %collective-permute-start.14) | collective-permute-done | bytes 65568 | tf_op jit(solution)/shard_map/ppermute | solution.py:104
  136.4 3.6 %collective-permute-done.15 = f32[128,128]{1,0:T(8,128)S(1)} collective-permute-done((f32[128,128]{1,0:T(8,128)S(1)}, f32[128,128]{1,0:T(8,128)S(1)}, u32[]{:S(2)}, u32[]{:S(2)}) %collective-permute-start.15) | collective-permute-done | bytes 65568 | tf_op jit(solution)/shard_map/ppermute | solution.py:104
  142.7 3.1 %collective-permute-done.16 = f32[128,128]{1,0:T(8,128)S(1)} collective-permute-done((f32[128,128]{1,0:T(8,128)S(1)}, f32[128,128]{1,0:T(8,128)S(1)}, u32[]{:S(2)}, u32[]{:S(2)}) %collective-permute-start.16) | collective-permute-done | bytes 65568 | tf_op jit(solution)/shard_map/ppermute | solution.py:104
  146.0 4.2 %collective-permute-done.17 = f32[128,128]{1,0:T(8,128)S(1)} collective-permute-done((f32[128,128]{1,0:T(8,128)S(1)}, f32[128,128]{1,0:T(8,128)S(1)}, u32[]{:S(2)}, u32[]{:S(2)}) %collective-permute-start.17) | collective-permute-done | bytes 65568 | tf_op jit(solution)/shard_map/ppermute | solution.py:104
  151.0 5.1 %collective-permute-done.18 = f32[128,128]{1,0:T(8,128)S(1)} collective-permute-done((f32[128,128]{1,0:T(8,128)S(1)}, f32[128,128]{1,0:T(8,128)S(1)}, u32[]{:S(2)}, u32[]{:S(2)}) %collective-permute-start.18) | collective-permute-done | bytes 65568 | tf_op jit(solution)/shard_map/ppermute | solution.py:104
  156.8 5.9 %custom-call.20 = f32[2,32,32]{2,1,0:T(8,128)S(1)} custom-call(f32[2,32,32]{2,1,0:T(8,128)S(1)} %fusion.7), custom_call_target="Cholesky" | custom-call | tf_op jit(solution)/shard_map/vmap(jit(cholesky))/cholesky | solution.py:111
  162.8 4.9 %custom-call.21 = f32[2,1,32,32]{2,3,1,0:T(8,128)S(1)} custom-call(f32[2,1,32,32]{3,2,1,0:T(8,128)S(1)} %select_bitcast_fusion.1), custom_call_target="InvertDiagBlocksLowerTriangular" | custom-call | tf_op jit(solution)/shard_map/vmap()/triangular_solve/custom-call.3 | solution.py:112
  168.5 5.9 %custom-call.22 = f32[2,32,32]{2,1,0:T(8,128)S(1)} custom-call(f32[2,32,32]{2,1,0:T(8,128)S(1)} %fusion.5), custom_call_target="Cholesky" | custom-call | tf_op jit(solution)/shard_map/vmap(jit(cholesky))/cholesky | solution.py:111
  174.6 4.9 %custom-call.23 = f32[2,1,32,32]{2,3,1,0:T(8,128)S(1)} custom-call(f32[2,1,32,32]{3,2,1,0:T(8,128)S(1)} %select_bitcast_fusion), custom_call_target="InvertDiagBlocksLowerTriangular" | custom-call | tf_op jit(solution)/shard_map/vmap()/triangular_solve/custom-call.3 | solution.py:112
  196.0 3.0 %fusion = f32[32,4096]{1,0:T(8,128)} fusion(f32[128,32]{1,0:T(8,128)S(1)} %bitcast_select_fusion, f32[32,4096]{1,0:T(8,128)S(1)} %collective-permute-done.10, f32[32,4096]{1,0:T(8,128)} %collective-permute-done.9, f32[32,4096]{1,0:T(8,128)S(1)} %collective-permute-done.8, f32[32,4096]{1,0:T(8,128)S(1)} %get-tuple-element.16), kind=kOutput, calls=%fused_computation.4 | convolution fusion | flops 202899456 | bytes 2637824 | tf_op jit(solution)/shard_map/dot_general | solution.py:184
  (126 shorter events, 64.4 us)
Async XLA Ops:
  0.0 156.2 %copy-start = (f32[64,32]{0,1:T(8,128)S(1)}, f32[64,32]{0,1:T(8,128)}, u32[]{:S(2)}) copy-start(f32[64,32]{0,1:T(8,128)} %param.17) | copy-start | bytes 24580
  0.9 7.2 %collective-permute-start = (bf16[256,128]{1,0:T(8,128)(2,1)S(1)}, bf16[256,128]{1,0:T(8,128)(2,1)S(1)}, u32[]{:S(2)}, u32[]{:S(2)}) collective-permute-start(bf16[256,128]{1,0:T(8,128)(2,1)S(1)} %get-tuple-element.15), channel_id=1, source_target_pairs={{0,4},{4,8},{8,12},{12,16},{16,20},{20,24},{24,28},{28,32},{32,36}... | collective-permute-start | bytes 196616 | tf_op jit(solution)/shard_map/ppermute | solution.py:158
  2.8 5.5 %collective-permute-start.1 = (bf16[256,128]{1,0:T(8,128)(2,1)S(1)}, bf16[256,128]{1,0:T(8,128)(2,1)S(1)}, u32[]{:S(2)}, u32[]{:S(2)}) collective-permute-start(bf16[256,128]{1,0:T(8,128)(2,1)S(1)} %get-tuple-element.14), channel_id=1, source_target_pairs={{4,0},{8,4},{12,8},{16,12},{20,16},{24,20},{28,24},{32,28},{36,32}... | collective-permute-start | bytes 196616 | tf_op jit(solution)/shard_map/ppermute | solution.py:159
  8.1 50.8 %copy-start.3 = (f32[128,32]{0,1:T(8,128)S(1)}, f32[128,32]{0,1:T(8,128)}, u32[]{:S(2)}) copy-start(f32[128,32]{0,1:T(8,128)} %param.16) | copy-start | bytes 49156
  8.1 0.6 copy-start.1
  8.7 0.6 copy-start.2
  23.9 2.8 %collective-permute-start.2 = (f32[128,128]{1,0:T(8,128)}, f32[128,128]{1,0:T(8,128)S(1)}, u32[]{:S(2)}, u32[]{:S(2)}) collective-permute-start(f32[128,128]{1,0:T(8,128)} %get-tuple-element.10), channel_id=1, source_target_pairs={{0,4},{4,0},{8,12},{12,8},{16,20},{20,16},{24,28},{28,24},{32,36},... | collective-permute-start | bytes 196616 | tf_op jit(solution)/shard_map/ppermute | solution.py:104
  27.6 4.4 %collective-permute-start.3 = (f32[128,128]{1,0:T(8,128)S(1)}, f32[128,128]{1,0:T(8,128)S(1)}, u32[]{:S(2)}, u32[]{:S(2)}) collective-permute-start(f32[128,128]{1,0:T(8,128)S(1)} %add.140), channel_id=1, source_target_pairs={{0,8},{4,12},{8,0},{12,4},{16,24},{20,28},{24,16},{28,20},{32,40},... | collective-permute-start | bytes 196616 | tf_op jit(solution)/shard_map/ppermute | solution.py:104
  32.1 8.2 %collective-permute-start.4 = (f32[128,128]{1,0:T(8,128)S(1)}, f32[128,128]{1,0:T(8,128)S(1)}, u32[]{:S(2)}, u32[]{:S(2)}) collective-permute-start(f32[128,128]{1,0:T(8,128)S(1)} %add.141), channel_id=1, source_target_pairs={{0,16},{4,20},{8,24},{12,28},{16,0},{20,4},{24,8},{28,12},{32,48},... | collective-permute-start | bytes 196616 | tf_op jit(solution)/shard_map/ppermute | solution.py:104
  40.3 8.3 %collective-permute-start.5 = (f32[128,128]{1,0:T(8,128)S(1)}, f32[128,128]{1,0:T(8,128)S(1)}, u32[]{:S(2)}, u32[]{:S(2)}) collective-permute-start(f32[128,128]{1,0:T(8,128)S(1)} %add.142), channel_id=1, source_target_pairs={{0,32},{4,36},{8,40},{12,44},{16,48},{20,52},{24,56},{28,60},{32,0... | collective-permute-start | bytes 196616 | tf_op jit(solution)/shard_map/ppermute | solution.py:104
  48.6 4.4 %collective-permute-start.6 = (f32[128,128]{1,0:T(8,128)S(1)}, f32[128,128]{1,0:T(8,128)S(1)}, u32[]{:S(2)}, u32[]{:S(2)}) collective-permute-start(f32[128,128]{1,0:T(8,128)S(1)} %add.143), channel_id=1, source_target_pairs={{0,64},{4,68},{8,72},{12,76},{16,80},{20,84},{24,88},{28,92},{32,9... | collective-permute-start | bytes 196616 | tf_op jit(solution)/shard_map/ppermute | solution.py:104
  52.9 5.9 %collective-permute-start.7 = (f32[128,128]{1,0:T(8,128)S(1)}, f32[128,128]{1,0:T(8,128)S(1)}, u32[]{:S(2)}, u32[]{:S(2)}) collective-permute-start(f32[128,128]{1,0:T(8,128)S(1)} %add.144), channel_id=1, source_target_pairs={{0,128},{4,132},{8,136},{12,140},{16,144},{20,148},{24,152},{28,15... | collective-permute-start | bytes 196616 | tf_op jit(solution)/shard_map/ppermute | solution.py:104
  84.5 20.6 %collective-permute-start.10 = (f32[32,4096]{1,0:T(8,128)S(1)}, f32[32,4096]{1,0:T(8,128)S(1)}, u32[]{:S(2)}, u32[]{:S(2)}) collective-permute-start(f32[32,4096]{1,0:T(8,128)S(1)} %get-tuple-element.17), channel_id=1, source_target_pairs={{0,3},{1,0},{2,1},{3,2},{4,7},{5,4},{6,5},{7,6},{8,11},{9,8},{10,9... | collective-permute-start | bytes 1572872 | tf_op jit(solution)/shard_map/ppermute | solution.py:173
  87.4 21.2 %collective-permute-start.8 = (f32[32,4096]{1,0:T(8,128)S(1)}, f32[32,4096]{1,0:T(8,128)S(1)}, u32[]{:S(2)}, u32[]{:S(2)}) collective-permute-start(f32[32,4096]{1,0:T(8,128)S(1)} %get-tuple-element.19), channel_id=1, source_target_pairs={{0,1},{1,2},{2,3},{3,0},{4,5},{5,6},{6,7},{7,4},{8,9},{9,10},{10,1... | collective-permute-start | bytes 1572872 | tf_op jit(solution)/shard_map/ppermute | solution.py:173
  87.4 21.2 %collective-permute-start.9 = (f32[32,4096]{1,0:T(8,128)S(1)}, f32[32,4096]{1,0:T(8,128)}, u32[]{:S(2)}, u32[]{:S(2)}) collective-permute-start(f32[32,4096]{1,0:T(8,128)S(1)} %get-tuple-element.18), channel_id=1, source_target_pairs={{0,2},{1,3},{2,0},{3,1},{4,6},{5,7},{6,4},{7,5},{8,10},{9,11},{10,... | collective-permute-start | bytes 1572872 | tf_op jit(solution)/shard_map/ppermute | solution.py:173
  113.4 1.3 collective-permute-start.11
  114.7 4.4 %collective-permute-start.12 = (f32[128,128]{1,0:T(8,128)S(1)}, f32[128,128]{1,0:T(8,128)S(1)}, u32[]{:S(2)}, u32[]{:S(2)}) collective-permute-start(f32[128,128]{1,0:T(8,128)S(1)} %fusion.89), channel_id=1, source_target_pairs={{0,8},{4,12},{8,0},{12,4},{16,24},{20,28},{24,16},{28,20},{32,40},... | collective-permute-start | bytes 196616 | tf_op jit(solution)/shard_map/ppermute | solution.py:104
  119.1 7.6 %collective-permute-start.13 = (f32[128,128]{1,0:T(8,128)S(1)}, f32[128,128]{1,0:T(8,128)S(1)}, u32[]{:S(2)}, u32[]{:S(2)}) collective-permute-start(f32[128,128]{1,0:T(8,128)S(1)} %add.159), channel_id=1, source_target_pairs={{0,16},{4,20},{8,24},{12,28},{16,0},{20,4},{24,8},{28,12},{32,48},... | collective-permute-start | bytes 196616 | tf_op jit(solution)/shard_map/ppermute | solution.py:104
  126.7 8.9 %collective-permute-start.14 = (f32[128,128]{1,0:T(8,128)S(1)}, f32[128,128]{1,0:T(8,128)S(1)}, u32[]{:S(2)}, u32[]{:S(2)}) collective-permute-start(f32[128,128]{1,0:T(8,128)S(1)} %add.160), channel_id=1, source_target_pairs={{0,32},{4,36},{8,40},{12,44},{16,48},{20,52},{24,56},{28,60},{32,0... | collective-permute-start | bytes 196616 | tf_op jit(solution)/shard_map/ppermute | solution.py:104
  135.6 4.4 %collective-permute-start.15 = (f32[128,128]{1,0:T(8,128)S(1)}, f32[128,128]{1,0:T(8,128)S(1)}, u32[]{:S(2)}, u32[]{:S(2)}) collective-permute-start(f32[128,128]{1,0:T(8,128)S(1)} %add.161), channel_id=1, source_target_pairs={{0,64},{4,68},{8,72},{12,76},{16,80},{20,84},{24,88},{28,92},{32,9... | collective-permute-start | bytes 196616 | tf_op jit(solution)/shard_map/ppermute | solution.py:104
  140.0 5.9 %collective-permute-start.16 = (f32[128,128]{1,0:T(8,128)S(1)}, f32[128,128]{1,0:T(8,128)S(1)}, u32[]{:S(2)}, u32[]{:S(2)}) collective-permute-start(f32[128,128]{1,0:T(8,128)S(1)} %add.162), channel_id=1, source_target_pairs={{0,128},{4,132},{8,136},{12,140},{16,144},{20,148},{24,152},{28,15... | collective-permute-start | bytes 196616 | tf_op jit(solution)/shard_map/ppermute | solution.py:104
  145.9 4.4 %collective-permute-start.17 = (f32[128,128]{1,0:T(8,128)S(1)}, f32[128,128]{1,0:T(8,128)S(1)}, u32[]{:S(2)}, u32[]{:S(2)}) collective-permute-start(f32[128,128]{1,0:T(8,128)S(1)} %add.163), channel_id=1, source_target_pairs={{0,1},{1,0},{2,3},{3,2},{4,5},{5,4},{6,7},{7,6},{8,9},{9,8},{10,11... | collective-permute-start | bytes 196616 | tf_op jit(solution)/shard_map/ppermute | solution.py:104
  150.2 5.9 %collective-permute-start.18 = (f32[128,128]{1,0:T(8,128)S(1)}, f32[128,128]{1,0:T(8,128)S(1)}, u32[]{:S(2)}, u32[]{:S(2)}) collective-permute-start(f32[128,128]{1,0:T(8,128)S(1)} %add.164), channel_id=1, source_target_pairs={{0,2},{1,3},{2,0},{3,1},{4,6},{5,7},{6,4},{7,5},{8,10},{9,11},{10,... | collective-permute-start | bytes 196616 | tf_op jit(solution)/shard_map/ppermute | solution.py:104
where the time goes:
time: 200 us; the launch traced here: 199 us
  waiting for transfers between devices  69.3 us (35%)
  other arithmetic  50.7 us (25%)
  starting transfers between devices  36.9 us (18%)
  matrix products  21.2 us (11%)
  Pallas kernels  14.6 us (7%)
  local copies, waits for them, and re-layouts  5.85 us (3%)
    ppermute x14, waiting for transfers between devices, butterfly_sum(): x = x + lax.ppermute(x, axis, pairs)  50.3 us
    another operation x19, other arithmetic, orthonormal(): lower_factor = jnp.linalg.cholesky(inner_gram)  26.4 us
    ppermute x14, starting transfers between devices, butterfly_sum(): x = x + lax.ppermute(x, axis, pairs)  26.2 us
    another operation x13, other arithmetic, orthonormal(): lax.linalg.triangular_solve(lower_factor, columns_block, left_side=False,...  22.3 us
    ppermute x3, waiting for transfers between devices, shards(): received.append(lax.ppermute(piece, 'freq', pairs))  18.7 us
    pallas_call x1, Pallas kernels, apply_mass(): pl.pallas_call(mass_kernel, grid_spec=grid_spec, out_shape=[jax.ShapeDtyp...  14.6 us
    dot_general x1, matrix products, shards(): lax.dot_general(weights, weighted, (((0,), (1,)), ((), ())), precision=HI...  10.7 us
    ppermute x3, starting transfers between devices, shards(): received.append(lax.ppermute(piece, 'freq', pairs))  5.14 us
  transfers between devices with their start and end apart: 19, of which 17 were waited for; matrix products, arithmetic and copies ran while one was open for 1% of the time, Pallas kernels for 0%

commit v1 on v0

--- a/solution.py
+++ b/solution.py
@@ -10,6 +10,7 @@
 
 
 HIGHEST = lax.Precision.HIGHEST
+HIGH = lax.Precision.HIGH
 
 
 def extended_2(block, sides, width):
@@ -100,9 +101,19 @@
         count = lax.axis_size(axis)
         step = 1
         while step < count:
-            pairs = [(i, i ^ step) for i in range(count)]
-            x = x + lax.ppermute(x, axis, pairs)
-            step *= 2
+            if step * 4 <= count:
+                parts = [x]
+                for mask in (1, 2, 3):
+                    pairs = [
+                        (i, (i & ~(3 * step)) | ((((i // step) & 3) ^ mask) * step))
+                        for i in range(count)
+                    ]
+                    parts.append(lax.ppermute(x, axis, pairs))
+                x = (parts[0] + parts[1]) + (parts[2] + parts[3])
+                step *= 4
+            else:
+                x = x + lax.ppermute(x, axis, [(i, i ^ step) for i in range(count)])
+                step *= 2
     return x
 
 
@@ -161,7 +172,7 @@
     weighted, local_gram = apply_mass(low, snapshots, high, mass_blocks, local_index)
     group_gram = butterfly_sum(local_gram, ("rows",)) / total_rows
     weights = subspace(group_gram, start_group)
-    modes = lax.dot_general(weights, weighted, (((0,), (1,)), ((), ())), precision=HIGHEST)
+    modes = lax.dot_general(weights, weighted, (((0,), (1,)), ((), ())), precision=HIGH)
     rank_size = modes.shape[0]
     freq_count = lax.axis_size("freq")
     group = lax.axis_index("freq")
@@ -173,7 +184,7 @@
         received.append(lax.ppermute(piece, "freq", pairs))
     stacked = jnp.concatenate(received, axis=0)
     source = (group - jnp.arange(freq_count)) % freq_count
-    local_full = jnp.dot(stacked, stacked.T, precision=HIGHEST)
+    local_full = jnp.dot(stacked, stacked.T, precision=HIGH)
     blocked = local_full.reshape(freq_count, rank_size, freq_count, rank_size)
     blocked = jnp.take(jnp.take(blocked, source, axis=0), source, axis=2)
     full_gram = butterfly_sum(
@@ -181,7 +192,7 @@
     ) / total_rows
     combined = coefficient_tree(full_gram, start_merge, rank_size, freq_count)
     shifted = jnp.take(combined.reshape(freq_count, rank_size, rank_size), source, axis=0)
-    result = jnp.dot(shifted.reshape(freq_count * rank_size, rank_size).T, stacked, precision=HIGHEST)
+    result = jnp.dot(shifted.reshape(freq_count * rank_size, rank_size).T, stacked, precision=HIGH)
     return result
 
 

time: 200 us -> 189 us (0.945)
  waiting for transfers between devices: 69.3 us -> 54.6 us
  starting transfers between devices: 36.9 us -> 46.8 us
  matrix products: 21.2 us -> 15.9 us
    ppermute x14 -> x21, waiting for transfers between devices: 50.3 us -> 34.3 us  [butterfly_sum(): parts.append(lax.ppermute(x, axis, pairs))]
    ppermute x14 -> x21, starting transfers between devices: 26.2 us -> 35.5 us  [butterfly_sum(): parts.append(lax.ppermute(x, axis, pairs))]
    dot_general x2, matrix products: 13.7 us -> 8.78 us  [the longest x1 6.5 us: shards(): lax.dot_general(weights, weighted, (((0,), (1,)), ((), ())), precision=HIGH)]
  transfers between devices with their start and end apart: 19 -> 26, of which waited for: 17 -> 19; matrix products, arithmetic and copies ran while one was open for 1% -> 1% of each run, Pallas kernels for 0% -> 0%
where the time goes in v1:
time: 189 us
  waiting for transfers between devices  54.6 us (29%)
  other arithmetic  50.7 us (27%)
  starting transfers between devices  46.8 us (25%)
  matrix products  15.9 us (8%)
  Pallas kernels  14.6 us (8%)
  local copies, waits for them, and re-layouts  5.88 us (3%)
    ppermute x21, starting transfers between devices, butterfly_sum(): parts.append(lax.ppermute(x, axis, pairs))  35.5 us
    ppermute x21, waiting for transfers between devices, butterfly_sum(): parts.append(lax.ppermute(x, axis, pairs))  34.3 us
    another operation x19, other arithmetic, orthonormal(): lower_factor = jnp.linalg.cholesky(inner_gram)  26.4 us
    another operation x13, other arithmetic, orthonormal(): lax.linalg.triangular_solve(lower_factor, columns_block, left_side=False,...  22.3 us
    ppermute x3, waiting for transfers between devices, shards(): received.append(lax.ppermute(piece, 'freq', pairs))  19.9 us
    pallas_call x1, Pallas kernels, apply_mass(): pl.pallas_call(mass_kernel, grid_spec=grid_spec, out_shape=[jax.ShapeDtyp...  14.6 us
    dot_general x1, matrix products, shards(): lax.dot_general(weights, weighted, (((0,), (1,)), ((), ())), precision=HIGH)  6.5 us
    ppermute x3, starting transfers between devices, shards(): received.append(lax.ppermute(piece, 'freq', pairs))  5.73 us
  transfers between devices with their start and end apart: 26, of which 19 were waited for; matrix products, arithmetic and copies ran while one was open for 1% of the time, Pallas kernels for 0%

profile of v1, /device:TPU:32, one launch (start us, length us, event | category | flops | bytes accessed | tf_op | source)
XLA Modules:
  0.0 188.8 jit_solution(2938268389153351349)
XLA Ops:
  2.8 3.6 %collective-permute-start.1 = (bf16[256,128]{1,0:T(8,128)(2,1)S(1)}, bf16[256,128]{1,0:T(8,128)(2,1)S(1)}, u32[]{:S(2)}, u32[]{:S(2)}) collective-permute-start(bf16[256,128]{1,0:T(8,128)(2,1)S(1)} %get-tuple-element.14), channel_id=1, source_target_pairs={{4,0},{8,4},{12,8},{16,12},{20,16},{24,20},{28,24},{32,28},{36,32}... | collective-permute-start | bytes 196616 | tf_op jit(solution)/shard_map/ppermute | solution.py:170
  9.3 14.6 %shard_map.55 = (f32[16384,128]{1,0:T(8,128)}, f32[128,128]{1,0:T(8,128)}) custom-call(s32[384]{0:T(512)} %reshape.98.index_ref, bf16[256,128]{1,0:T(8,128)(2,1)} %copy-done.1, bf16[16384,128]{1,0:T(8,128)(2,1)} %own_ref.1, bf16[256,128]{1,0:T(8,128)(2,1)} %copy-done.2, bf16[128,3,128,128]{3,2,1,0:T(8,128)(2,1)} %mass_ref.1), custom_call_target="tpu_custom_call" | custom-call | tf_op jit(solution)/shard_map/pallas_call | solution.py:88
  27.1 3.6 %collective-permute-done.3 = f32[128,128]{1,0:T(8,128)S(1)} collective-permute-done((f32[128,128]{1,0:T(8,128)}, f32[128,128]{1,0:T(8,128)S(1)}, u32[]{:S(2)}, u32[]{:S(2)}) %collective-permute-start.3) | collective-permute-done | bytes 65568 | tf_op jit(solution)/shard_map/ppermute | solution.py:111
  31.5 5.8 %collective-permute-start.5 = (f32[128,128]{1,0:T(8,128)S(1)}, f32[128,128]{1,0:T(8,128)S(1)}, u32[]{:S(2)}, u32[]{:S(2)}) collective-permute-start(f32[128,128]{1,0:T(8,128)S(1)} %add_add_fusion.4), channel_id=1, source_target_pairs={{0,16},{4,20},{8,24},{12,28},{16,0},{20,4},{24,8},{28,12},{32,48},... | collective-permute-start | bytes 196616 | tf_op jit(solution)/shard_map/ppermute | solution.py:111
  41.5 5.3 %collective-permute-done.6 = f32[128,128]{1,0:T(8,128)S(1)} collective-permute-done((f32[128,128]{1,0:T(8,128)S(1)}, f32[128,128]{1,0:T(8,128)S(1)}, u32[]{:S(2)}, u32[]{:S(2)}) %collective-permute-start.6) | collective-permute-done | bytes 65568 | tf_op jit(solution)/shard_map/ppermute | solution.py:111
  48.8 2.6 %collective-permute-start.10 = (f32[128,128]{1,0:T(8,128)S(1)}, f32[128,128]{1,0:T(8,128)S(1)}, u32[]{:S(2)}, u32[]{:S(2)}) collective-permute-start(f32[128,128]{1,0:T(8,128)S(1)} %add_add_fusion.3), channel_id=1, source_target_pairs={{0,192},{4,196},{8,200},{12,204},{16,208},{20,212},{24,216},{28,22... | collective-permute-start | bytes 196616 | tf_op jit(solution)/shard_map/ppermute | solution.py:111
  58.3 2.9 %cholesky.117 = f32[32,32]{1,0:T(8,128)S(1)} custom-call(f32[32,32]{1,0:T(8,128)S(1)} %fusion.20), custom_call_target="Cholesky" | custom-call | tf_op jit(solution)/shard_map/jit(cholesky)/cholesky | solution.py:122
  62.6 2.4 %custom-call.18 = f32[1,32,32]{1,2,0:T(8,128)S(1)} custom-call(f32[1,32,32]{2,1,0:T(8,128)S(1)} %fusion.8), custom_call_target="InvertDiagBlocksLowerTriangular" | custom-call | tf_op jit(solution)/shard_map/triangular_solve/custom-call.2 | solution.py:123
  65.8 2.9 %cholesky.128 = f32[32,32]{1,0:T(8,128)S(1)} custom-call(f32[32,32]{1,0:T(8,128)S(1)} %fusion.18), custom_call_target="Cholesky" | custom-call | tf_op jit(solution)/shard_map/jit(cholesky)/cholesky | solution.py:122
  72.7 6.5 %fusion.49 = f32[32,16384]{1,0:T(8,128)S(1)} fusion(f32[128,32]{0,1:T(8,128)S(1)} %convolution_bitcast_fusion.4, f32[16384,128]{1,0:T(8,128)} %get-tuple-element.12), kind=kOutput, calls=%fused_computation.116 | convolution fusion | flops 402653184 | bytes 10502144 | tf_op jit(solution)/shard_map/dot_general | solution.py:175
  81.0 2.7 %collective-permute-start.12 = (f32[32,4096]{1,0:T(8,128)S(1)}, f32[32,4096]{1,0:T(8,128)S(1)}, u32[]{:S(2)}, u32[]{:S(2)}) collective-permute-start(f32[32,4096]{1,0:T(8,128)S(1)} %get-tuple-element.18), channel_id=1, source_target_pairs={{0,2},{1,3},{2,0},{3,1},{4,6},{5,7},{6,4},{7,5},{8,10},{9,11},{10,... | collective-permute-start | bytes 1572872 | tf_op jit(solution)/shard_map/ppermute | solution.py:184
  85.3 9.2 %collective-permute-done.11 = f32[32,4096]{1,0:T(8,128)S(1)} collective-permute-done((f32[32,4096]{1,0:T(8,128)S(1)}, f32[32,4096]{1,0:T(8,128)S(1)}, u32[]{:S(2)}, u32[]{:S(2)}) %collective-permute-start.11) | collective-permute-done | bytes 524320 | tf_op jit(solution)/shard_map/ppermute | solution.py:184
  94.5 10.8 %collective-permute-done.12 = f32[32,4096]{1,0:T(8,128)S(1)} collective-permute-done((f32[32,4096]{1,0:T(8,128)S(1)}, f32[32,4096]{1,0:T(8,128)S(1)}, u32[]{:S(2)}, u32[]{:S(2)}) %collective-permute-start.12) | collective-permute-done | bytes 524320 | tf_op jit(solution)/shard_map/ppermute | solution.py:184
  111.3 3.2 %collective-permute-done.15 = f32[128,128]{1,0:T(8,128)S(1)} collective-permute-done((f32[128,128]{1,0:T(8,128)S(1)}, f32[128,128]{1,0:T(8,128)S(1)}, u32[]{:S(2)}, u32[]{:S(2)}) %collective-permute-start.15) | collective-permute-done | bytes 65568 | tf_op jit(solution)/shard_map/ppermute | solution.py:111
  116.4 2.7 %collective-permute-start.18 = (f32[128,128]{1,0:T(8,128)S(1)}, f32[128,128]{1,0:T(8,128)S(1)}, u32[]{:S(2)}, u32[]{:S(2)}) collective-permute-start(f32[128,128]{1,0:T(8,128)S(1)} %add_add_fusion.2), channel_id=1, source_target_pairs={{0,32},{4,36},{8,40},{12,44},{16,48},{20,52},{24,56},{28,60},{32,0... | collective-permute-start | bytes 196616 | tf_op jit(solution)/shard_map/ppermute | solution.py:111
  121.4 5.4 %collective-permute-done.18 = f32[128,128]{1,0:T(8,128)S(1)} collective-permute-done((f32[128,128]{1,0:T(8,128)S(1)}, f32[128,128]{1,0:T(8,128)S(1)}, u32[]{:S(2)}, u32[]{:S(2)}) %collective-permute-start.18) | collective-permute-done | bytes 65568 | tf_op jit(solution)/shard_map/ppermute | solution.py:111
  141.7 2.5 %collective-permute-done.24 = f32[128,128]{1,0:T(8,128)S(1)} collective-permute-done((f32[128,128]{1,0:T(8,128)S(1)}, f32[128,128]{1,0:T(8,128)S(1)}, u32[]{:S(2)}, u32[]{:S(2)}) %collective-permute-start.24) | collective-permute-done | bytes 65568 | tf_op jit(solution)/shard_map/ppermute | solution.py:111
  146.9 5.9 %custom-call.20 = f32[2,32,32]{2,1,0:T(8,128)S(1)} custom-call(f32[2,32,32]{2,1,0:T(8,128)S(1)} %fusion.7), custom_call_target="Cholesky" | custom-call | tf_op jit(solution)/shard_map/vmap(jit(cholesky))/cholesky | solution.py:122
  153.0 4.9 %custom-call.21 = f32[2,1,32,32]{2,3,1,0:T(8,128)S(1)} custom-call(f32[2,1,32,32]{3,2,1,0:T(8,128)S(1)} %select_bitcast_fusion.1), custom_call_target="InvertDiagBlocksLowerTriangular" | custom-call | tf_op jit(solution)/shard_map/vmap()/triangular_solve/custom-call.3 | solution.py:123
  158.7 5.9 %custom-call.22 = f32[2,32,32]{2,1,0:T(8,128)S(1)} custom-call(f32[2,32,32]{2,1,0:T(8,128)S(1)} %fusion.5), custom_call_target="Cholesky" | custom-call | tf_op jit(solution)/shard_map/vmap(jit(cholesky))/cholesky | solution.py:122
  164.8 4.9 %custom-call.23 = f32[2,1,32,32]{2,3,1,0:T(8,128)S(1)} custom-call(f32[2,1,32,32]{3,2,1,0:T(8,128)S(1)} %select_bitcast_fusion), custom_call_target="InvertDiagBlocksLowerTriangular" | custom-call | tf_op jit(solution)/shard_map/vmap()/triangular_solve/custom-call.3 | solution.py:123
  170.9 2.9 %cholesky.161 = f32[32,32]{1,0:T(8,128)S(1)} custom-call(f32[32,32]{1,0:T(8,128)S(1)} %fusion.15), custom_call_target="Cholesky" | custom-call | tf_op jit(solution)/shard_map/jit(cholesky)/cholesky | solution.py:122
  178.3 2.9 %cholesky.172 = f32[32,32]{1,0:T(8,128)S(1)} custom-call(f32[32,32]{1,0:T(8,128)S(1)} %fusion.13), custom_call_target="Cholesky" | custom-call | tf_op jit(solution)/shard_map/jit(cholesky)/cholesky | solution.py:122
  186.2 2.6 %fusion = f32[32,4096]{1,0:T(8,128)} fusion(f32[128,32]{1,0:T(8,128)S(1)} %bitcast_select_fusion, f32[32,4096]{1,0:T(8,128)} %collective-permute-done.13, f32[32,4096]{1,0:T(8,128)S(1)} %collective-permute-done.12, f32[32,4096]{1,0:T(8,128)S(1)} %collective-permute-done.11, f32[32,4096]{1,0:T(8,128)S(1)} %get-tuple-element.16), kind=kOutput, calls=%fused_computation.4 | convolution fusion | flops 102236160 | bytes 2637824 | tf_op jit(solution)/shard_map/dot_general | solution.py:195
  (134 shorter events, 71.6 us)
Async XLA Ops:
  0.9 7.2 %collective-permute-start = (bf16[256,128]{1,0:T(8,128)(2,1)S(1)}, bf16[256,128]{1,0:T(8,128)(2,1)S(1)}, u32[]{:S(2)}, u32[]{:S(2)}) collective-permute-start(bf16[256,128]{1,0:T(8,128)(2,1)S(1)} %get-tuple-element.15), channel_id=1, source_target_pairs={{0,4},{4,8},{8,12},{12,16},{16,20},{20,24},{24,28},{28,32},{32,36}... | collective-permute-start | bytes 196616 | tf_op jit(solution)/shard_map/ppermute | solution.py:169
  2.8 5.5 %collective-permute-start.1 = (bf16[256,128]{1,0:T(8,128)(2,1)S(1)}, bf16[256,128]{1,0:T(8,128)(2,1)S(1)}, u32[]{:S(2)}, u32[]{:S(2)}) collective-permute-start(bf16[256,128]{1,0:T(8,128)(2,1)S(1)} %get-tuple-element.14), channel_id=1, source_target_pairs={{4,0},{8,4},{12,8},{16,12},{20,16},{24,20},{28,24},{32,28},{36,32}... | collective-permute-start | bytes 196616 | tf_op jit(solution)/shard_map/ppermute | solution.py:170
  25.7 5.0 %collective-permute-start.3 = (f32[128,128]{1,0:T(8,128)}, f32[128,128]{1,0:T(8,128)S(1)}, u32[]{:S(2)}, u32[]{:S(2)}) collective-permute-start(f32[128,128]{1,0:T(8,128)} %get-tuple-element.10), channel_id=1, source_target_pairs={{0,8},{4,12},{8,0},{12,4},{16,24},{20,28},{24,16},{28,20},{32,40},... | collective-permute-start | bytes 196616 | tf_op jit(solution)/shard_map/ppermute | solution.py:111
  25.8 4.9 %collective-permute-start.4 = (f32[128,128]{1,0:T(8,128)}, f32[128,128]{1,0:T(8,128)S(1)}, u32[]{:S(2)}, u32[]{:S(2)}) collective-permute-start(f32[128,128]{1,0:T(8,128)} %get-tuple-element.10), channel_id=1, source_target_pairs={{0,12},{4,8},{8,4},{12,0},{16,28},{20,24},{24,20},{28,16},{32,44},... | collective-permute-start | bytes 196616 | tf_op jit(solution)/shard_map/ppermute | solution.py:111
  31.5 10.0 %collective-permute-start.5 = (f32[128,128]{1,0:T(8,128)S(1)}, f32[128,128]{1,0:T(8,128)S(1)}, u32[]{:S(2)}, u32[]{:S(2)}) collective-permute-start(f32[128,128]{1,0:T(8,128)S(1)} %add_add_fusion.4), channel_id=1, source_target_pairs={{0,16},{4,20},{8,24},{12,28},{16,0},{20,4},{24,8},{28,12},{32,48},... | collective-permute-start | bytes 196616 | tf_op jit(solution)/shard_map/ppermute | solution.py:111
  37.3 9.5 %collective-permute-start.6 = (f32[128,128]{1,0:T(8,128)S(1)}, f32[128,128]{1,0:T(8,128)S(1)}, u32[]{:S(2)}, u32[]{:S(2)}) collective-permute-start(f32[128,128]{1,0:T(8,128)S(1)} %add_add_fusion.4), channel_id=1, source_target_pairs={{0,32},{4,36},{8,40},{12,44},{16,48},{20,52},{24,56},{28,60},{32,0... | collective-permute-start | bytes 196616 | tf_op jit(solution)/shard_map/ppermute | solution.py:111
  39.3 9.5 %collective-permute-start.7 = (f32[128,128]{1,0:T(8,128)S(1)}, f32[128,128]{1,0:T(8,128)S(1)}, u32[]{:S(2)}, u32[]{:S(2)}) collective-permute-start(f32[128,128]{1,0:T(8,128)S(1)} %add_add_fusion.4), channel_id=1, source_target_pairs={{0,48},{4,52},{8,56},{12,60},{16,32},{20,36},{24,40},{28,44},{32,1... | collective-permute-start | bytes 196616 | tf_op jit(solution)/shard_map/ppermute | solution.py:111
  48.8 5.6 %collective-permute-start.10 = (f32[128,128]{1,0:T(8,128)S(1)}, f32[128,128]{1,0:T(8,128)S(1)}, u32[]{:S(2)}, u32[]{:S(2)}) collective-permute-start(f32[128,128]{1,0:T(8,128)S(1)} %add_add_fusion.3), channel_id=1, source_target_pairs={{0,192},{4,196},{8,200},{12,204},{16,208},{20,212},{24,216},{28,22... | collective-permute-start | bytes 196616 | tf_op jit(solution)/shard_map/ppermute | solution.py:111
  51.5 4.4 %collective-permute-start.8 = (f32[128,128]{1,0:T(8,128)S(1)}, f32[128,128]{1,0:T(8,128)S(1)}, u32[]{:S(2)}, u32[]{:S(2)}) collective-permute-start(f32[128,128]{1,0:T(8,128)S(1)} %add_add_fusion.3), channel_id=1, source_target_pairs={{0,64},{4,68},{8,72},{12,76},{16,80},{20,84},{24,88},{28,92},{32,9... | collective-permute-start | bytes 196616 | tf_op jit(solution)/shard_map/ppermute | solution.py:111
  52.1 5.8 %collective-permute-start.9 = (f32[128,128]{1,0:T(8,128)S(1)}, f32[128,128]{1,0:T(8,128)S(1)}, u32[]{:S(2)}, u32[]{:S(2)}) collective-permute-start(f32[128,128]{1,0:T(8,128)S(1)} %add_add_fusion.3), channel_id=1, source_target_pairs={{0,128},{4,132},{8,136},{12,140},{16,144},{20,148},{24,152},{28,15... | collective-permute-start | bytes 196616 | tf_op jit(solution)/shard_map/ppermute | solution.py:111
  79.4 15.1 %collective-permute-start.11 = (f32[32,4096]{1,0:T(8,128)S(1)}, f32[32,4096]{1,0:T(8,128)S(1)}, u32[]{:S(2)}, u32[]{:S(2)}) collective-permute-start(f32[32,4096]{1,0:T(8,128)S(1)} %get-tuple-element.19), channel_id=1, source_target_pairs={{0,1},{1,2},{2,3},{3,0},{4,5},{5,6},{6,7},{7,4},{8,9},{9,10},{10,1... | collective-permute-start | bytes 1572872 | tf_op jit(solution)/shard_map/ppermute | solution.py:184
  81.0 24.3 %collective-permute-start.12 = (f32[32,4096]{1,0:T(8,128)S(1)}, f32[32,4096]{1,0:T(8,128)S(1)}, u32[]{:S(2)}, u32[]{:S(2)}) collective-permute-start(f32[32,4096]{1,0:T(8,128)S(1)} %get-tuple-element.18), channel_id=1, source_target_pairs={{0,2},{1,3},{2,0},{3,1},{4,6},{5,7},{6,4},{7,5},{8,10},{9,11},{10,... | collective-permute-start | bytes 1572872 | tf_op jit(solution)/shard_map/ppermute | solution.py:184
  83.7 21.6 %collective-permute-start.13 = (f32[32,4096]{1,0:T(8,128)S(1)}, f32[32,4096]{1,0:T(8,128)}, u32[]{:S(2)}, u32[]{:S(2)}) collective-permute-start(f32[32,4096]{1,0:T(8,128)S(1)} %get-tuple-element.17), channel_id=1, source_target_pairs={{0,3},{1,0},{2,1},{3,2},{4,7},{5,4},{6,5},{7,6},{8,11},{9,8},{10,9... | collective-permute-start | bytes 1572872 | tf_op jit(solution)/shard_map/ppermute | solution.py:184
  109.5 5.1 %collective-permute-start.15 = (f32[128,128]{1,0:T(8,128)S(1)}, f32[128,128]{1,0:T(8,128)S(1)}, u32[]{:S(2)}, u32[]{:S(2)}) collective-permute-start(f32[128,128]{1,0:T(8,128)S(1)} %broadcast_select_fusion.1), channel_id=1, source_target_pairs={{0,8},{4,12},{8,0},{12,4},{16,24},{20,28},{24,16},{28,20},{32,40},... | collective-permute-start | bytes 196616 | tf_op jit(solution)/shard_map/ppermute | solution.py:111
  109.6 5.2 %collective-permute-start.16 = (f32[128,128]{1,0:T(8,128)S(1)}, f32[128,128]{1,0:T(8,128)S(1)}, u32[]{:S(2)}, u32[]{:S(2)}) collective-permute-start(f32[128,128]{1,0:T(8,128)S(1)} %broadcast_select_fusion.1), channel_id=1, source_target_pairs={{0,12},{4,8},{8,4},{12,0},{16,28},{20,24},{24,20},{28,16},{32,44},... | collective-permute-start | bytes 196616 | tf_op jit(solution)/shard_map/ppermute | solution.py:111
  114.8 6.6 %collective-permute-start.17 = (f32[128,128]{1,0:T(8,128)S(1)}, f32[128,128]{1,0:T(8,128)S(1)}, u32[]{:S(2)}, u32[]{:S(2)}) collective-permute-start(f32[128,128]{1,0:T(8,128)S(1)} %add_add_fusion.2), channel_id=1, source_target_pairs={{0,16},{4,20},{8,24},{12,28},{16,0},{20,4},{24,8},{28,12},{32,48},... | collective-permute-start | bytes 196616 | tf_op jit(solution)/shard_map/ppermute | solution.py:111
  116.4 10.3 %collective-permute-start.18 = (f32[128,128]{1,0:T(8,128)S(1)}, f32[128,128]{1,0:T(8,128)S(1)}, u32[]{:S(2)}, u32[]{:S(2)}) collective-permute-start(f32[128,128]{1,0:T(8,128)S(1)} %add_add_fusion.2), channel_id=1, source_target_pairs={{0,32},{4,36},{8,40},{12,44},{16,48},{20,52},{24,56},{28,60},{32,0... | collective-permute-start | bytes 196616 | tf_op jit(solution)/shard_map/ppermute | solution.py:111
  119.2 9.2 %collective-permute-start.19 = (f32[128,128]{1,0:T(8,128)S(1)}, f32[128,128]{1,0:T(8,128)S(1)}, u32[]{:S(2)}, u32[]{:S(2)}) collective-permute-start(f32[128,128]{1,0:T(8,128)S(1)} %add_add_fusion.2), channel_id=1, source_target_pairs={{0,48},{4,52},{8,56},{12,60},{16,32},{20,36},{24,40},{28,44},{32,1... | collective-permute-start | bytes 196616 | tf_op jit(solution)/shard_map/ppermute | solution.py:111
  128.3 4.9 %collective-permute-start.20 = (f32[128,128]{1,0:T(8,128)S(1)}, f32[128,128]{1,0:T(8,128)S(1)}, u32[]{:S(2)}, u32[]{:S(2)}) collective-permute-start(f32[128,128]{1,0:T(8,128)S(1)} %add_add_fusion.1), channel_id=1, source_target_pairs={{0,64},{4,68},{8,72},{12,76},{16,80},{20,84},{24,88},{28,92},{32,9... | collective-permute-start | bytes 196616 | tf_op jit(solution)/shard_map/ppermute | solution.py:111
  129.6 5.9 %collective-permute-start.21 = (f32[128,128]{1,0:T(8,128)S(1)}, f32[128,128]{1,0:T(8,128)S(1)}, u32[]{:S(2)}, u32[]{:S(2)}) collective-permute-start(f32[128,128]{1,0:T(8,128)S(1)} %add_add_fusion.1), channel_id=1, source_target_pairs={{0,128},{4,132},{8,136},{12,140},{16,144},{20,148},{24,152},{28,15... | collective-permute-start | bytes 196616 | tf_op jit(solution)/shard_map/ppermute | solution.py:111
  131.4 5.5 %collective-permute-start.22 = (f32[128,128]{1,0:T(8,128)S(1)}, f32[128,128]{1,0:T(8,128)S(1)}, u32[]{:S(2)}, u32[]{:S(2)}) collective-permute-start(f32[128,128]{1,0:T(8,128)S(1)} %add_add_fusion.1), channel_id=1, source_target_pairs={{0,192},{4,196},{8,200},{12,204},{16,208},{20,212},{24,216},{28,22... | collective-permute-start | bytes 196616 | tf_op jit(solution)/shard_map/ppermute | solution.py:111
  136.9 4.8 %collective-permute-start.23 = (f32[128,128]{1,0:T(8,128)S(1)}, f32[128,128]{1,0:T(8,128)S(1)}, u32[]{:S(2)}, u32[]{:S(2)}) collective-permute-start(f32[128,128]{1,0:T(8,128)S(1)} %add_add_fusion), channel_id=1, source_target_pairs={{0,1},{1,0},{2,3},{3,2},{4,5},{5,4},{6,7},{7,6},{8,9},{9,8},{10,11... | collective-permute-start | bytes 196616 | tf_op jit(solution)/shard_map/ppermute | solution.py:111
  138.4 5.8 %collective-permute-start.24 = (f32[128,128]{1,0:T(8,128)S(1)}, f32[128,128]{1,0:T(8,128)S(1)}, u32[]{:S(2)}, u32[]{:S(2)}) collective-permute-start(f32[128,128]{1,0:T(8,128)S(1)} %add_add_fusion), channel_id=1, source_target_pairs={{0,2},{1,3},{2,0},{3,1},{4,6},{5,7},{6,4},{7,5},{8,10},{9,11},{10,... | collective-permute-start | bytes 196616 | tf_op jit(solution)/shard_map/ppermute | solution.py:111
  140.8 5.5 %collective-permute-start.25 = (f32[128,128]{1,0:T(8,128)S(1)}, f32[128,128]{1,0:T(8,128)S(1)}, u32[]{:S(2)}, u32[]{:S(2)}) collective-permute-start(f32[128,128]{1,0:T(8,128)S(1)} %add_add_fusion), channel_id=1, source_target_pairs={{0,3},{1,2},{2,1},{3,0},{4,7},{5,6},{6,5},{7,4},{8,11},{9,10},{10,... | collective-permute-start | bytes 196616 | tf_op jit(solution)/shard_map/ppermute | solution.py:111
  (6 other events, 202.6 us)

commit v2 on v1

--- a/solution.py
+++ b/solution.py
@@ -117,6 +117,57 @@
     return x
 
 
+def subspace_kernel(g_ref, v_ref, out_ref):
+    gram = g_ref[...]
+    current = v_ref[...]
+    rank = current.shape[0]
+    nt = (((1,), (1,)), ((), ()))
+    sub = lax.broadcasted_iota(jnp.int32, (rank, rank), 0)
+    lane = lax.broadcasted_iota(jnp.int32, (rank, rank), 1)
+    sub_wide = lax.broadcasted_iota(jnp.int32, current.shape, 0)
+    for repeat in range(POWER):
+        product = lax.dot_general(current, gram, nt, precision=HIGHEST, preferred_element_type=jnp.float32)
+        inner = lax.dot_general(product, product, nt, precision=HIGHEST, preferred_element_type=jnp.float32)
+
+        def one_column(j, carry):
+            inner, rest, solved = carry
+            row = jnp.sum(jnp.where(sub == j, inner, 0.0), axis=0, keepdims=True)
+            col = jnp.sum(jnp.where(lane == j, inner, 0.0), axis=1, keepdims=True)
+            pivot = jnp.sum(jnp.where(lane[:1] == j, row, 0.0), axis=1, keepdims=True)
+            root = jnp.sqrt(pivot)
+            factor_row = jnp.where(lane[:1] >= j, row / root, 0.0)
+            factor_col = jnp.where(sub[:, :1] >= j, col / root, 0.0)
+            inner = inner - factor_col * factor_row
+            answer = jnp.sum(jnp.where(sub_wide == j, rest, 0.0), axis=0, keepdims=True) / root
+            rest = rest - factor_row.T * answer
+            solved = jnp.where(sub_wide == j, answer, solved)
+            return inner, rest, solved
+
+        _, _, current = lax.fori_loop(
+            0, rank, one_column, (inner, product, jnp.zeros_like(product)), unroll=True
+        )
+    out_ref[...] = current
+
+
+def subspace_batch(grams, starts_t):
+    batch, size, _ = grams.shape
+    rank = starts_t.shape[1]
+    return pl.pallas_call(
+        subspace_kernel,
+        grid=(batch,),
+        in_specs=[
+            pl.BlockSpec((None, size, size), lambda b: (b, 0, 0)),
+            pl.BlockSpec((None, rank, size), lambda b: (b, 0, 0)),
+        ],
+        out_specs=pl.BlockSpec((None, rank, size), lambda b: (b, 0, 0)),
+        out_shape=jax.ShapeDtypeStruct((batch, rank, size), jnp.float32),
+    )(grams, starts_t)
+
+
+def fast_subspace(gram_matrix, start_block):
+    return subspace_batch(gram_matrix[None], start_block.T[None])[0].T
+
+
 def orthonormal(columns_block):
     inner_gram = jnp.dot(columns_block.T, columns_block, precision=HIGHEST)
     lower_factor = jnp.linalg.cholesky(inner_gram)
@@ -138,7 +189,8 @@
     blocks = jnp.stack(
         [full_gram[p * width : (p + 1) * width, p * width : (p + 1) * width] for p in range(pairs)]
     )
-    pair_weights = jax.vmap(subspace, in_axes=(0, None))(blocks, start_merge)
+    starts_t = jnp.broadcast_to(start_merge.T[None], (pairs,) + start_merge.T.shape)
+    pair_weights = jnp.swapaxes(subspace_batch(blocks, starts_t), 1, 2)
     zero = jnp.zeros((width, rank_size), jnp.float32)
     coefficients = []
     for p in range(pairs):
@@ -152,7 +204,7 @@
             pair_gram = jnp.dot(
                 joined.T, jnp.dot(full_gram, joined, precision=HIGHEST), precision=HIGHEST
             )
-            merged.append(jnp.dot(joined, subspace(pair_gram, start_merge), precision=HIGHEST))
+            merged.append(jnp.dot(joined, fast_subspace(pair_gram, start_merge), precision=HIGHEST))
         coefficients = merged
     return coefficients[0]
 
@@ -171,7 +223,7 @@
     local_index = block_cols - lax.axis_index("rows") * local_blocks + HB
     weighted, local_gram = apply_mass(low, snapshots, high, mass_blocks, local_index)
     group_gram = butterfly_sum(local_gram, ("rows",)) / total_rows
-    weights = subspace(group_gram, start_group)
+    weights = fast_subspace(group_gram, start_group)
     modes = lax.dot_general(weights, weighted, (((0,), (1,)), ((), ())), precision=HIGH)
     rank_size = modes.shape[0]
     freq_count = lax.axis_size("freq")

time: 189 us -> 177 us (0.937)
  other arithmetic: 50.7 us -> 3.21 us
  Pallas kernels: 14.6 us -> 51.3 us
  matrix products: 15.9 us -> 13.4 us
    another operation x32 -> x1, other arithmetic: 48.8 us -> 0.64 us  [coefficient_tree(): jnp.stack([full_gram[p * width:(p + 1) * width, p * width:(p + 1) * width...]
    pallas_call x0 -> x3, Pallas kernels: none -> 36.6 us  [subspace_batch(): pl.pallas_call(subspace_kernel, grid=(batch,), in_specs=[pl.BlockSpec((No...]
where the time goes in v2:
time: 177 us; the launch traced here: 176 us
  waiting for transfers between devices  54.6 us (31%)
  Pallas kernels  51.3 us (29%)
  starting transfers between devices  46.8 us (26%)
  matrix products  13.4 us (8%)
  local copies, waits for them, and re-layouts  6.82 us (4%)
  other arithmetic  3.21 us (2%)
    pallas_call x3, Pallas kernels, subspace_batch(): pl.pallas_call(subspace_kernel, grid=(batch,), in_specs=[pl.BlockSpec((No...  36.6 us
    ppermute x21, starting transfers between devices, butterfly_sum(): parts.append(lax.ppermute(x, axis, pairs))  35.5 us
    ppermute x21, waiting for transfers between devices, butterfly_sum(): parts.append(lax.ppermute(x, axis, pairs))  34.4 us
    ppermute x3, waiting for transfers between devices, shards(): received.append(lax.ppermute(piece, 'freq', pairs))  19.9 us
    pallas_call x1, Pallas kernels, apply_mass(): pl.pallas_call(mass_kernel, grid_spec=grid_spec, out_shape=[jax.ShapeDtyp...  14.7 us
    dot_general x1, matrix products, shards(): lax.dot_general(weights, weighted, (((0,), (1,)), ((), ())), precision=HIGH)  6.49 us
    ppermute x3, starting transfers between devices, shards(): received.append(lax.ppermute(piece, 'freq', pairs))  5.74 us
    ppermute x1, starting transfers between devices, shards(): high = lax.ppermute(snapshots[:width], 'rows', backward)  3.64 us
  transfers between devices with their start and end apart: 26, of which 19 were waited for; matrix products, arithmetic and copies ran while one was open for 1% of the time, Pallas kernels for 0%

profile of v2, /device:TPU:32, one launch (start us, length us, event | category | flops | bytes accessed | tf_op | source)
XLA Modules:
  0.0 176.2 jit_solution(16628617135731429816)
XLA Ops:
  2.8 3.6 %collective-permute-start.1 = (bf16[256,128]{1,0:T(8,128)(2,1)S(1)}, bf16[256,128]{1,0:T(8,128)(2,1)S(1)}, u32[]{:S(2)}, u32[]{:S(2)}) collective-permute-start(bf16[256,128]{1,0:T(8,128)(2,1)S(1)} %get-tuple-element.9), channel_id=1, source_target_pairs={{4,0},{8,4},{12,8},{16,12},{20,16},{24,20},{28,24},{32,28},{36,32}... | collective-permute-start | bytes 196616 | tf_op jit(solution)/shard_map/ppermute | solution.py:222
  9.3 14.7 %shard_map.55 = (f32[16384,128]{1,0:T(8,128)}, f32[128,128]{1,0:T(8,128)}) custom-call(s32[384]{0:T(512)} %reshape.69.index_ref, bf16[256,128]{1,0:T(8,128)(2,1)} %copy-done, bf16[16384,128]{1,0:T(8,128)(2,1)} %own_ref.1, bf16[256,128]{1,0:T(8,128)(2,1)} %copy-done.1, bf16[128,3,128,128]{3,2,1,0:T(8,128)(2,1)} %mass_ref.1), custom_call_target="tpu_custom_call" | custom-call | tf_op jit(solution)/shard_map/pallas_call | solution.py:88
  27.2 3.6 %collective-permute-done.3 = f32[128,128]{1,0:T(8,128)S(1)} collective-permute-done((f32[128,128]{1,0:T(8,128)}, f32[128,128]{1,0:T(8,128)S(1)}, u32[]{:S(2)}, u32[]{:S(2)}) %collective-permute-start.3) | collective-permute-done | bytes 65568 | tf_op jit(solution)/shard_map/ppermute | solution.py:111
  31.6 5.8 %collective-permute-start.5 = (f32[128,128]{1,0:T(8,128)S(1)}, f32[128,128]{1,0:T(8,128)S(1)}, u32[]{:S(2)}, u32[]{:S(2)}) collective-permute-start(f32[128,128]{1,0:T(8,128)S(1)} %add_add_fusion.4), channel_id=1, source_target_pairs={{0,16},{4,20},{8,24},{12,28},{16,0},{20,4},{24,8},{28,12},{32,48},... | collective-permute-start | bytes 196616 | tf_op jit(solution)/shard_map/ppermute | solution.py:111
  41.6 5.3 %collective-permute-done.6 = f32[128,128]{1,0:T(8,128)S(1)} collective-permute-done((f32[128,128]{1,0:T(8,128)S(1)}, f32[128,128]{1,0:T(8,128)S(1)}, u32[]{:S(2)}, u32[]{:S(2)}) %collective-permute-start.6) | collective-permute-done | bytes 65568 | tf_op jit(solution)/shard_map/ppermute | solution.py:111
  48.9 2.6 %collective-permute-start.10 = (f32[128,128]{1,0:T(8,128)S(1)}, f32[128,128]{1,0:T(8,128)S(1)}, u32[]{:S(2)}, u32[]{:S(2)}) collective-permute-start(f32[128,128]{1,0:T(8,128)S(1)} %add_add_fusion.3), channel_id=1, source_target_pairs={{0,192},{4,196},{8,200},{12,204},{16,208},{20,212},{24,216},{28,22... | collective-permute-start | bytes 196616 | tf_op jit(solution)/shard_map/ppermute | solution.py:111
  55.9 2.0 %collective-permute-done.9 = f32[128,128]{1,0:T(8,128)S(1)} collective-permute-done((f32[128,128]{1,0:T(8,128)S(1)}, f32[128,128]{1,0:T(8,128)S(1)}, u32[]{:S(2)}, u32[]{:S(2)}) %collective-permute-start.9) | collective-permute-done | bytes 65568 | tf_op jit(solution)/shard_map/ppermute | solution.py:111
  58.6 9.6 %shard_map.56 = f32[1,32,128]{2,1,0:T(8,128)} custom-call(f32[1,128,128]{2,1,0:T(8,128)} %multiply_bitcast_fusion.g_ref, f32[1,32,128]{2,1,0:T(8,128)} %bitcast.42), custom_call_target="tpu_custom_call" | custom-call | tf_op jit(solution)/shard_map/pallas_call | solution.py:155
  68.2 6.5 %fusion.4 = f32[32,16384]{1,0:T(8,128)S(1)} fusion(f32[16384,128]{1,0:T(8,128)} %get-tuple-element.8, f32[1,32,128]{2,1,0:T(8,128)} %shard_map.56), kind=kOutput, calls=%fused_computation.27 | convolution fusion | flops 402653184 | bytes 10502144 | tf_op jit(solution)/shard_map/dot_general | solution.py:227
  76.4 2.7 %collective-permute-start.12 = (f32[32,4096]{1,0:T(8,128)S(1)}, f32[32,4096]{1,0:T(8,128)S(1)}, u32[]{:S(2)}, u32[]{:S(2)}) collective-permute-start(f32[32,4096]{1,0:T(8,128)S(1)} %get-tuple-element.13), channel_id=1, source_target_pairs={{0,2},{1,3},{2,0},{3,1},{4,6},{5,7},{6,4},{7,5},{8,10},{9,11},{10,... | collective-permute-start | bytes 1572872 | tf_op jit(solution)/shard_map/ppermute | solution.py:236
  80.8 9.2 %collective-permute-done.11 = f32[32,4096]{1,0:T(8,128)S(1)} collective-permute-done((f32[32,4096]{1,0:T(8,128)S(1)}, f32[32,4096]{1,0:T(8,128)S(1)}, u32[]{:S(2)}, u32[]{:S(2)}) %collective-permute-start.11) | collective-permute-done | bytes 524320 | tf_op jit(solution)/shard_map/ppermute | solution.py:236
  89.9 10.8 %collective-permute-done.12 = f32[32,4096]{1,0:T(8,128)S(1)} collective-permute-done((f32[32,4096]{1,0:T(8,128)S(1)}, f32[32,4096]{1,0:T(8,128)S(1)}, u32[]{:S(2)}, u32[]{:S(2)}) %collective-permute-start.12) | collective-permute-done | bytes 524320 | tf_op jit(solution)/shard_map/ppermute | solution.py:236
  100.7 2.3 %fusion.1 = f32[128,128]{1,0:T(8,128)S(1)} fusion(f32[32,4096]{1,0:T(8,128)} %collective-permute-done.13, f32[32,4096]{1,0:T(8,128)S(1)} %collective-permute-done.12, f32[32,4096]{1,0:T(8,128)S(1)} %collective-permute-done.11, f32[32,4096]{1,0:T(8,128)S(1)} %get-tuple-element.11), kind=kOutput, calls=%fused_computation.5 | convolution fusion | flops 404226048 | bytes 2162688 | tf_op jit(solution)/shard_map/dot_general | solution.py:239
  106.8 3.2 %collective-permute-done.15 = f32[128,128]{1,0:T(8,128)S(1)} collective-permute-done((f32[128,128]{1,0:T(8,128)S(1)}, f32[128,128]{1,0:T(8,128)S(1)}, u32[]{:S(2)}, u32[]{:S(2)}) %collective-permute-start.15) | collective-permute-done | bytes 65568 | tf_op jit(solution)/shard_map/ppermute | solution.py:111
  111.9 2.7 %collective-permute-start.18 = (f32[128,128]{1,0:T(8,128)S(1)}, f32[128,128]{1,0:T(8,128)S(1)}, u32[]{:S(2)}, u32[]{:S(2)}) collective-permute-start(f32[128,128]{1,0:T(8,128)S(1)} %add_add_fusion.2), channel_id=1, source_target_pairs={{0,32},{4,36},{8,40},{12,44},{16,48},{20,52},{24,56},{28,60},{32,0... | collective-permute-start | bytes 196616 | tf_op jit(solution)/shard_map/ppermute | solution.py:111
  114.6 2.2 %collective-permute-start.19 = (f32[128,128]{1,0:T(8,128)S(1)}, f32[128,128]{1,0:T(8,128)S(1)}, u32[]{:S(2)}, u32[]{:S(2)}) collective-permute-start(f32[128,128]{1,0:T(8,128)S(1)} %add_add_fusion.2), channel_id=1, source_target_pairs={{0,48},{4,52},{8,56},{12,60},{16,32},{20,36},{24,40},{28,44},{32,1... | collective-permute-start | bytes 196616 | tf_op jit(solution)/shard_map/ppermute | solution.py:111
  116.8 5.4 %collective-permute-done.18 = f32[128,128]{1,0:T(8,128)S(1)} collective-permute-done((f32[128,128]{1,0:T(8,128)S(1)}, f32[128,128]{1,0:T(8,128)S(1)}, u32[]{:S(2)}, u32[]{:S(2)}) %collective-permute-start.18) | collective-permute-done | bytes 65568 | tf_op jit(solution)/shard_map/ppermute | solution.py:111
  128.7 2.3 %collective-permute-done.21 = f32[128,128]{1,0:T(8,128)S(1)} collective-permute-done((f32[128,128]{1,0:T(8,128)S(1)}, f32[128,128]{1,0:T(8,128)S(1)}, u32[]{:S(2)}, u32[]{:S(2)}) %collective-permute-start.21) | collective-permute-done | bytes 65568 | tf_op jit(solution)/shard_map/ppermute | solution.py:111
  133.8 2.4 %collective-permute-start.24 = (f32[128,128]{1,0:T(8,128)S(1)}, f32[128,128]{1,0:T(8,128)S(1)}, u32[]{:S(2)}, u32[]{:S(2)}) collective-permute-start(f32[128,128]{1,0:T(8,128)S(1)} %add_add_fusion), channel_id=1, source_target_pairs={{0,2},{1,3},{2,0},{3,1},{4,6},{5,7},{6,4},{7,5},{8,10},{9,11},{10,... | collective-permute-start | bytes 196616 | tf_op jit(solution)/shard_map/ppermute | solution.py:111
  137.1 2.5 %collective-permute-done.24 = f32[128,128]{1,0:T(8,128)S(1)} collective-permute-done((f32[128,128]{1,0:T(8,128)S(1)}, f32[128,128]{1,0:T(8,128)S(1)}, u32[]{:S(2)}, u32[]{:S(2)}) %collective-permute-start.24) | collective-permute-done | bytes 65568 | tf_op jit(solution)/shard_map/ppermute | solution.py:111
  139.6 2.1 %collective-permute-done.25 = f32[128,128]{1,0:T(8,128)S(1)} collective-permute-done((f32[128,128]{1,0:T(8,128)S(1)}, f32[128,128]{1,0:T(8,128)S(1)}, u32[]{:S(2)}, u32[]{:S(2)}) %collective-permute-start.25) | collective-permute-done | bytes 65568 | tf_op jit(solution)/shard_map/ppermute | solution.py:111
  143.1 17.5 %shard_map.57 = f32[2,32,64]{2,1,0:T(8,128)} custom-call(f32[2,64,64]{2,1,0:T(8,128)} %pad_maximum_fusion.3.g_ref, f32[2,32,64]{2,1,0:T(8,128)} %broadcast_in_dim.62.v_ref), custom_call_target="tpu_custom_call" | custom-call | tf_op jit(solution)/shard_map/pallas_call | solution.py:155
  162.6 9.4 %shard_map.58 = f32[1,32,64]{2,1,0:T(8,128)} custom-call(f32[1,64,64]{2,1,0:T(8,128)} %convolution_bitcast_fusion.g_ref, f32[1,32,64]{2,1,0:T(8,128)} %bitcast.40), custom_call_target="tpu_custom_call" | custom-call | tf_op jit(solution)/shard_map/pallas_call | solution.py:155
  173.6 2.6 %fusion = f32[32,4096]{1,0:T(8,128)} fusion(f32[128,32]{1,0:T(8,128)S(1)} %bitcast_select_fusion, f32[32,4096]{1,0:T(8,128)} %collective-permute-done.13, f32[32,4096]{1,0:T(8,128)S(1)} %collective-permute-done.12, f32[32,4096]{1,0:T(8,128)S(1)} %collective-permute-done.11, f32[32,4096]{1,0:T(8,128)S(1)} %get-tuple-element.11), kind=kOutput, calls=%fused_computation.4 | convolution fusion | flops 102236160 | bytes 2637824 | tf_op jit(solution)/shard_map/dot_general | solution.py:247
  (77 shorter events, 45.0 us)
Async XLA Ops:
  0.9 7.2 %collective-permute-start = (bf16[256,128]{1,0:T(8,128)(2,1)S(1)}, bf16[256,128]{1,0:T(8,128)(2,1)S(1)}, u32[]{:S(2)}, u32[]{:S(2)}) collective-permute-start(bf16[256,128]{1,0:T(8,128)(2,1)S(1)} %get-tuple-element.10), channel_id=1, source_target_pairs={{0,4},{4,8},{8,12},{12,16},{16,20},{20,24},{24,28},{28,32},{32,36}... | collective-permute-start | bytes 196616 | tf_op jit(solution)/shard_map/ppermute | solution.py:221
  2.8 5.5 %collective-permute-start.1 = (bf16[256,128]{1,0:T(8,128)(2,1)S(1)}, bf16[256,128]{1,0:T(8,128)(2,1)S(1)}, u32[]{:S(2)}, u32[]{:S(2)}) collective-permute-start(bf16[256,128]{1,0:T(8,128)(2,1)S(1)} %get-tuple-element.9), channel_id=1, source_target_pairs={{4,0},{8,4},{12,8},{16,12},{20,16},{24,20},{28,24},{32,28},{36,32}... | collective-permute-start | bytes 196616 | tf_op jit(solution)/shard_map/ppermute | solution.py:222
  25.8 5.0 %collective-permute-start.3 = (f32[128,128]{1,0:T(8,128)}, f32[128,128]{1,0:T(8,128)S(1)}, u32[]{:S(2)}, u32[]{:S(2)}) collective-permute-start(f32[128,128]{1,0:T(8,128)} %get-tuple-element.7), channel_id=1, source_target_pairs={{0,8},{4,12},{8,0},{12,4},{16,24},{20,28},{24,16},{28,20},{32,40},... | collective-permute-start | bytes 196616 | tf_op jit(solution)/shard_map/ppermute | solution.py:111
  25.9 4.9 %collective-permute-start.4 = (f32[128,128]{1,0:T(8,128)}, f32[128,128]{1,0:T(8,128)S(1)}, u32[]{:S(2)}, u32[]{:S(2)}) collective-permute-start(f32[128,128]{1,0:T(8,128)} %get-tuple-element.7), channel_id=1, source_target_pairs={{0,12},{4,8},{8,4},{12,0},{16,28},{20,24},{24,20},{28,16},{32,44},... | collective-permute-start | bytes 196616 | tf_op jit(solution)/shard_map/ppermute | solution.py:111
  31.6 10.0 %collective-permute-start.5 = (f32[128,128]{1,0:T(8,128)S(1)}, f32[128,128]{1,0:T(8,128)S(1)}, u32[]{:S(2)}, u32[]{:S(2)}) collective-permute-start(f32[128,128]{1,0:T(8,128)S(1)} %add_add_fusion.4), channel_id=1, source_target_pairs={{0,16},{4,20},{8,24},{12,28},{16,0},{20,4},{24,8},{28,12},{32,48},... | collective-permute-start | bytes 196616 | tf_op jit(solution)/shard_map/ppermute | solution.py:111
  37.4 9.5 %collective-permute-start.6 = (f32[128,128]{1,0:T(8,128)S(1)}, f32[128,128]{1,0:T(8,128)S(1)}, u32[]{:S(2)}, u32[]{:S(2)}) collective-permute-start(f32[128,128]{1,0:T(8,128)S(1)} %add_add_fusion.4), channel_id=1, source_target_pairs={{0,32},{4,36},{8,40},{12,44},{16,48},{20,52},{24,56},{28,60},{32,0... | collective-permute-start | bytes 196616 | tf_op jit(solution)/shard_map/ppermute | solution.py:111
  39.4 9.5 %collective-permute-start.7 = (f32[128,128]{1,0:T(8,128)S(1)}, f32[128,128]{1,0:T(8,128)S(1)}, u32[]{:S(2)}, u32[]{:S(2)}) collective-permute-start(f32[128,128]{1,0:T(8,128)S(1)} %add_add_fusion.4), channel_id=1, source_target_pairs={{0,48},{4,52},{8,56},{12,60},{16,32},{20,36},{24,40},{28,44},{32,1... | collective-permute-start | bytes 196616 | tf_op jit(solution)/shard_map/ppermute | solution.py:111
  48.9 5.6 %collective-permute-start.10 = (f32[128,128]{1,0:T(8,128)S(1)}, f32[128,128]{1,0:T(8,128)S(1)}, u32[]{:S(2)}, u32[]{:S(2)}) collective-permute-start(f32[128,128]{1,0:T(8,128)S(1)} %add_add_fusion.3), channel_id=1, source_target_pairs={{0,192},{4,196},{8,200},{12,204},{16,208},{20,212},{24,216},{28,22... | collective-permute-start | bytes 196616 | tf_op jit(solution)/shard_map/ppermute | solution.py:111
  51.5 4.4 %collective-permute-start.8 = (f32[128,128]{1,0:T(8,128)S(1)}, f32[128,128]{1,0:T(8,128)S(1)}, u32[]{:S(2)}, u32[]{:S(2)}) collective-permute-start(f32[128,128]{1,0:T(8,128)S(1)} %add_add_fusion.3), channel_id=1, source_target_pairs={{0,64},{4,68},{8,72},{12,76},{16,80},{20,84},{24,88},{28,92},{32,9... | collective-permute-start | bytes 196616 | tf_op jit(solution)/shard_map/ppermute | solution.py:111
  52.2 5.8 %collective-permute-start.9 = (f32[128,128]{1,0:T(8,128)S(1)}, f32[128,128]{1,0:T(8,128)S(1)}, u32[]{:S(2)}, u32[]{:S(2)}) collective-permute-start(f32[128,128]{1,0:T(8,128)S(1)} %add_add_fusion.3), channel_id=1, source_target_pairs={{0,128},{4,132},{8,136},{12,140},{16,144},{20,148},{24,152},{28,15... | collective-permute-start | bytes 196616 | tf_op jit(solution)/shard_map/ppermute | solution.py:111
  74.8 15.1 %collective-permute-start.11 = (f32[32,4096]{1,0:T(8,128)S(1)}, f32[32,4096]{1,0:T(8,128)S(1)}, u32[]{:S(2)}, u32[]{:S(2)}) collective-permute-start(f32[32,4096]{1,0:T(8,128)S(1)} %get-tuple-element.14), channel_id=1, source_target_pairs={{0,1},{1,2},{2,3},{3,0},{4,5},{5,6},{6,7},{7,4},{8,9},{9,10},{10,1... | collective-permute-start | bytes 1572872 | tf_op jit(solution)/shard_map/ppermute | solution.py:236
  76.4 24.3 %collective-permute-start.12 = (f32[32,4096]{1,0:T(8,128)S(1)}, f32[32,4096]{1,0:T(8,128)S(1)}, u32[]{:S(2)}, u32[]{:S(2)}) collective-permute-start(f32[32,4096]{1,0:T(8,128)S(1)} %get-tuple-element.13), channel_id=1, source_target_pairs={{0,2},{1,3},{2,0},{3,1},{4,6},{5,7},{6,4},{7,5},{8,10},{9,11},{10,... | collective-permute-start | bytes 1572872 | tf_op jit(solution)/shard_map/ppermute | solution.py:236
  79.1 21.6 %collective-permute-start.13 = (f32[32,4096]{1,0:T(8,128)S(1)}, f32[32,4096]{1,0:T(8,128)}, u32[]{:S(2)}, u32[]{:S(2)}) collective-permute-start(f32[32,4096]{1,0:T(8,128)S(1)} %get-tuple-element.12), channel_id=1, source_target_pairs={{0,3},{1,0},{2,1},{3,2},{4,7},{5,4},{6,5},{7,6},{8,11},{9,8},{10,9... | collective-permute-start | bytes 1572872 | tf_op jit(solution)/shard_map/ppermute | solution.py:236
  104.9 5.1 %collective-permute-start.15 = (f32[128,128]{1,0:T(8,128)S(1)}, f32[128,128]{1,0:T(8,128)S(1)}, u32[]{:S(2)}, u32[]{:S(2)}) collective-permute-start(f32[128,128]{1,0:T(8,128)S(1)} %broadcast_select_fusion.1), channel_id=1, source_target_pairs={{0,8},{4,12},{8,0},{12,4},{16,24},{20,28},{24,16},{28,20},{32,40},... | collective-permute-start | bytes 196616 | tf_op jit(solution)/shard_map/ppermute | solution.py:111
  105.0 5.2 %collective-permute-start.16 = (f32[128,128]{1,0:T(8,128)S(1)}, f32[128,128]{1,0:T(8,128)S(1)}, u32[]{:S(2)}, u32[]{:S(2)}) collective-permute-start(f32[128,128]{1,0:T(8,128)S(1)} %broadcast_select_fusion.1), channel_id=1, source_target_pairs={{0,12},{4,8},{8,4},{12,0},{16,28},{20,24},{24,20},{28,16},{32,44},... | collective-permute-start | bytes 196616 | tf_op jit(solution)/shard_map/ppermute | solution.py:111
  110.3 6.6 %collective-permute-start.17 = (f32[128,128]{1,0:T(8,128)S(1)}, f32[128,128]{1,0:T(8,128)S(1)}, u32[]{:S(2)}, u32[]{:S(2)}) collective-permute-start(f32[128,128]{1,0:T(8,128)S(1)} %add_add_fusion.2), channel_id=1, source_target_pairs={{0,16},{4,20},{8,24},{12,28},{16,0},{20,4},{24,8},{28,12},{32,48},... | collective-permute-start | bytes 196616 | tf_op jit(solution)/shard_map/ppermute | solution.py:111
  111.9 10.3 %collective-permute-start.18 = (f32[128,128]{1,0:T(8,128)S(1)}, f32[128,128]{1,0:T(8,128)S(1)}, u32[]{:S(2)}, u32[]{:S(2)}) collective-permute-start(f32[128,128]{1,0:T(8,128)S(1)} %add_add_fusion.2), channel_id=1, source_target_pairs={{0,32},{4,36},{8,40},{12,44},{16,48},{20,52},{24,56},{28,60},{32,0... | collective-permute-start | bytes 196616 | tf_op jit(solution)/shard_map/ppermute | solution.py:111
  114.6 9.1 %collective-permute-start.19 = (f32[128,128]{1,0:T(8,128)S(1)}, f32[128,128]{1,0:T(8,128)S(1)}, u32[]{:S(2)}, u32[]{:S(2)}) collective-permute-start(f32[128,128]{1,0:T(8,128)S(1)} %add_add_fusion.2), channel_id=1, source_target_pairs={{0,48},{4,52},{8,56},{12,60},{16,32},{20,36},{24,40},{28,44},{32,1... | collective-permute-start | bytes 196616 | tf_op jit(solution)/shard_map/ppermute | solution.py:111
  123.8 4.9 %collective-permute-start.20 = (f32[128,128]{1,0:T(8,128)S(1)}, f32[128,128]{1,0:T(8,128)S(1)}, u32[]{:S(2)}, u32[]{:S(2)}) collective-permute-start(f32[128,128]{1,0:T(8,128)S(1)} %add_add_fusion.1), channel_id=1, source_target_pairs={{0,64},{4,68},{8,72},{12,76},{16,80},{20,84},{24,88},{28,92},{32,9... | collective-permute-start | bytes 196616 | tf_op jit(solution)/shard_map/ppermute | solution.py:111
  125.1 5.9 %collective-permute-start.21 = (f32[128,128]{1,0:T(8,128)S(1)}, f32[128,128]{1,0:T(8,128)S(1)}, u32[]{:S(2)}, u32[]{:S(2)}) collective-permute-start(f32[128,128]{1,0:T(8,128)S(1)} %add_add_fusion.1), channel_id=1, source_target_pairs={{0,128},{4,132},{8,136},{12,140},{16,144},{20,148},{24,152},{28,15... | collective-permute-start | bytes 196616 | tf_op jit(solution)/shard_map/ppermute | solution.py:111
  126.8 5.5 %collective-permute-start.22 = (f32[128,128]{1,0:T(8,128)S(1)}, f32[128,128]{1,0:T(8,128)S(1)}, u32[]{:S(2)}, u32[]{:S(2)}) collective-permute-start(f32[128,128]{1,0:T(8,128)S(1)} %add_add_fusion.1), channel_id=1, source_target_pairs={{0,192},{4,196},{8,200},{12,204},{16,208},{20,212},{24,216},{28,22... | collective-permute-start | bytes 196616 | tf_op jit(solution)/shard_map/ppermute | solution.py:111
  132.3 4.8 %collective-permute-start.23 = (f32[128,128]{1,0:T(8,128)S(1)}, f32[128,128]{1,0:T(8,128)S(1)}, u32[]{:S(2)}, u32[]{:S(2)}) collective-permute-start(f32[128,128]{1,0:T(8,128)S(1)} %add_add_fusion), channel_id=1, source_target_pairs={{0,1},{1,0},{2,3},{3,2},{4,5},{5,4},{6,7},{7,6},{8,9},{9,8},{10,11... | collective-permute-start | bytes 196616 | tf_op jit(solution)/shard_map/ppermute | solution.py:111
  133.8 5.8 %collective-permute-start.24 = (f32[128,128]{1,0:T(8,128)S(1)}, f32[128,128]{1,0:T(8,128)S(1)}, u32[]{:S(2)}, u32[]{:S(2)}) collective-permute-start(f32[128,128]{1,0:T(8,128)S(1)} %add_add_fusion), channel_id=1, source_target_pairs={{0,2},{1,3},{2,0},{3,1},{4,6},{5,7},{6,4},{7,5},{8,10},{9,11},{10,... | collective-permute-start | bytes 196616 | tf_op jit(solution)/shard_map/ppermute | solution.py:111
  136.2 5.5 %collective-permute-start.25 = (f32[128,128]{1,0:T(8,128)S(1)}, f32[128,128]{1,0:T(8,128)S(1)}, u32[]{:S(2)}, u32[]{:S(2)}) collective-permute-start(f32[128,128]{1,0:T(8,128)S(1)} %add_add_fusion), channel_id=1, source_target_pairs={{0,3},{1,2},{2,1},{3,0},{4,7},{5,6},{6,5},{7,4},{8,11},{9,10},{10,... | collective-permute-start | bytes 196616 | tf_op jit(solution)/shard_map/ppermute | solution.py:111
  (5 other events, 45.6 us)

commit v3 on v1

--- a/solution.py
+++ b/solution.py
@@ -117,6 +117,59 @@
     return x
 
 
+def subspace_kernel(g_ref, v_ref, out_ref):
+    batch = g_ref.shape[0]
+    rank = v_ref.shape[1]
+    nt = (((1,), (1,)), ((), ()))
+    sub = lax.broadcasted_iota(jnp.int32, (rank, rank), 0)
+    lane = lax.broadcasted_iota(jnp.int32, (rank, rank), 1)
+    sub_wide = lax.broadcasted_iota(jnp.int32, v_ref.shape[1:], 0)
+    grams = [g_ref[b] for b in range(batch)]
+    currents = [v_ref[b] for b in range(batch)]
+    for repeat in range(POWER):
+        carry = []
+        for b in range(batch):
+            product = lax.dot_general(
+                currents[b], grams[b], nt, precision=HIGHEST, preferred_element_type=jnp.float32
+            )
+            inner = lax.dot_general(product, product, nt, precision=HIGHEST, preferred_element_type=jnp.float32)
+            carry.append((inner, product, jnp.zeros_like(product)))
+
+        def one_column(j, carry):
+            out = []
+            for inner, rest, solved in carry:
+                row = jnp.sum(jnp.where(sub == j, inner, 0.0), axis=0, keepdims=True)
+                col = jnp.sum(jnp.where(lane == j, inner, 0.0), axis=1, keepdims=True)
+                pivot = jnp.sum(jnp.where(lane[:1] == j, row, 0.0), axis=1, keepdims=True)
+                root = jnp.sqrt(pivot)
+                factor_row = jnp.where(lane[:1] >= j, row / root, 0.0)
+                factor_col = jnp.where(sub[:, :1] >= j, col / root, 0.0)
+                inner = inner - factor_col * factor_row
+                answer = jnp.sum(jnp.where(sub_wide == j, rest, 0.0), axis=0, keepdims=True) / root
+                rest = rest - factor_col * answer
+                solved = jnp.where(sub_wide == j, answer, solved)
+                out.append((inner, rest, solved))
+            return tuple(out)
+
+        carry = lax.fori_loop(0, rank, one_column, tuple(carry), unroll=True)
+        currents = [solved for _, _, solved in carry]
+    for b in range(batch):
+        out_ref[b] = currents[b]
+
+
+def subspace_batch(grams, starts_t):
+    batch, size, _ = grams.shape
+    rank = starts_t.shape[1]
+    return pl.pallas_call(
+        subspace_kernel,
+        out_shape=jax.ShapeDtypeStruct((batch, rank, size), jnp.float32),
+    )(grams, starts_t)
+
+
+def fast_subspace(gram_matrix, start_block):
+    return subspace_batch(gram_matrix[None], start_block.T[None])[0].T
+
+
 def orthonormal(columns_block):
     inner_gram = jnp.dot(columns_block.T, columns_block, precision=HIGHEST)
     lower_factor = jnp.linalg.cholesky(inner_gram)
@@ -138,7 +191,8 @@
     blocks = jnp.stack(
         [full_gram[p * width : (p + 1) * width, p * width : (p + 1) * width] for p in range(pairs)]
     )
-    pair_weights = jax.vmap(subspace, in_axes=(0, None))(blocks, start_merge)
+    starts_t = jnp.broadcast_to(start_merge.T[None], (pairs,) + start_merge.T.shape)
+    pair_weights = jnp.swapaxes(subspace_batch(blocks, starts_t), 1, 2)
     zero = jnp.zeros((width, rank_size), jnp.float32)
     coefficients = []
     for p in range(pairs):
@@ -152,7 +206,7 @@
             pair_gram = jnp.dot(
                 joined.T, jnp.dot(full_gram, joined, precision=HIGHEST), precision=HIGHEST
             )
-            merged.append(jnp.dot(joined, subspace(pair_gram, start_merge), precision=HIGHEST))
+            merged.append(jnp.dot(joined, fast_subspace(pair_gram, start_merge), precision=HIGHEST))
         coefficients = merged
     return coefficients[0]
 
@@ -171,17 +225,22 @@
     local_index = block_cols - lax.axis_index("rows") * local_blocks + HB
     weighted, local_gram = apply_mass(low, snapshots, high, mass_blocks, local_index)
     group_gram = butterfly_sum(local_gram, ("rows",)) / total_rows
-    weights = subspace(group_gram, start_group)
-    modes = lax.dot_general(weights, weighted, (((0,), (1,)), ((), ())), precision=HIGH)
-    rank_size = modes.shape[0]
+    weights = fast_subspace(group_gram, start_group)
+    rank_size = weights.shape[1]
     freq_count = lax.axis_size("freq")
     group = lax.axis_index("freq")
-    share = modes.shape[1] // freq_count
-    received = [lax.dynamic_slice_in_dim(modes, group * share, share, 1)]
+    share = weighted.shape[0] // freq_count
+
+    def modes_of(part):
+        rows_part = lax.dynamic_slice_in_dim(weighted, part * share, share, 0)
+        return lax.dot_general(weights, rows_part, (((0,), (1,)), ((), ())), precision=HIGH)
+
+    received = [None] * freq_count
     for shift in range(1, freq_count):
-        piece = lax.dynamic_slice_in_dim(modes, ((group + shift) % freq_count) * share, share, 1)
+        piece = modes_of((group + shift) % freq_count)
         pairs = [(i, (i + shift) % freq_count) for i in range(freq_count)]
-        received.append(lax.ppermute(piece, "freq", pairs))
+        received[shift] = lax.ppermute(piece, "freq", pairs)
+    received[0] = modes_of(group)
     stacked = jnp.concatenate(received, axis=0)
     source = (group - jnp.arange(freq_count)) % freq_count
     local_full = jnp.dot(stacked, stacked.T, precision=HIGH)

time: 189 us -> 168 us (0.89)
  other arithmetic: 50.7 us -> 3.21 us
  Pallas kernels: 14.6 us -> 43 us
  waiting for transfers between devices: 54.6 us -> 48.6 us
  matrix products: 15.9 us -> 17.8 us
    another operation x32 -> x1, other arithmetic: 48.8 us -> 0.64 us  [coefficient_tree(): jnp.stack([full_gram[p * width:(p + 1) * width, p * width:(p + 1) * width...]
    pallas_call x0 -> x3, Pallas kernels: none -> 28.3 us  [subspace_batch(): pl.pallas_call(subspace_kernel, out_shape=jax.ShapeDtypeStruct((batch, ra...]
    ppermute x3, waiting for transfers between devices: 19.9 us -> 14.1 us  [shards(): received[shift] = lax.ppermute(piece, 'freq', pairs)]
    dot_general x13 -> x5, matrix products: 8.69 us -> 11.8 us  [the longest x4 10.9 us: modes_of(): lax.dot_general(weights, rows_part, (((0,), (1,)), ((), ())), precision=H...]
  transfers between devices with their start and end apart: 26 -> 26, of which waited for: 19 -> 20; matrix products, arithmetic and copies ran while one was open for 1% -> 6% of each run, Pallas kernels for 0% -> 0%
where the time goes in v3:
time: 168 us; the launch traced here: 167 us
  waiting for transfers between devices  48.6 us (29%)
  starting transfers between devices  47.6 us (28%)
  Pallas kernels  43 us (26%)
  matrix products  17.8 us (11%)
  local copies, waits for them, and re-layouts  6.66 us (4%)
  other arithmetic  3.21 us (2%)
    ppermute x21, starting transfers between devices, butterfly_sum(): parts.append(lax.ppermute(x, axis, pairs))  35.9 us
    ppermute x21, waiting for transfers between devices, butterfly_sum(): parts.append(lax.ppermute(x, axis, pairs))  34.2 us
    pallas_call x3, Pallas kernels, subspace_batch(): pl.pallas_call(subspace_kernel, out_shape=jax.ShapeDtypeStruct((batch, ra...  28.3 us
    pallas_call x1, Pallas kernels, apply_mass(): pl.pallas_call(mass_kernel, grid_spec=grid_spec, out_shape=[jax.ShapeDtyp...  14.7 us
    ppermute x3, waiting for transfers between devices, shards(): received[shift] = lax.ppermute(piece, 'freq', pairs)  14.1 us
    dot_general x4, matrix products, modes_of(): lax.dot_general(weights, rows_part, (((0,), (1,)), ((), ())), precision=H...  10.9 us
    ppermute x3, starting transfers between devices, shards(): received[shift] = lax.ppermute(piece, 'freq', pairs)  6.08 us
    ppermute x1, starting transfers between devices, shards(): high = lax.ppermute(snapshots[:width], 'rows', backward)  3.64 us
  transfers between devices with their start and end apart: 26, of which 20 were waited for; matrix products, arithmetic and copies ran while one was open for 6% of the time, Pallas kernels for 0%

profile of v3, /device:TPU:32, one launch (start us, length us, event | category | flops | bytes accessed | tf_op | source)
XLA Modules:
  0.0 167.1 jit_solution(10287195137360255398)
XLA Ops:
  2.8 3.6 %collective-permute-start.1 = (bf16[256,128]{1,0:T(8,128)(2,1)S(1)}, bf16[256,128]{1,0:T(8,128)(2,1)S(1)}, u32[]{:S(2)}, u32[]{:S(2)}) collective-permute-start(bf16[256,128]{1,0:T(8,128)(2,1)S(1)} %get-tuple-element.9), channel_id=1, source_target_pairs={{4,0},{8,4},{12,8},{16,12},{20,16},{24,20},{28,24},{32,28},{36,32}... | collective-permute-start | bytes 196616 | tf_op jit(solution)/shard_map/ppermute | solution.py:224
  9.3 14.7 %shard_map.55 = (f32[16384,128]{1,0:T(8,128)}, f32[128,128]{1,0:T(8,128)}) custom-call(s32[384]{0:T(512)} %reshape.69.index_ref, bf16[256,128]{1,0:T(8,128)(2,1)} %copy-done.1, bf16[16384,128]{1,0:T(8,128)(2,1)} %own_ref.1, bf16[256,128]{1,0:T(8,128)(2,1)} %copy-done.2, bf16[128,3,128,128]{3,2,1,0:T(8,128)(2,1)} %mass_ref.1), custom_call_target="tpu_custom_call" | custom-call | tf_op jit(solution)/shard_map/pallas_call | solution.py:88
  27.2 3.6 %collective-permute-done.3 = f32[128,128]{1,0:T(8,128)S(1)} collective-permute-done((f32[128,128]{1,0:T(8,128)}, f32[128,128]{1,0:T(8,128)S(1)}, u32[]{:S(2)}, u32[]{:S(2)}) %collective-permute-start.3) | collective-permute-done | bytes 65568 | tf_op jit(solution)/shard_map/ppermute | solution.py:111
  31.6 5.8 %collective-permute-start.5 = (f32[128,128]{1,0:T(8,128)S(1)}, f32[128,128]{1,0:T(8,128)S(1)}, u32[]{:S(2)}, u32[]{:S(2)}) collective-permute-start(f32[128,128]{1,0:T(8,128)S(1)} %add_add_fusion.4), channel_id=1, source_target_pairs={{0,16},{4,20},{8,24},{12,28},{16,0},{20,4},{24,8},{28,12},{32,48},... | collective-permute-start | bytes 196616 | tf_op jit(solution)/shard_map/ppermute | solution.py:111
  41.6 5.3 %collective-permute-done.6 = f32[128,128]{1,0:T(8,128)S(1)} collective-permute-done((f32[128,128]{1,0:T(8,128)S(1)}, f32[128,128]{1,0:T(8,128)S(1)}, u32[]{:S(2)}, u32[]{:S(2)}) %collective-permute-start.6) | collective-permute-done | bytes 65568 | tf_op jit(solution)/shard_map/ppermute | solution.py:111
  48.9 2.6 %collective-permute-start.10 = (f32[128,128]{1,0:T(8,128)S(1)}, f32[128,128]{1,0:T(8,128)S(1)}, u32[]{:S(2)}, u32[]{:S(2)}) collective-permute-start(f32[128,128]{1,0:T(8,128)S(1)} %add_add_fusion.3), channel_id=1, source_target_pairs={{0,192},{4,196},{8,200},{12,204},{16,208},{20,212},{24,216},{28,22... | collective-permute-start | bytes 196616 | tf_op jit(solution)/shard_map/ppermute | solution.py:111
  58.6 9.4 %shard_map.56 = f32[1,32,128]{2,1,0:T(8,128)} custom-call(f32[1,128,128]{2,1,0:T(8,128)} %multiply_bitcast_fusion.g_ref, f32[1,32,128]{2,1,0:T(8,128)} %bitcast.47), custom_call_target="tpu_custom_call" | custom-call | tf_op jit(solution)/shard_map/pallas_call | solution.py:163
  68.0 2.7 %fusion.4 = f32[32,4096]{1,0:T(8,128)S(1)} fusion(f32[16384,128]{1,0:T(8,128)} %get-tuple-element.8, s32[]{:T(128)S(6)} %select_n.82, f32[1,32,128]{2,1,0:T(8,128)} %shard_map.56), kind=kOutput, calls=%fused_computation.8 | convolution fusion | flops 100663296 | bytes 2637828 | tf_op jit(solution)/shard_map/dot_general | solution.py:236
  72.3 2.7 %fusion.2 = f32[32,4096]{1,0:T(8,128)S(1)} fusion(f32[16384,128]{1,0:T(8,128)} %get-tuple-element.8, s32[]{:T(128)S(6)} %select_n.84, f32[1,32,128]{2,1,0:T(8,128)S(1)} %copy-done), kind=kOutput, calls=%fused_computation.6 | convolution fusion | flops 100663296 | bytes 2637828 | tf_op jit(solution)/shard_map/dot_general | solution.py:236
  75.0 3.0 %collective-permute-start.12 = (f32[32,4096]{1,0:T(8,128)S(1)}, f32[32,4096]{1,0:T(8,128)S(1)}, u32[]{:S(2)}, u32[]{:S(2)}) collective-permute-start(f32[32,4096]{1,0:T(8,128)S(1)} %fusion.2), channel_id=1, source_target_pairs={{0,2},{1,3},{2,0},{3,1},{4,6},{5,7},{6,4},{7,5},{8,10},{9,11},{10,... | collective-permute-start | bytes 1572872 | tf_op jit(solution)/shard_map/ppermute | solution.py:242
  78.0 2.7 %fusion = f32[32,4096]{1,0:T(8,128)S(1)} fusion(f32[16384,128]{1,0:T(8,128)} %get-tuple-element.8, s32[]{:T(128)S(6)} %select_n.86, f32[1,32,128]{2,1,0:T(8,128)S(1)} %copy-done), kind=kOutput, calls=%fused_computation.4 | convolution fusion | flops 100663296 | bytes 2637828 | tf_op jit(solution)/shard_map/dot_general | solution.py:236
  82.5 2.7 %fusion.6 = f32[32,4096]{1,0:T(8,128)S(1)} fusion(f32[16384,128]{1,0:T(8,128)} %get-tuple-element.8, s32[]{:T(128)S(6)} %select_n.80, f32[1,32,128]{2,1,0:T(8,128)S(1)} %copy-done), kind=kOutput, calls=%fused_computation.10 | convolution fusion | flops 100663296 | bytes 2637828 | tf_op jit(solution)/shard_map/dot_general | solution.py:236
  85.8 10.8 %collective-permute-done.12 = f32[32,4096]{1,0:T(8,128)S(1)} collective-permute-done((f32[32,4096]{1,0:T(8,128)S(1)}, f32[32,4096]{1,0:T(8,128)S(1)}, u32[]{:S(2)}, u32[]{:S(2)}) %collective-permute-start.12) | collective-permute-done | bytes 524320 | tf_op jit(solution)/shard_map/ppermute | solution.py:242
  96.6 2.7 %collective-permute-done.13 = f32[32,4096]{1,0:T(8,128)} collective-permute-done((f32[32,4096]{1,0:T(8,128)S(1)}, f32[32,4096]{1,0:T(8,128)}, u32[]{:S(2)}, u32[]{:S(2)}) %collective-permute-start.13) | collective-permute-done | bytes 524320 | tf_op jit(solution)/shard_map/ppermute | solution.py:242
  99.3 2.3 %fusion.9 = f32[128,128]{1,0:T(8,128)S(1)} fusion(f32[32,4096]{1,0:T(8,128)} %collective-permute-done.13, f32[32,4096]{1,0:T(8,128)S(1)} %collective-permute-done.12, f32[32,4096]{1,0:T(8,128)S(1)} %collective-permute-done.11, f32[32,4096]{1,0:T(8,128)S(1)} %fusion.6), kind=kOutput, calls=%fused_computation.13 | convolution fusion | flops 404226048 | bytes 2162688 | tf_op jit(solution)/shard_map/dot_general | solution.py:246
  105.4 3.2 %collective-permute-done.15 = f32[128,128]{1,0:T(8,128)S(1)} collective-permute-done((f32[128,128]{1,0:T(8,128)S(1)}, f32[128,128]{1,0:T(8,128)S(1)}, u32[]{:S(2)}, u32[]{:S(2)}) %collective-permute-start.15) | collective-permute-done | bytes 65568 | tf_op jit(solution)/shard_map/ppermute | solution.py:111
  110.5 2.7 %collective-permute-start.18 = (f32[128,128]{1,0:T(8,128)S(1)}, f32[128,128]{1,0:T(8,128)S(1)}, u32[]{:S(2)}, u32[]{:S(2)}) collective-permute-start(f32[128,128]{1,0:T(8,128)S(1)} %add_add_fusion.2), channel_id=1, source_target_pairs={{0,32},{4,36},{8,40},{12,44},{16,48},{20,52},{24,56},{28,60},{32,0... | collective-permute-start | bytes 196616 | tf_op jit(solution)/shard_map/ppermute | solution.py:111
  115.5 5.4 %collective-permute-done.18 = f32[128,128]{1,0:T(8,128)S(1)} collective-permute-done((f32[128,128]{1,0:T(8,128)S(1)}, f32[128,128]{1,0:T(8,128)S(1)}, u32[]{:S(2)}, u32[]{:S(2)}) %collective-permute-start.18) | collective-permute-done | bytes 65568 | tf_op jit(solution)/shard_map/ppermute | solution.py:111
  127.3 2.2 %collective-permute-done.21 = f32[128,128]{1,0:T(8,128)S(1)} collective-permute-done((f32[128,128]{1,0:T(8,128)S(1)}, f32[128,128]{1,0:T(8,128)S(1)}, u32[]{:S(2)}, u32[]{:S(2)}) %collective-permute-start.21) | collective-permute-done | bytes 65568 | tf_op jit(solution)/shard_map/ppermute | solution.py:111
  131.0 2.5 %collective-permute-start.23 = (f32[128,128]{1,0:T(8,128)S(1)}, f32[128,128]{1,0:T(8,128)S(1)}, u32[]{:S(2)}, u32[]{:S(2)}) collective-permute-start(f32[128,128]{1,0:T(8,128)S(1)} %add_add_fusion), channel_id=1, source_target_pairs={{0,1},{1,0},{2,3},{3,2},{4,5},{5,4},{6,7},{7,6},{8,9},{9,8},{10,11... | collective-permute-start | bytes 196616 | tf_op jit(solution)/shard_map/ppermute | solution.py:111
  136.2 3.0 %collective-permute-done.24 = f32[128,128]{1,0:T(8,128)S(1)} collective-permute-done((f32[128,128]{1,0:T(8,128)S(1)}, f32[128,128]{1,0:T(8,128)S(1)}, u32[]{:S(2)}, u32[]{:S(2)}) %collective-permute-start.24) | collective-permute-done | bytes 65568 | tf_op jit(solution)/shard_map/ppermute | solution.py:111
  142.0 9.8 %shard_map.57 = f32[2,32,64]{2,1,0:T(8,128)} custom-call(f32[2,64,64]{2,1,0:T(8,128)} %pad_maximum_fusion.3.g_ref, f32[2,32,64]{2,1,0:T(8,128)} %broadcast_in_dim.62.v_ref), custom_call_target="tpu_custom_call" | custom-call | tf_op jit(solution)/shard_map/pallas_call | solution.py:163
  153.7 9.1 %shard_map.58 = f32[1,32,64]{2,1,0:T(8,128)} custom-call(f32[1,64,64]{2,1,0:T(8,128)} %convolution_bitcast_fusion.g_ref, f32[1,32,64]{2,1,0:T(8,128)} %bitcast.45), custom_call_target="tpu_custom_call" | custom-call | tf_op jit(solution)/shard_map/pallas_call | solution.py:163
  164.5 2.6 %fusion.8 = f32[32,4096]{1,0:T(8,128)} fusion(f32[128,32]{1,0:T(8,128)S(1)} %bitcast_select_fusion, f32[32,4096]{1,0:T(8,128)} %collective-permute-done.13, f32[32,4096]{1,0:T(8,128)S(1)} %collective-permute-done.12, f32[32,4096]{1,0:T(8,128)S(1)} %collective-permute-done.11, f32[32,4096]{1,0:T(8,128)S(1)} %fusion.6), kind=kOutput, calls=%fused_computation.12 | convolution fusion | flops 102236160 | bytes 2637824 | tf_op jit(solution)/shard_map/dot_general | solution.py:254
  (81 shorter events, 51.6 us)
Async XLA Ops:
  0.9 7.2 %collective-permute-start = (bf16[256,128]{1,0:T(8,128)(2,1)S(1)}, bf16[256,128]{1,0:T(8,128)(2,1)S(1)}, u32[]{:S(2)}, u32[]{:S(2)}) collective-permute-start(bf16[256,128]{1,0:T(8,128)(2,1)S(1)} %get-tuple-element.10), channel_id=1, source_target_pairs={{0,4},{4,8},{8,12},{12,16},{16,20},{20,24},{24,28},{28,32},{32,36}... | collective-permute-start | bytes 196616 | tf_op jit(solution)/shard_map/ppermute | solution.py:223
  2.8 5.5 %collective-permute-start.1 = (bf16[256,128]{1,0:T(8,128)(2,1)S(1)}, bf16[256,128]{1,0:T(8,128)(2,1)S(1)}, u32[]{:S(2)}, u32[]{:S(2)}) collective-permute-start(bf16[256,128]{1,0:T(8,128)(2,1)S(1)} %get-tuple-element.9), channel_id=1, source_target_pairs={{4,0},{8,4},{12,8},{16,12},{20,16},{24,20},{28,24},{32,28},{36,32}... | collective-permute-start | bytes 196616 | tf_op jit(solution)/shard_map/ppermute | solution.py:224
  25.8 5.0 %collective-permute-start.3 = (f32[128,128]{1,0:T(8,128)}, f32[128,128]{1,0:T(8,128)S(1)}, u32[]{:S(2)}, u32[]{:S(2)}) collective-permute-start(f32[128,128]{1,0:T(8,128)} %get-tuple-element.7), channel_id=1, source_target_pairs={{0,8},{4,12},{8,0},{12,4},{16,24},{20,28},{24,16},{28,20},{32,40},... | collective-permute-start | bytes 196616 | tf_op jit(solution)/shard_map/ppermute | solution.py:111
  25.9 4.9 %collective-permute-start.4 = (f32[128,128]{1,0:T(8,128)}, f32[128,128]{1,0:T(8,128)S(1)}, u32[]{:S(2)}, u32[]{:S(2)}) collective-permute-start(f32[128,128]{1,0:T(8,128)} %get-tuple-element.7), channel_id=1, source_target_pairs={{0,12},{4,8},{8,4},{12,0},{16,28},{20,24},{24,20},{28,16},{32,44},... | collective-permute-start | bytes 196616 | tf_op jit(solution)/shard_map/ppermute | solution.py:111
  31.6 10.0 %collective-permute-start.5 = (f32[128,128]{1,0:T(8,128)S(1)}, f32[128,128]{1,0:T(8,128)S(1)}, u32[]{:S(2)}, u32[]{:S(2)}) collective-permute-start(f32[128,128]{1,0:T(8,128)S(1)} %add_add_fusion.4), channel_id=1, source_target_pairs={{0,16},{4,20},{8,24},{12,28},{16,0},{20,4},{24,8},{28,12},{32,48},... | collective-permute-start | bytes 196616 | tf_op jit(solution)/shard_map/ppermute | solution.py:111
  37.4 9.5 %collective-permute-start.6 = (f32[128,128]{1,0:T(8,128)S(1)}, f32[128,128]{1,0:T(8,128)S(1)}, u32[]{:S(2)}, u32[]{:S(2)}) collective-permute-start(f32[128,128]{1,0:T(8,128)S(1)} %add_add_fusion.4), channel_id=1, source_target_pairs={{0,32},{4,36},{8,40},{12,44},{16,48},{20,52},{24,56},{28,60},{32,0... | collective-permute-start | bytes 196616 | tf_op jit(solution)/shard_map/ppermute | solution.py:111
  39.4 9.5 %collective-permute-start.7 = (f32[128,128]{1,0:T(8,128)S(1)}, f32[128,128]{1,0:T(8,128)S(1)}, u32[]{:S(2)}, u32[]{:S(2)}) collective-permute-start(f32[128,128]{1,0:T(8,128)S(1)} %add_add_fusion.4), channel_id=1, source_target_pairs={{0,48},{4,52},{8,56},{12,60},{16,32},{20,36},{24,40},{28,44},{32,1... | collective-permute-start | bytes 196616 | tf_op jit(solution)/shard_map/ppermute | solution.py:111
  48.9 5.6 %collective-permute-start.10 = (f32[128,128]{1,0:T(8,128)S(1)}, f32[128,128]{1,0:T(8,128)S(1)}, u32[]{:S(2)}, u32[]{:S(2)}) collective-permute-start(f32[128,128]{1,0:T(8,128)S(1)} %add_add_fusion.3), channel_id=1, source_target_pairs={{0,192},{4,196},{8,200},{12,204},{16,208},{20,212},{24,216},{28,22... | collective-permute-start | bytes 196616 | tf_op jit(solution)/shard_map/ppermute | solution.py:111
  51.5 4.4 %collective-permute-start.8 = (f32[128,128]{1,0:T(8,128)S(1)}, f32[128,128]{1,0:T(8,128)S(1)}, u32[]{:S(2)}, u32[]{:S(2)}) collective-permute-start(f32[128,128]{1,0:T(8,128)S(1)} %add_add_fusion.3), channel_id=1, source_target_pairs={{0,64},{4,68},{8,72},{12,76},{16,80},{20,84},{24,88},{28,92},{32,9... | collective-permute-start | bytes 196616 | tf_op jit(solution)/shard_map/ppermute | solution.py:111
  52.2 5.8 %collective-permute-start.9 = (f32[128,128]{1,0:T(8,128)S(1)}, f32[128,128]{1,0:T(8,128)S(1)}, u32[]{:S(2)}, u32[]{:S(2)}) collective-permute-start(f32[128,128]{1,0:T(8,128)S(1)} %add_add_fusion.3), channel_id=1, source_target_pairs={{0,128},{4,132},{8,136},{12,140},{16,144},{20,148},{24,152},{28,15... | collective-permute-start | bytes 196616 | tf_op jit(solution)/shard_map/ppermute | solution.py:111
  70.7 15.1 %collective-permute-start.11 = (f32[32,4096]{1,0:T(8,128)S(1)}, f32[32,4096]{1,0:T(8,128)S(1)}, u32[]{:S(2)}, u32[]{:S(2)}) collective-permute-start(f32[32,4096]{1,0:T(8,128)S(1)} %fusion.4), channel_id=1, source_target_pairs={{0,1},{1,2},{2,3},{3,0},{4,5},{5,6},{6,7},{7,4},{8,9},{9,10},{10,1... | collective-permute-start | bytes 1572872 | tf_op jit(solution)/shard_map/ppermute | solution.py:242
  75.0 21.6 %collective-permute-start.12 = (f32[32,4096]{1,0:T(8,128)S(1)}, f32[32,4096]{1,0:T(8,128)S(1)}, u32[]{:S(2)}, u32[]{:S(2)}) collective-permute-start(f32[32,4096]{1,0:T(8,128)S(1)} %fusion.2), channel_id=1, source_target_pairs={{0,2},{1,3},{2,0},{3,1},{4,6},{5,7},{6,4},{7,5},{8,10},{9,11},{10,... | collective-permute-start | bytes 1572872 | tf_op jit(solution)/shard_map/ppermute | solution.py:242
  80.7 18.6 %collective-permute-start.13 = (f32[32,4096]{1,0:T(8,128)S(1)}, f32[32,4096]{1,0:T(8,128)}, u32[]{:S(2)}, u32[]{:S(2)}) collective-permute-start(f32[32,4096]{1,0:T(8,128)S(1)} %fusion), channel_id=1, source_target_pairs={{0,3},{1,0},{2,1},{3,2},{4,7},{5,4},{6,5},{7,6},{8,11},{9,8},{10,9... | collective-permute-start | bytes 1572872 | tf_op jit(solution)/shard_map/ppermute | solution.py:242
  103.6 5.1 %collective-permute-start.15 = (f32[128,128]{1,0:T(8,128)S(1)}, f32[128,128]{1,0:T(8,128)S(1)}, u32[]{:S(2)}, u32[]{:S(2)}) collective-permute-start(f32[128,128]{1,0:T(8,128)S(1)} %broadcast_select_fusion.1), channel_id=1, source_target_pairs={{0,8},{4,12},{8,0},{12,4},{16,24},{20,28},{24,16},{28,20},{32,40},... | collective-permute-start | bytes 196616 | tf_op jit(solution)/shard_map/ppermute | solution.py:111
  103.7 5.2 %collective-permute-start.16 = (f32[128,128]{1,0:T(8,128)S(1)}, f32[128,128]{1,0:T(8,128)S(1)}, u32[]{:S(2)}, u32[]{:S(2)}) collective-permute-start(f32[128,128]{1,0:T(8,128)S(1)} %broadcast_select_fusion.1), channel_id=1, source_target_pairs={{0,12},{4,8},{8,4},{12,0},{16,28},{20,24},{24,20},{28,16},{32,44},... | collective-permute-start | bytes 196616 | tf_op jit(solution)/shard_map/ppermute | solution.py:111
  108.9 6.6 %collective-permute-start.17 = (f32[128,128]{1,0:T(8,128)S(1)}, f32[128,128]{1,0:T(8,128)S(1)}, u32[]{:S(2)}, u32[]{:S(2)}) collective-permute-start(f32[128,128]{1,0:T(8,128)S(1)} %add_add_fusion.2), channel_id=1, source_target_pairs={{0,16},{4,20},{8,24},{12,28},{16,0},{20,4},{24,8},{28,12},{32,48},... | collective-permute-start | bytes 196616 | tf_op jit(solution)/shard_map/ppermute | solution.py:111
  110.5 10.4 %collective-permute-start.18 = (f32[128,128]{1,0:T(8,128)S(1)}, f32[128,128]{1,0:T(8,128)S(1)}, u32[]{:S(2)}, u32[]{:S(2)}) collective-permute-start(f32[128,128]{1,0:T(8,128)S(1)} %add_add_fusion.2), channel_id=1, source_target_pairs={{0,32},{4,36},{8,40},{12,44},{16,48},{20,52},{24,56},{28,60},{32,0... | collective-permute-start | bytes 196616 | tf_op jit(solution)/shard_map/ppermute | solution.py:111
  113.2 9.2 %collective-permute-start.19 = (f32[128,128]{1,0:T(8,128)S(1)}, f32[128,128]{1,0:T(8,128)S(1)}, u32[]{:S(2)}, u32[]{:S(2)}) collective-permute-start(f32[128,128]{1,0:T(8,128)S(1)} %add_add_fusion.2), channel_id=1, source_target_pairs={{0,48},{4,52},{8,56},{12,60},{16,32},{20,36},{24,40},{28,44},{32,1... | collective-permute-start | bytes 196616 | tf_op jit(solution)/shard_map/ppermute | solution.py:111
  122.4 4.9 %collective-permute-start.20 = (f32[128,128]{1,0:T(8,128)S(1)}, f32[128,128]{1,0:T(8,128)S(1)}, u32[]{:S(2)}, u32[]{:S(2)}) collective-permute-start(f32[128,128]{1,0:T(8,128)S(1)} %add_add_fusion.1), channel_id=1, source_target_pairs={{0,64},{4,68},{8,72},{12,76},{16,80},{20,84},{24,88},{28,92},{32,9... | collective-permute-start | bytes 196616 | tf_op jit(solution)/shard_map/ppermute | solution.py:111
  123.7 5.9 %collective-permute-start.21 = (f32[128,128]{1,0:T(8,128)S(1)}, f32[128,128]{1,0:T(8,128)S(1)}, u32[]{:S(2)}, u32[]{:S(2)}) collective-permute-start(f32[128,128]{1,0:T(8,128)S(1)} %add_add_fusion.1), channel_id=1, source_target_pairs={{0,128},{4,132},{8,136},{12,140},{16,144},{20,148},{24,152},{28,15... | collective-permute-start | bytes 196616 | tf_op jit(solution)/shard_map/ppermute | solution.py:111
  125.5 5.5 %collective-permute-start.22 = (f32[128,128]{1,0:T(8,128)S(1)}, f32[128,128]{1,0:T(8,128)S(1)}, u32[]{:S(2)}, u32[]{:S(2)}) collective-permute-start(f32[128,128]{1,0:T(8,128)S(1)} %add_add_fusion.1), channel_id=1, source_target_pairs={{0,192},{4,196},{8,200},{12,204},{16,208},{20,212},{24,216},{28,22... | collective-permute-start | bytes 196616 | tf_op jit(solution)/shard_map/ppermute | solution.py:111
  131.0 5.2 %collective-permute-start.23 = (f32[128,128]{1,0:T(8,128)S(1)}, f32[128,128]{1,0:T(8,128)S(1)}, u32[]{:S(2)}, u32[]{:S(2)}) collective-permute-start(f32[128,128]{1,0:T(8,128)S(1)} %add_add_fusion), channel_id=1, source_target_pairs={{0,1},{1,0},{2,3},{3,2},{4,5},{5,4},{6,7},{7,6},{8,9},{9,8},{10,11... | collective-permute-start | bytes 196616 | tf_op jit(solution)/shard_map/ppermute | solution.py:111
  133.4 5.8 %collective-permute-start.24 = (f32[128,128]{1,0:T(8,128)S(1)}, f32[128,128]{1,0:T(8,128)S(1)}, u32[]{:S(2)}, u32[]{:S(2)}) collective-permute-start(f32[128,128]{1,0:T(8,128)S(1)} %add_add_fusion), channel_id=1, source_target_pairs={{0,2},{1,3},{2,0},{3,1},{4,6},{5,7},{6,4},{7,5},{8,10},{9,11},{10,... | collective-permute-start | bytes 196616 | tf_op jit(solution)/shard_map/ppermute | solution.py:111
  135.1 5.5 %collective-permute-start.25 = (f32[128,128]{1,0:T(8,128)S(1)}, f32[128,128]{1,0:T(8,128)S(1)}, u32[]{:S(2)}, u32[]{:S(2)}) collective-permute-start(f32[128,128]{1,0:T(8,128)S(1)} %add_add_fusion), channel_id=1, source_target_pairs={{0,3},{1,2},{2,1},{3,0},{4,7},{5,6},{6,5},{7,4},{8,11},{9,10},{10,... | collective-permute-start | bytes 196616 | tf_op jit(solution)/shard_map/ppermute | solution.py:111
  (6 other events, 50.2 us)

commit v4 on v3

--- a/solution.py
+++ b/solution.py
@@ -141,11 +141,11 @@
                 row = jnp.sum(jnp.where(sub == j, inner, 0.0), axis=0, keepdims=True)
                 col = jnp.sum(jnp.where(lane == j, inner, 0.0), axis=1, keepdims=True)
                 pivot = jnp.sum(jnp.where(lane[:1] == j, row, 0.0), axis=1, keepdims=True)
-                root = jnp.sqrt(pivot)
-                factor_row = jnp.where(lane[:1] >= j, row / root, 0.0)
-                factor_col = jnp.where(sub[:, :1] >= j, col / root, 0.0)
+                scale = lax.rsqrt(pivot)
+                factor_row = jnp.where(lane[:1] >= j, row * scale, 0.0)
+                factor_col = jnp.where(sub[:, :1] >= j, col * scale, 0.0)
                 inner = inner - factor_col * factor_row
-                answer = jnp.sum(jnp.where(sub_wide == j, rest, 0.0), axis=0, keepdims=True) / root
+                answer = jnp.sum(jnp.where(sub_wide == j, rest, 0.0), axis=0, keepdims=True) * scale
                 rest = rest - factor_col * answer
                 solved = jnp.where(sub_wide == j, answer, solved)
                 out.append((inner, rest, solved))

time: 168 us -> 165 us (0.982)
  Pallas kernels: 43 us -> 40.7 us
    pallas_call x3, Pallas kernels: 28.3 us -> 26 us  [subspace_batch(): pl.pallas_call(subspace_kernel, out_shape=jax.ShapeDtypeStruct((batch, ra...]
where the time goes in v4:
time: 165 us
  waiting for transfers between devices  48.4 us (29%)
  starting transfers between devices  47.6 us (29%)
  Pallas kernels  40.7 us (25%)
  matrix products  17.8 us (11%)
  local copies, waits for them, and re-layouts  6.66 us (4%)
  other arithmetic  3.21 us (2%)
    ppermute x21, starting transfers between devices, butterfly_sum(): parts.append(lax.ppermute(x, axis, pairs))  35.9 us
    ppermute x21, waiting for transfers between devices, butterfly_sum(): parts.append(lax.ppermute(x, axis, pairs))  34.2 us
    pallas_call x3, Pallas kernels, subspace_batch(): pl.pallas_call(subspace_kernel, out_shape=jax.ShapeDtypeStruct((batch, ra...  26 us
    pallas_call x1, Pallas kernels, apply_mass(): pl.pallas_call(mass_kernel, grid_spec=grid_spec, out_shape=[jax.ShapeDtyp...  14.7 us
    ppermute x3, waiting for transfers between devices, shards(): received[shift] = lax.ppermute(piece, 'freq', pairs)  14 us
    dot_general x4, matrix products, modes_of(): lax.dot_general(weights, rows_part, (((0,), (1,)), ((), ())), precision=H...  10.9 us
    ppermute x3, starting transfers between devices, shards(): received[shift] = lax.ppermute(piece, 'freq', pairs)  6.08 us
    ppermute x1, starting transfers between devices, shards(): high = lax.ppermute(snapshots[:width], 'rows', backward)  3.64 us
  transfers between devices with their start and end apart: 26, of which 20 were waited for; matrix products, arithmetic and copies ran while one was open for 6% of the time, Pallas kernels for 0%

profile of v4, /device:TPU:32, one launch (start us, length us, event | category | flops | bytes accessed | tf_op | source)
XLA Modules:
  0.0 164.6 jit_solution(3094017165615427290)
XLA Ops:
  2.8 3.6 %collective-permute-start.1 = (bf16[256,128]{1,0:T(8,128)(2,1)S(1)}, bf16[256,128]{1,0:T(8,128)(2,1)S(1)}, u32[]{:S(2)}, u32[]{:S(2)}) collective-permute-start(bf16[256,128]{1,0:T(8,128)(2,1)S(1)} %get-tuple-element.9), channel_id=1, source_target_pairs={{4,0},{8,4},{12,8},{16,12},{20,16},{24,20},{28,24},{32,28},{36,32}... | collective-permute-start | bytes 196616 | tf_op jit(solution)/shard_map/ppermute | solution.py:224
  9.3 14.7 %shard_map.55 = (f32[16384,128]{1,0:T(8,128)}, f32[128,128]{1,0:T(8,128)}) custom-call(s32[384]{0:T(512)} %reshape.69.index_ref, bf16[256,128]{1,0:T(8,128)(2,1)} %copy-done.1, bf16[16384,128]{1,0:T(8,128)(2,1)} %own_ref.1, bf16[256,128]{1,0:T(8,128)(2,1)} %copy-done.2, bf16[128,3,128,128]{3,2,1,0:T(8,128)(2,1)} %mass_ref.1), custom_call_target="tpu_custom_call" | custom-call | tf_op jit(solution)/shard_map/pallas_call | solution.py:88
  27.2 3.6 %collective-permute-done.3 = f32[128,128]{1,0:T(8,128)S(1)} collective-permute-done((f32[128,128]{1,0:T(8,128)}, f32[128,128]{1,0:T(8,128)S(1)}, u32[]{:S(2)}, u32[]{:S(2)}) %collective-permute-start.3) | collective-permute-done | bytes 65568 | tf_op jit(solution)/shard_map/ppermute | solution.py:111
  31.6 5.8 %collective-permute-start.5 = (f32[128,128]{1,0:T(8,128)S(1)}, f32[128,128]{1,0:T(8,128)S(1)}, u32[]{:S(2)}, u32[]{:S(2)}) collective-permute-start(f32[128,128]{1,0:T(8,128)S(1)} %add_add_fusion.4), channel_id=1, source_target_pairs={{0,16},{4,20},{8,24},{12,28},{16,0},{20,4},{24,8},{28,12},{32,48},... | collective-permute-start | bytes 196616 | tf_op jit(solution)/shard_map/ppermute | solution.py:111
  41.6 5.3 %collective-permute-done.6 = f32[128,128]{1,0:T(8,128)S(1)} collective-permute-done((f32[128,128]{1,0:T(8,128)S(1)}, f32[128,128]{1,0:T(8,128)S(1)}, u32[]{:S(2)}, u32[]{:S(2)}) %collective-permute-start.6) | collective-permute-done | bytes 65568 | tf_op jit(solution)/shard_map/ppermute | solution.py:111
  48.9 2.6 %collective-permute-start.10 = (f32[128,128]{1,0:T(8,128)S(1)}, f32[128,128]{1,0:T(8,128)S(1)}, u32[]{:S(2)}, u32[]{:S(2)}) collective-permute-start(f32[128,128]{1,0:T(8,128)S(1)} %add_add_fusion.3), channel_id=1, source_target_pairs={{0,192},{4,196},{8,200},{12,204},{16,208},{20,212},{24,216},{28,22... | collective-permute-start | bytes 196616 | tf_op jit(solution)/shard_map/ppermute | solution.py:111
  58.6 8.6 %shard_map.56 = f32[1,32,128]{2,1,0:T(8,128)} custom-call(f32[1,128,128]{2,1,0:T(8,128)} %multiply_bitcast_fusion.g_ref, f32[1,32,128]{2,1,0:T(8,128)} %bitcast.47), custom_call_target="tpu_custom_call" | custom-call | tf_op jit(solution)/shard_map/pallas_call | solution.py:163
  67.2 2.7 %fusion.4 = f32[32,4096]{1,0:T(8,128)S(1)} fusion(f32[16384,128]{1,0:T(8,128)} %get-tuple-element.8, s32[]{:T(128)S(6)} %select_n.82, f32[1,32,128]{2,1,0:T(8,128)} %shard_map.56), kind=kOutput, calls=%fused_computation.8 | convolution fusion | flops 100663296 | bytes 2637828 | tf_op jit(solution)/shard_map/dot_general | solution.py:236
  71.5 2.7 %fusion.2 = f32[32,4096]{1,0:T(8,128)S(1)} fusion(f32[16384,128]{1,0:T(8,128)} %get-tuple-element.8, s32[]{:T(128)S(6)} %select_n.84, f32[1,32,128]{2,1,0:T(8,128)S(1)} %copy-done), kind=kOutput, calls=%fused_computation.6 | convolution fusion | flops 100663296 | bytes 2637828 | tf_op jit(solution)/shard_map/dot_general | solution.py:236
  74.2 2.8 %collective-permute-start.12 = (f32[32,4096]{1,0:T(8,128)S(1)}, f32[32,4096]{1,0:T(8,128)S(1)}, u32[]{:S(2)}, u32[]{:S(2)}) collective-permute-start(f32[32,4096]{1,0:T(8,128)S(1)} %fusion.2), channel_id=1, source_target_pairs={{0,2},{1,3},{2,0},{3,1},{4,6},{5,7},{6,4},{7,5},{8,10},{9,11},{10,... | collective-permute-start | bytes 1572872 | tf_op jit(solution)/shard_map/ppermute | solution.py:242
  77.1 2.7 %fusion = f32[32,4096]{1,0:T(8,128)S(1)} fusion(f32[16384,128]{1,0:T(8,128)} %get-tuple-element.8, s32[]{:T(128)S(6)} %select_n.86, f32[1,32,128]{2,1,0:T(8,128)S(1)} %copy-done), kind=kOutput, calls=%fused_computation.4 | convolution fusion | flops 100663296 | bytes 2637828 | tf_op jit(solution)/shard_map/dot_general | solution.py:236
  81.7 2.7 %fusion.6 = f32[32,4096]{1,0:T(8,128)S(1)} fusion(f32[16384,128]{1,0:T(8,128)} %get-tuple-element.8, s32[]{:T(128)S(6)} %select_n.80, f32[1,32,128]{2,1,0:T(8,128)S(1)} %copy-done), kind=kOutput, calls=%fused_computation.10 | convolution fusion | flops 100663296 | bytes 2637828 | tf_op jit(solution)/shard_map/dot_general | solution.py:236
  85.1 10.8 %collective-permute-done.12 = f32[32,4096]{1,0:T(8,128)S(1)} collective-permute-done((f32[32,4096]{1,0:T(8,128)S(1)}, f32[32,4096]{1,0:T(8,128)S(1)}, u32[]{:S(2)}, u32[]{:S(2)}) %collective-permute-start.12) | collective-permute-done | bytes 524320 | tf_op jit(solution)/shard_map/ppermute | solution.py:242
  95.8 2.6 %collective-permute-done.13 = f32[32,4096]{1,0:T(8,128)} collective-permute-done((f32[32,4096]{1,0:T(8,128)S(1)}, f32[32,4096]{1,0:T(8,128)}, u32[]{:S(2)}, u32[]{:S(2)}) %collective-permute-start.13) | collective-permute-done | bytes 524320 | tf_op jit(solution)/shard_map/ppermute | solution.py:242
  98.4 2.3 %fusion.9 = f32[128,128]{1,0:T(8,128)S(1)} fusion(f32[32,4096]{1,0:T(8,128)} %collective-permute-done.13, f32[32,4096]{1,0:T(8,128)S(1)} %collective-permute-done.12, f32[32,4096]{1,0:T(8,128)S(1)} %collective-permute-done.11, f32[32,4096]{1,0:T(8,128)S(1)} %fusion.6), kind=kOutput, calls=%fused_computation.13 | convolution fusion | flops 404226048 | bytes 2162688 | tf_op jit(solution)/shard_map/dot_general | solution.py:246
  104.5 3.2 %collective-permute-done.15 = f32[128,128]{1,0:T(8,128)S(1)} collective-permute-done((f32[128,128]{1,0:T(8,128)S(1)}, f32[128,128]{1,0:T(8,128)S(1)}, u32[]{:S(2)}, u32[]{:S(2)}) %collective-permute-start.15) | collective-permute-done | bytes 65568 | tf_op jit(solution)/shard_map/ppermute | solution.py:111
  109.6 2.7 %collective-permute-start.18 = (f32[128,128]{1,0:T(8,128)S(1)}, f32[128,128]{1,0:T(8,128)S(1)}, u32[]{:S(2)}, u32[]{:S(2)}) collective-permute-start(f32[128,128]{1,0:T(8,128)S(1)} %add_add_fusion.2), channel_id=1, source_target_pairs={{0,32},{4,36},{8,40},{12,44},{16,48},{20,52},{24,56},{28,60},{32,0... | collective-permute-start | bytes 196616 | tf_op jit(solution)/shard_map/ppermute | solution.py:111
  112.3 2.2 %collective-permute-start.19 = (f32[128,128]{1,0:T(8,128)S(1)}, f32[128,128]{1,0:T(8,128)S(1)}, u32[]{:S(2)}, u32[]{:S(2)}) collective-permute-start(f32[128,128]{1,0:T(8,128)S(1)} %add_add_fusion.2), channel_id=1, source_target_pairs={{0,48},{4,52},{8,56},{12,60},{16,32},{20,36},{24,40},{28,44},{32,1... | collective-permute-start | bytes 196616 | tf_op jit(solution)/shard_map/ppermute | solution.py:111
  114.5 5.4 %collective-permute-done.18 = f32[128,128]{1,0:T(8,128)S(1)} collective-permute-done((f32[128,128]{1,0:T(8,128)S(1)}, f32[128,128]{1,0:T(8,128)S(1)}, u32[]{:S(2)}, u32[]{:S(2)}) %collective-permute-start.18) | collective-permute-done | bytes 65568 | tf_op jit(solution)/shard_map/ppermute | solution.py:111
  130.0 2.5 %collective-permute-start.23 = (f32[128,128]{1,0:T(8,128)S(1)}, f32[128,128]{1,0:T(8,128)S(1)}, u32[]{:S(2)}, u32[]{:S(2)}) collective-permute-start(f32[128,128]{1,0:T(8,128)S(1)} %add_add_fusion), channel_id=1, source_target_pairs={{0,1},{1,0},{2,3},{3,2},{4,5},{5,4},{6,7},{7,6},{8,9},{9,8},{10,11... | collective-permute-start | bytes 196616 | tf_op jit(solution)/shard_map/ppermute | solution.py:111
  135.2 3.0 %collective-permute-done.24 = f32[128,128]{1,0:T(8,128)S(1)} collective-permute-done((f32[128,128]{1,0:T(8,128)S(1)}, f32[128,128]{1,0:T(8,128)S(1)}, u32[]{:S(2)}, u32[]{:S(2)}) %collective-permute-start.24) | collective-permute-done | bytes 65568 | tf_op jit(solution)/shard_map/ppermute | solution.py:111
  141.0 9.0 %shard_map.57 = f32[2,32,64]{2,1,0:T(8,128)} custom-call(f32[2,64,64]{2,1,0:T(8,128)} %pad_maximum_fusion.3.g_ref, f32[2,32,64]{2,1,0:T(8,128)} %broadcast_in_dim.62.v_ref), custom_call_target="tpu_custom_call" | custom-call | tf_op jit(solution)/shard_map/pallas_call | solution.py:163
  152.0 8.4 %shard_map.58 = f32[1,32,64]{2,1,0:T(8,128)} custom-call(f32[1,64,64]{2,1,0:T(8,128)} %convolution_bitcast_fusion.g_ref, f32[1,32,64]{2,1,0:T(8,128)} %bitcast.45), custom_call_target="tpu_custom_call" | custom-call | tf_op jit(solution)/shard_map/pallas_call | solution.py:163
  162.0 2.6 %fusion.8 = f32[32,4096]{1,0:T(8,128)} fusion(f32[128,32]{1,0:T(8,128)S(1)} %bitcast_select_fusion, f32[32,4096]{1,0:T(8,128)} %collective-permute-done.13, f32[32,4096]{1,0:T(8,128)S(1)} %collective-permute-done.12, f32[32,4096]{1,0:T(8,128)S(1)} %collective-permute-done.11, f32[32,4096]{1,0:T(8,128)S(1)} %fusion.6), kind=kOutput, calls=%fused_computation.12 | convolution fusion | flops 102236160 | bytes 2637824 | tf_op jit(solution)/shard_map/dot_general | solution.py:254
  (81 shorter events, 51.8 us)
Async XLA Ops:
  0.9 7.2 %collective-permute-start = (bf16[256,128]{1,0:T(8,128)(2,1)S(1)}, bf16[256,128]{1,0:T(8,128)(2,1)S(1)}, u32[]{:S(2)}, u32[]{:S(2)}) collective-permute-start(bf16[256,128]{1,0:T(8,128)(2,1)S(1)} %get-tuple-element.10), channel_id=1, source_target_pairs={{0,4},{4,8},{8,12},{12,16},{16,20},{20,24},{24,28},{28,32},{32,36}... | collective-permute-start | bytes 196616 | tf_op jit(solution)/shard_map/ppermute | solution.py:223
  2.8 5.5 %collective-permute-start.1 = (bf16[256,128]{1,0:T(8,128)(2,1)S(1)}, bf16[256,128]{1,0:T(8,128)(2,1)S(1)}, u32[]{:S(2)}, u32[]{:S(2)}) collective-permute-start(bf16[256,128]{1,0:T(8,128)(2,1)S(1)} %get-tuple-element.9), channel_id=1, source_target_pairs={{4,0},{8,4},{12,8},{16,12},{20,16},{24,20},{28,24},{32,28},{36,32}... | collective-permute-start | bytes 196616 | tf_op jit(solution)/shard_map/ppermute | solution.py:224
  25.8 5.0 %collective-permute-start.3 = (f32[128,128]{1,0:T(8,128)}, f32[128,128]{1,0:T(8,128)S(1)}, u32[]{:S(2)}, u32[]{:S(2)}) collective-permute-start(f32[128,128]{1,0:T(8,128)} %get-tuple-element.7), channel_id=1, source_target_pairs={{0,8},{4,12},{8,0},{12,4},{16,24},{20,28},{24,16},{28,20},{32,40},... | collective-permute-start | bytes 196616 | tf_op jit(solution)/shard_map/ppermute | solution.py:111
  25.9 4.9 %collective-permute-start.4 = (f32[128,128]{1,0:T(8,128)}, f32[128,128]{1,0:T(8,128)S(1)}, u32[]{:S(2)}, u32[]{:S(2)}) collective-permute-start(f32[128,128]{1,0:T(8,128)} %get-tuple-element.7), channel_id=1, source_target_pairs={{0,12},{4,8},{8,4},{12,0},{16,28},{20,24},{24,20},{28,16},{32,44},... | collective-permute-start | bytes 196616 | tf_op jit(solution)/shard_map/ppermute | solution.py:111
  31.6 10.0 %collective-permute-start.5 = (f32[128,128]{1,0:T(8,128)S(1)}, f32[128,128]{1,0:T(8,128)S(1)}, u32[]{:S(2)}, u32[]{:S(2)}) collective-permute-start(f32[128,128]{1,0:T(8,128)S(1)} %add_add_fusion.4), channel_id=1, source_target_pairs={{0,16},{4,20},{8,24},{12,28},{16,0},{20,4},{24,8},{28,12},{32,48},... | collective-permute-start | bytes 196616 | tf_op jit(solution)/shard_map/ppermute | solution.py:111
  37.4 9.5 %collective-permute-start.6 = (f32[128,128]{1,0:T(8,128)S(1)}, f32[128,128]{1,0:T(8,128)S(1)}, u32[]{:S(2)}, u32[]{:S(2)}) collective-permute-start(f32[128,128]{1,0:T(8,128)S(1)} %add_add_fusion.4), channel_id=1, source_target_pairs={{0,32},{4,36},{8,40},{12,44},{16,48},{20,52},{24,56},{28,60},{32,0... | collective-permute-start | bytes 196616 | tf_op jit(solution)/shard_map/ppermute | solution.py:111
  39.4 9.5 %collective-permute-start.7 = (f32[128,128]{1,0:T(8,128)S(1)}, f32[128,128]{1,0:T(8,128)S(1)}, u32[]{:S(2)}, u32[]{:S(2)}) collective-permute-start(f32[128,128]{1,0:T(8,128)S(1)} %add_add_fusion.4), channel_id=1, source_target_pairs={{0,48},{4,52},{8,56},{12,60},{16,32},{20,36},{24,40},{28,44},{32,1... | collective-permute-start | bytes 196616 | tf_op jit(solution)/shard_map/ppermute | solution.py:111
  48.9 5.6 %collective-permute-start.10 = (f32[128,128]{1,0:T(8,128)S(1)}, f32[128,128]{1,0:T(8,128)S(1)}, u32[]{:S(2)}, u32[]{:S(2)}) collective-permute-start(f32[128,128]{1,0:T(8,128)S(1)} %add_add_fusion.3), channel_id=1, source_target_pairs={{0,192},{4,196},{8,200},{12,204},{16,208},{20,212},{24,216},{28,22... | collective-permute-start | bytes 196616 | tf_op jit(solution)/shard_map/ppermute | solution.py:111
  51.5 4.4 %collective-permute-start.8 = (f32[128,128]{1,0:T(8,128)S(1)}, f32[128,128]{1,0:T(8,128)S(1)}, u32[]{:S(2)}, u32[]{:S(2)}) collective-permute-start(f32[128,128]{1,0:T(8,128)S(1)} %add_add_fusion.3), channel_id=1, source_target_pairs={{0,64},{4,68},{8,72},{12,76},{16,80},{20,84},{24,88},{28,92},{32,9... | collective-permute-start | bytes 196616 | tf_op jit(solution)/shard_map/ppermute | solution.py:111
  52.2 5.8 %collective-permute-start.9 = (f32[128,128]{1,0:T(8,128)S(1)}, f32[128,128]{1,0:T(8,128)S(1)}, u32[]{:S(2)}, u32[]{:S(2)}) collective-permute-start(f32[128,128]{1,0:T(8,128)S(1)} %add_add_fusion.3), channel_id=1, source_target_pairs={{0,128},{4,132},{8,136},{12,140},{16,144},{20,148},{24,152},{28,15... | collective-permute-start | bytes 196616 | tf_op jit(solution)/shard_map/ppermute | solution.py:111
  69.9 15.1 %collective-permute-start.11 = (f32[32,4096]{1,0:T(8,128)S(1)}, f32[32,4096]{1,0:T(8,128)S(1)}, u32[]{:S(2)}, u32[]{:S(2)}) collective-permute-start(f32[32,4096]{1,0:T(8,128)S(1)} %fusion.4), channel_id=1, source_target_pairs={{0,1},{1,2},{2,3},{3,0},{4,5},{5,6},{6,7},{7,4},{8,9},{9,10},{10,1... | collective-permute-start | bytes 1572872 | tf_op jit(solution)/shard_map/ppermute | solution.py:242
  74.2 21.6 %collective-permute-start.12 = (f32[32,4096]{1,0:T(8,128)S(1)}, f32[32,4096]{1,0:T(8,128)S(1)}, u32[]{:S(2)}, u32[]{:S(2)}) collective-permute-start(f32[32,4096]{1,0:T(8,128)S(1)} %fusion.2), channel_id=1, source_target_pairs={{0,2},{1,3},{2,0},{3,1},{4,6},{5,7},{6,4},{7,5},{8,10},{9,11},{10,... | collective-permute-start | bytes 1572872 | tf_op jit(solution)/shard_map/ppermute | solution.py:242
  79.8 18.6 %collective-permute-start.13 = (f32[32,4096]{1,0:T(8,128)S(1)}, f32[32,4096]{1,0:T(8,128)}, u32[]{:S(2)}, u32[]{:S(2)}) collective-permute-start(f32[32,4096]{1,0:T(8,128)S(1)} %fusion), channel_id=1, source_target_pairs={{0,3},{1,0},{2,1},{3,2},{4,7},{5,4},{6,5},{7,6},{8,11},{9,8},{10,9... | collective-permute-start | bytes 1572872 | tf_op jit(solution)/shard_map/ppermute | solution.py:242
  102.6 5.1 %collective-permute-start.15 = (f32[128,128]{1,0:T(8,128)S(1)}, f32[128,128]{1,0:T(8,128)S(1)}, u32[]{:S(2)}, u32[]{:S(2)}) collective-permute-start(f32[128,128]{1,0:T(8,128)S(1)} %broadcast_select_fusion.1), channel_id=1, source_target_pairs={{0,8},{4,12},{8,0},{12,4},{16,24},{20,28},{24,16},{28,20},{32,40},... | collective-permute-start | bytes 196616 | tf_op jit(solution)/shard_map/ppermute | solution.py:111
  102.7 5.2 %collective-permute-start.16 = (f32[128,128]{1,0:T(8,128)S(1)}, f32[128,128]{1,0:T(8,128)S(1)}, u32[]{:S(2)}, u32[]{:S(2)}) collective-permute-start(f32[128,128]{1,0:T(8,128)S(1)} %broadcast_select_fusion.1), channel_id=1, source_target_pairs={{0,12},{4,8},{8,4},{12,0},{16,28},{20,24},{24,20},{28,16},{32,44},... | collective-permute-start | bytes 196616 | tf_op jit(solution)/shard_map/ppermute | solution.py:111
  108.0 6.6 %collective-permute-start.17 = (f32[128,128]{1,0:T(8,128)S(1)}, f32[128,128]{1,0:T(8,128)S(1)}, u32[]{:S(2)}, u32[]{:S(2)}) collective-permute-start(f32[128,128]{1,0:T(8,128)S(1)} %add_add_fusion.2), channel_id=1, source_target_pairs={{0,16},{4,20},{8,24},{12,28},{16,0},{20,4},{24,8},{28,12},{32,48},... | collective-permute-start | bytes 196616 | tf_op jit(solution)/shard_map/ppermute | solution.py:111
  109.6 10.4 %collective-permute-start.18 = (f32[128,128]{1,0:T(8,128)S(1)}, f32[128,128]{1,0:T(8,128)S(1)}, u32[]{:S(2)}, u32[]{:S(2)}) collective-permute-start(f32[128,128]{1,0:T(8,128)S(1)} %add_add_fusion.2), channel_id=1, source_target_pairs={{0,32},{4,36},{8,40},{12,44},{16,48},{20,52},{24,56},{28,60},{32,0... | collective-permute-start | bytes 196616 | tf_op jit(solution)/shard_map/ppermute | solution.py:111
  112.3 9.2 %collective-permute-start.19 = (f32[128,128]{1,0:T(8,128)S(1)}, f32[128,128]{1,0:T(8,128)S(1)}, u32[]{:S(2)}, u32[]{:S(2)}) collective-permute-start(f32[128,128]{1,0:T(8,128)S(1)} %add_add_fusion.2), channel_id=1, source_target_pairs={{0,48},{4,52},{8,56},{12,60},{16,32},{20,36},{24,40},{28,44},{32,1... | collective-permute-start | bytes 196616 | tf_op jit(solution)/shard_map/ppermute | solution.py:111
  121.5 4.9 %collective-permute-start.20 = (f32[128,128]{1,0:T(8,128)S(1)}, f32[128,128]{1,0:T(8,128)S(1)}, u32[]{:S(2)}, u32[]{:S(2)}) collective-permute-start(f32[128,128]{1,0:T(8,128)S(1)} %add_add_fusion.1), channel_id=1, source_target_pairs={{0,64},{4,68},{8,72},{12,76},{16,80},{20,84},{24,88},{28,92},{32,9... | collective-permute-start | bytes 196616 | tf_op jit(solution)/shard_map/ppermute | solution.py:111
  122.8 5.9 %collective-permute-start.21 = (f32[128,128]{1,0:T(8,128)S(1)}, f32[128,128]{1,0:T(8,128)S(1)}, u32[]{:S(2)}, u32[]{:S(2)}) collective-permute-start(f32[128,128]{1,0:T(8,128)S(1)} %add_add_fusion.1), channel_id=1, source_target_pairs={{0,128},{4,132},{8,136},{12,140},{16,144},{20,148},{24,152},{28,15... | collective-permute-start | bytes 196616 | tf_op jit(solution)/shard_map/ppermute | solution.py:111
  124.5 5.5 %collective-permute-start.22 = (f32[128,128]{1,0:T(8,128)S(1)}, f32[128,128]{1,0:T(8,128)S(1)}, u32[]{:S(2)}, u32[]{:S(2)}) collective-permute-start(f32[128,128]{1,0:T(8,128)S(1)} %add_add_fusion.1), channel_id=1, source_target_pairs={{0,192},{4,196},{8,200},{12,204},{16,208},{20,212},{24,216},{28,22... | collective-permute-start | bytes 196616 | tf_op jit(solution)/shard_map/ppermute | solution.py:111
  130.0 5.2 %collective-permute-start.23 = (f32[128,128]{1,0:T(8,128)S(1)}, f32[128,128]{1,0:T(8,128)S(1)}, u32[]{:S(2)}, u32[]{:S(2)}) collective-permute-start(f32[128,128]{1,0:T(8,128)S(1)} %add_add_fusion), channel_id=1, source_target_pairs={{0,1},{1,0},{2,3},{3,2},{4,5},{5,4},{6,7},{7,6},{8,9},{9,8},{10,11... | collective-permute-start | bytes 196616 | tf_op jit(solution)/shard_map/ppermute | solution.py:111
  132.5 5.8 %collective-permute-start.24 = (f32[128,128]{1,0:T(8,128)S(1)}, f32[128,128]{1,0:T(8,128)S(1)}, u32[]{:S(2)}, u32[]{:S(2)}) collective-permute-start(f32[128,128]{1,0:T(8,128)S(1)} %add_add_fusion), channel_id=1, source_target_pairs={{0,2},{1,3},{2,0},{3,1},{4,6},{5,7},{6,4},{7,5},{8,10},{9,11},{10,... | collective-permute-start | bytes 196616 | tf_op jit(solution)/shard_map/ppermute | solution.py:111
  134.2 5.5 %collective-permute-start.25 = (f32[128,128]{1,0:T(8,128)S(1)}, f32[128,128]{1,0:T(8,128)S(1)}, u32[]{:S(2)}, u32[]{:S(2)}) collective-permute-start(f32[128,128]{1,0:T(8,128)S(1)} %add_add_fusion), channel_id=1, source_target_pairs={{0,3},{1,2},{2,1},{3,0},{4,7},{5,6},{6,5},{7,4},{8,11},{9,10},{10,... | collective-permute-start | bytes 196616 | tf_op jit(solution)/shard_map/ppermute | solution.py:111
  (6 other events, 50.2 us)

commit v5 on v4

--- a/solution.py
+++ b/solution.py
@@ -236,10 +236,17 @@
         return lax.dot_general(weights, rows_part, (((0,), (1,)), ((), ())), precision=HIGH)
 
     received = [None] * freq_count
+    back = [(i, (i - 1) % freq_count) for i in range(freq_count)]
     for shift in range(1, freq_count):
         piece = modes_of((group + shift) % freq_count)
         pairs = [(i, (i + shift) % freq_count) for i in range(freq_count)]
-        received[shift] = lax.ppermute(piece, "freq", pairs)
+        if freq_count == 4 and shift == 2:
+            half = piece.shape[1] // 2
+            direct = lax.ppermute(piece[:, :half], "freq", pairs)
+            relayed = lax.ppermute(lax.ppermute(piece[:, half:], "freq", back), "freq", back)
+            received[shift] = jnp.concatenate([direct, relayed], axis=1)
+        else:
+            received[shift] = lax.ppermute(piece, "freq", pairs)
     received[0] = modes_of(group)
     stacked = jnp.concatenate(received, axis=0)
     source = (group - jnp.arange(freq_count)) % freq_count

time: 165 us -> 169 us (1.024)
  waiting for transfers between devices: 48.4 us -> 51.1 us
  starting transfers between devices: 47.6 us -> 50.3 us
  matrix products: 17.8 us -> 15.6 us
    ppermute x0 -> x3, waiting for transfers between devices: none -> 15.9 us  [the longest x1 13.3 us: shards(): lax.ppermute(lax.ppermute(piece[:, half:], 'freq', back), 'freq', back)]
    ppermute x3 -> x2, waiting for transfers between devices: 14 us -> 0.01 us  [shards(): received[shift] = lax.ppermute(piece, 'freq', pairs)]
    ppermute x0 -> x3, starting transfers between devices: none -> 6.07 us  [the longest x1 3.17 us: shards(): lax.ppermute(lax.ppermute(piece[:, half:], 'freq', back), 'freq', back)]
    ppermute x3 -> x2, starting transfers between devices: 6.08 us -> 3.18 us  [shards(): received[shift] = lax.ppermute(piece, 'freq', pairs)]
  transfers between devices with their start and end apart: 26 -> 28, of which waited for: 20 -> 20; matrix products, arithmetic and copies ran while one was open for 6% -> 6% of each run, Pallas kernels for 0% -> 0%
where the time goes in v5:
time: 169 us; the launch traced here: 168 us
  waiting for transfers between devices  51.1 us (30%)
  starting transfers between devices  50.3 us (30%)
  Pallas kernels  40.7 us (24%)
  matrix products  15.6 us (9%)
  local copies, waits for them, and re-layouts  6.71 us (4%)
  other arithmetic  3.21 us (2%)
    ppermute x21, starting transfers between devices, butterfly_sum(): parts.append(lax.ppermute(x, axis, pairs))  35.5 us
    ppermute x21, waiting for transfers between devices, butterfly_sum(): parts.append(lax.ppermute(x, axis, pairs))  34.9 us
    pallas_call x3, Pallas kernels, subspace_batch(): pl.pallas_call(subspace_kernel, out_shape=jax.ShapeDtypeStruct((batch, ra...  26 us
    pallas_call x1, Pallas kernels, apply_mass(): pl.pallas_call(mass_kernel, grid_spec=grid_spec, out_shape=[jax.ShapeDtyp...  14.7 us
    ppermute x1, waiting for transfers between devices, shards(): lax.ppermute(lax.ppermute(piece[:, half:], 'freq', back), 'freq', back)  13.3 us
    dot_general x4, matrix products, modes_of(): lax.dot_general(weights, rows_part, (((0,), (1,)), ((), ())), precision=H...  10.9 us
    ppermute x1, starting transfers between devices, shards(): high = lax.ppermute(snapshots[:width], 'rows', backward)  3.64 us
  transfers between devices with their start and end apart: 28, of which 20 were waited for; matrix products, arithmetic and copies ran while one was open for 6% of the time, Pallas kernels for 0%

profile of v5, /device:TPU:32, one launch (start us, length us, event | category | flops | bytes accessed | tf_op | source)
XLA Modules:
  0.0 167.8 jit_solution(10958873107803693096)
XLA Ops:
  2.8 3.6 %collective-permute-start.1 = (bf16[256,128]{1,0:T(8,128)(2,1)S(1)}, bf16[256,128]{1,0:T(8,128)(2,1)S(1)}, u32[]{:S(2)}, u32[]{:S(2)}) collective-permute-start(bf16[256,128]{1,0:T(8,128)(2,1)S(1)} %get-tuple-element.9), channel_id=1, source_target_pairs={{4,0},{8,4},{12,8},{16,12},{20,16},{24,20},{28,24},{32,28},{36,32}... | collective-permute-start | bytes 196616 | tf_op jit(solution)/shard_map/ppermute | solution.py:224
  9.3 14.7 %shard_map.55 = (f32[16384,128]{1,0:T(8,128)}, f32[128,128]{1,0:T(8,128)}) custom-call(s32[384]{0:T(512)} %reshape.69.index_ref, bf16[256,128]{1,0:T(8,128)(2,1)} %copy-done.1, bf16[16384,128]{1,0:T(8,128)(2,1)} %own_ref.1, bf16[256,128]{1,0:T(8,128)(2,1)} %copy-done.2, bf16[128,3,128,128]{3,2,1,0:T(8,128)(2,1)} %mass_ref.1), custom_call_target="tpu_custom_call" | custom-call | tf_op jit(solution)/shard_map/pallas_call | solution.py:88
  27.2 3.6 %collective-permute-done.3 = f32[128,128]{1,0:T(8,128)S(1)} collective-permute-done((f32[128,128]{1,0:T(8,128)}, f32[128,128]{1,0:T(8,128)S(1)}, u32[]{:S(2)}, u32[]{:S(2)}) %collective-permute-start.3) | collective-permute-done | bytes 65568 | tf_op jit(solution)/shard_map/ppermute | solution.py:111
  31.6 5.8 %collective-permute-start.5 = (f32[128,128]{1,0:T(8,128)S(1)}, f32[128,128]{1,0:T(8,128)S(1)}, u32[]{:S(2)}, u32[]{:S(2)}) collective-permute-start(f32[128,128]{1,0:T(8,128)S(1)} %add_add_fusion.4), channel_id=1, source_target_pairs={{0,16},{4,20},{8,24},{12,28},{16,0},{20,4},{24,8},{28,12},{32,48},... | collective-permute-start | bytes 196616 | tf_op jit(solution)/shard_map/ppermute | solution.py:111
  41.6 5.3 %collective-permute-done.6 = f32[128,128]{1,0:T(8,128)S(1)} collective-permute-done((f32[128,128]{1,0:T(8,128)S(1)}, f32[128,128]{1,0:T(8,128)S(1)}, u32[]{:S(2)}, u32[]{:S(2)}) %collective-permute-start.6) | collective-permute-done | bytes 65568 | tf_op jit(solution)/shard_map/ppermute | solution.py:111
  48.9 2.6 %collective-permute-start.10 = (f32[128,128]{1,0:T(8,128)S(1)}, f32[128,128]{1,0:T(8,128)S(1)}, u32[]{:S(2)}, u32[]{:S(2)}) collective-permute-start(f32[128,128]{1,0:T(8,128)S(1)} %add_add_fusion.3), channel_id=1, source_target_pairs={{0,192},{4,196},{8,200},{12,204},{16,208},{20,212},{24,216},{28,22... | collective-permute-start | bytes 196616 | tf_op jit(solution)/shard_map/ppermute | solution.py:111
  55.9 2.0 %collective-permute-done.9 = f32[128,128]{1,0:T(8,128)S(1)} collective-permute-done((f32[128,128]{1,0:T(8,128)S(1)}, f32[128,128]{1,0:T(8,128)S(1)}, u32[]{:S(2)}, u32[]{:S(2)}) %collective-permute-start.9) | collective-permute-done | bytes 65568 | tf_op jit(solution)/shard_map/ppermute | solution.py:111
  58.6 8.6 %shard_map.56 = f32[1,32,128]{2,1,0:T(8,128)} custom-call(f32[1,128,128]{2,1,0:T(8,128)} %multiply_bitcast_fusion.g_ref, f32[1,32,128]{2,1,0:T(8,128)} %bitcast.47), custom_call_target="tpu_custom_call" | custom-call | tf_op jit(solution)/shard_map/pallas_call | solution.py:163
  67.2 2.8 %fusion.4 = f32[32,4096]{1,0:T(8,128)S(1)} fusion(f32[16384,128]{1,0:T(8,128)} %get-tuple-element.8, s32[]{:T(128)S(6)} %select_n.82, f32[1,32,128]{2,1,0:T(8,128)} %shard_map.56), kind=kOutput, calls=%fused_computation.8 | convolution fusion | flops 100663296 | bytes 2637828 | tf_op jit(solution)/shard_map/dot_general | solution.py:236
  71.5 2.7 %fusion.2 = f32[32,4096]{1,0:T(8,128)S(1)} fusion(f32[16384,128]{1,0:T(8,128)} %get-tuple-element.8, s32[]{:T(128)S(6)} %select_n.84, f32[1,32,128]{2,1,0:T(8,128)S(1)} %copy-done), kind=kOutput, calls=%fused_computation.6 | convolution fusion | flops 100663296 | bytes 2637828 | tf_op jit(solution)/shard_map/dot_general | solution.py:236
  76.3 2.7 %fusion = f32[32,4096]{1,0:T(8,128)S(1)} fusion(f32[16384,128]{1,0:T(8,128)} %get-tuple-element.8, s32[]{:T(128)S(6)} %select_n.86, f32[1,32,128]{2,1,0:T(8,128)S(1)} %copy-done), kind=kOutput, calls=%fused_computation.4 | convolution fusion | flops 100663296 | bytes 2637828 | tf_op jit(solution)/shard_map/dot_general | solution.py:236
  82.5 3.2 %collective-permute-start.14 = (f32[32,2048]{1,0:T(8,128)}, f32[32,2048]{1,0:T(8,128)S(1)}, u32[]{:S(2)}, u32[]{:S(2)}) collective-permute-start(f32[32,2048]{1,0:T(8,128)} %collective-permute-done.13), channel_id=1, source_target_pairs={{0,3},{1,0},{2,1},{3,2},{4,7},{5,4},{6,5},{7,6},{8,11},{9,8},{10,9... | collective-permute-start | bytes 786440 | tf_op jit(solution)/shard_map/ppermute | solution.py:246
  85.8 2.7 %fusion.6 = f32[32,4096]{1,0:T(8,128)S(1)} fusion(f32[16384,128]{1,0:T(8,128)} %get-tuple-element.8, s32[]{:T(128)S(6)} %select_n.80, f32[1,32,128]{2,1,0:T(8,128)S(1)} %copy-done), kind=kOutput, calls=%fused_computation.10 | convolution fusion | flops 100663296 | bytes 2637828 | tf_op jit(solution)/shard_map/dot_general | solution.py:236
  90.2 13.3 %collective-permute-done.14 = f32[32,2048]{1,0:T(8,128)S(1)} collective-permute-done((f32[32,2048]{1,0:T(8,128)}, f32[32,2048]{1,0:T(8,128)S(1)}, u32[]{:S(2)}, u32[]{:S(2)}) %collective-permute-start.14) | collective-permute-done | bytes 262176 | tf_op jit(solution)/shard_map/ppermute | solution.py:246
  108.4 3.2 %collective-permute-done.17 = f32[128,128]{1,0:T(8,128)S(1)} collective-permute-done((f32[128,128]{1,0:T(8,128)S(1)}, f32[128,128]{1,0:T(8,128)S(1)}, u32[]{:S(2)}, u32[]{:S(2)}) %collective-permute-start.17) | collective-permute-done | bytes 65568 | tf_op jit(solution)/shard_map/ppermute | solution.py:111
  113.5 2.7 %collective-permute-start.20 = (f32[128,128]{1,0:T(8,128)S(1)}, f32[128,128]{1,0:T(8,128)S(1)}, u32[]{:S(2)}, u32[]{:S(2)}) collective-permute-start(f32[128,128]{1,0:T(8,128)S(1)} %add_add_fusion.2), channel_id=1, source_target_pairs={{0,32},{4,36},{8,40},{12,44},{16,48},{20,52},{24,56},{28,60},{32,0... | collective-permute-start | bytes 196616 | tf_op jit(solution)/shard_map/ppermute | solution.py:111
  116.2 2.2 %collective-permute-start.21 = (f32[128,128]{1,0:T(8,128)S(1)}, f32[128,128]{1,0:T(8,128)S(1)}, u32[]{:S(2)}, u32[]{:S(2)}) collective-permute-start(f32[128,128]{1,0:T(8,128)S(1)} %add_add_fusion.2), channel_id=1, source_target_pairs={{0,48},{4,52},{8,56},{12,60},{16,32},{20,36},{24,40},{28,44},{32,1... | collective-permute-start | bytes 196616 | tf_op jit(solution)/shard_map/ppermute | solution.py:111
  118.5 5.4 %collective-permute-done.20 = f32[128,128]{1,0:T(8,128)S(1)} collective-permute-done((f32[128,128]{1,0:T(8,128)S(1)}, f32[128,128]{1,0:T(8,128)S(1)}, u32[]{:S(2)}, u32[]{:S(2)}) %collective-permute-start.20) | collective-permute-done | bytes 65568 | tf_op jit(solution)/shard_map/ppermute | solution.py:111
  130.3 2.4 %collective-permute-done.23 = f32[128,128]{1,0:T(8,128)S(1)} collective-permute-done((f32[128,128]{1,0:T(8,128)S(1)}, f32[128,128]{1,0:T(8,128)S(1)}, u32[]{:S(2)}, u32[]{:S(2)}) %collective-permute-start.23) | collective-permute-done | bytes 65568 | tf_op jit(solution)/shard_map/ppermute | solution.py:111
  135.5 2.9 %collective-permute-start.26 = (f32[128,128]{1,0:T(8,128)S(1)}, f32[128,128]{1,0:T(8,128)S(1)}, u32[]{:S(2)}, u32[]{:S(2)}) collective-permute-start(f32[128,128]{1,0:T(8,128)S(1)} %add_add_fusion), channel_id=1, source_target_pairs={{0,2},{1,3},{2,0},{3,1},{4,6},{5,7},{6,4},{7,5},{8,10},{9,11},{10,... | collective-permute-start | bytes 196616 | tf_op jit(solution)/shard_map/ppermute | solution.py:111
  138.8 2.7 %collective-permute-done.26 = f32[128,128]{1,0:T(8,128)S(1)} collective-permute-done((f32[128,128]{1,0:T(8,128)S(1)}, f32[128,128]{1,0:T(8,128)S(1)}, u32[]{:S(2)}, u32[]{:S(2)}) %collective-permute-start.26) | collective-permute-done | bytes 65568 | tf_op jit(solution)/shard_map/ppermute | solution.py:111
  141.5 2.4 %collective-permute-done.27 = f32[128,128]{1,0:T(8,128)S(1)} collective-permute-done((f32[128,128]{1,0:T(8,128)S(1)}, f32[128,128]{1,0:T(8,128)S(1)}, u32[]{:S(2)}, u32[]{:S(2)}) %collective-permute-start.27) | collective-permute-done | bytes 65568 | tf_op jit(solution)/shard_map/ppermute | solution.py:111
  145.3 9.0 %shard_map.57 = f32[2,32,64]{2,1,0:T(8,128)} custom-call(f32[2,64,64]{2,1,0:T(8,128)} %pad_maximum_fusion.3.g_ref, f32[2,32,64]{2,1,0:T(8,128)} %broadcast_in_dim.62.v_ref), custom_call_target="tpu_custom_call" | custom-call | tf_op jit(solution)/shard_map/pallas_call | solution.py:163
  156.3 8.4 %shard_map.58 = f32[1,32,64]{2,1,0:T(8,128)} custom-call(f32[1,64,64]{2,1,0:T(8,128)} %convolution_bitcast_fusion.g_ref, f32[1,32,64]{2,1,0:T(8,128)} %bitcast.45), custom_call_target="tpu_custom_call" | custom-call | tf_op jit(solution)/shard_map/pallas_call | solution.py:163
  (86 shorter events, 52.6 us)
Async XLA Ops:
  0.9 7.2 %collective-permute-start = (bf16[256,128]{1,0:T(8,128)(2,1)S(1)}, bf16[256,128]{1,0:T(8,128)(2,1)S(1)}, u32[]{:S(2)}, u32[]{:S(2)}) collective-permute-start(bf16[256,128]{1,0:T(8,128)(2,1)S(1)} %get-tuple-element.10), channel_id=1, source_target_pairs={{0,4},{4,8},{8,12},{12,16},{16,20},{20,24},{24,28},{28,32},{32,36}... | collective-permute-start | bytes 196616 | tf_op jit(solution)/shard_map/ppermute | solution.py:223
  2.8 5.5 %collective-permute-start.1 = (bf16[256,128]{1,0:T(8,128)(2,1)S(1)}, bf16[256,128]{1,0:T(8,128)(2,1)S(1)}, u32[]{:S(2)}, u32[]{:S(2)}) collective-permute-start(bf16[256,128]{1,0:T(8,128)(2,1)S(1)} %get-tuple-element.9), channel_id=1, source_target_pairs={{4,0},{8,4},{12,8},{16,12},{20,16},{24,20},{28,24},{32,28},{36,32}... | collective-permute-start | bytes 196616 | tf_op jit(solution)/shard_map/ppermute | solution.py:224
  25.7 5.0 %collective-permute-start.3 = (f32[128,128]{1,0:T(8,128)}, f32[128,128]{1,0:T(8,128)S(1)}, u32[]{:S(2)}, u32[]{:S(2)}) collective-permute-start(f32[128,128]{1,0:T(8,128)} %get-tuple-element.7), channel_id=1, source_target_pairs={{0,8},{4,12},{8,0},{12,4},{16,24},{20,28},{24,16},{28,20},{32,40},... | collective-permute-start | bytes 196616 | tf_op jit(solution)/shard_map/ppermute | solution.py:111
  25.9 4.9 %collective-permute-start.4 = (f32[128,128]{1,0:T(8,128)}, f32[128,128]{1,0:T(8,128)S(1)}, u32[]{:S(2)}, u32[]{:S(2)}) collective-permute-start(f32[128,128]{1,0:T(8,128)} %get-tuple-element.7), channel_id=1, source_target_pairs={{0,12},{4,8},{8,4},{12,0},{16,28},{20,24},{24,20},{28,16},{32,44},... | collective-permute-start | bytes 196616 | tf_op jit(solution)/shard_map/ppermute | solution.py:111
  31.6 10.0 %collective-permute-start.5 = (f32[128,128]{1,0:T(8,128)S(1)}, f32[128,128]{1,0:T(8,128)S(1)}, u32[]{:S(2)}, u32[]{:S(2)}) collective-permute-start(f32[128,128]{1,0:T(8,128)S(1)} %add_add_fusion.4), channel_id=1, source_target_pairs={{0,16},{4,20},{8,24},{12,28},{16,0},{20,4},{24,8},{28,12},{32,48},... | collective-permute-start | bytes 196616 | tf_op jit(solution)/shard_map/ppermute | solution.py:111
  37.4 9.5 %collective-permute-start.6 = (f32[128,128]{1,0:T(8,128)S(1)}, f32[128,128]{1,0:T(8,128)S(1)}, u32[]{:S(2)}, u32[]{:S(2)}) collective-permute-start(f32[128,128]{1,0:T(8,128)S(1)} %add_add_fusion.4), channel_id=1, source_target_pairs={{0,32},{4,36},{8,40},{12,44},{16,48},{20,52},{24,56},{28,60},{32,0... | collective-permute-start | bytes 196616 | tf_op jit(solution)/shard_map/ppermute | solution.py:111
  39.4 9.5 %collective-permute-start.7 = (f32[128,128]{1,0:T(8,128)S(1)}, f32[128,128]{1,0:T(8,128)S(1)}, u32[]{:S(2)}, u32[]{:S(2)}) collective-permute-start(f32[128,128]{1,0:T(8,128)S(1)} %add_add_fusion.4), channel_id=1, source_target_pairs={{0,48},{4,52},{8,56},{12,60},{16,32},{20,36},{24,40},{28,44},{32,1... | collective-permute-start | bytes 196616 | tf_op jit(solution)/shard_map/ppermute | solution.py:111
  48.9 5.6 %collective-permute-start.10 = (f32[128,128]{1,0:T(8,128)S(1)}, f32[128,128]{1,0:T(8,128)S(1)}, u32[]{:S(2)}, u32[]{:S(2)}) collective-permute-start(f32[128,128]{1,0:T(8,128)S(1)} %add_add_fusion.3), channel_id=1, source_target_pairs={{0,192},{4,196},{8,200},{12,204},{16,208},{20,212},{24,216},{28,22... | collective-permute-start | bytes 196616 | tf_op jit(solution)/shard_map/ppermute | solution.py:111
  52.2 5.8 %collective-permute-start.9 = (f32[128,128]{1,0:T(8,128)S(1)}, f32[128,128]{1,0:T(8,128)S(1)}, u32[]{:S(2)}, u32[]{:S(2)}) collective-permute-start(f32[128,128]{1,0:T(8,128)S(1)} %add_add_fusion.3), channel_id=1, source_target_pairs={{0,128},{4,132},{8,136},{12,140},{16,144},{20,148},{24,152},{28,15... | collective-permute-start | bytes 196616 | tf_op jit(solution)/shard_map/ppermute | solution.py:111
  69.9 20.3 %collective-permute-start.11 = (f32[32,4096]{1,0:T(8,128)S(1)}, f32[32,4096]{1,0:T(8,128)S(1)}, u32[]{:S(2)}, u32[]{:S(2)}) collective-permute-start(f32[32,4096]{1,0:T(8,128)S(1)} %fusion.4), channel_id=1, source_target_pairs={{0,1},{1,2},{2,3},{3,0},{4,5},{5,6},{6,7},{7,4},{8,9},{9,10},{10,1... | collective-permute-start | bytes 1572872 | tf_op jit(solution)/shard_map/ppermute | solution.py:249
  74.3 8.2 %collective-permute-start.13 = (f32[32,2048]{1,0:T(8,128)S(1)}, f32[32,2048]{1,0:T(8,128)}, u32[]{:S(2)}, u32[]{:S(2)}) collective-permute-start(f32[32,2048]{1,0:T(8,128)S(1)} %get-tuple-element.12), channel_id=1, source_target_pairs={{0,3},{1,0},{2,1},{3,2},{4,7},{5,4},{6,5},{7,6},{8,11},{9,8},{10,9... | collective-permute-start | bytes 786440 | tf_op jit(solution)/shard_map/ppermute | solution.py:246
  79.0 24.5 %collective-permute-start.15 = (f32[32,4096]{1,0:T(8,128)S(1)}, f32[32,4096]{1,0:T(8,128)S(1)}, u32[]{:S(2)}, u32[]{:S(2)}) collective-permute-start(f32[32,4096]{1,0:T(8,128)S(1)} %fusion), channel_id=1, source_target_pairs={{0,3},{1,0},{2,1},{3,2},{4,7},{5,4},{6,5},{7,6},{8,11},{9,8},{10,9... | collective-permute-start | bytes 1572872 | tf_op jit(solution)/shard_map/ppermute | solution.py:249
  80.7 9.5 %collective-permute-start.12 = (f32[32,2048]{1,0:T(8,128)S(1)}, f32[32,2048]{1,0:T(8,128)S(1)}, u32[]{:S(2)}, u32[]{:S(2)}) collective-permute-start(f32[32,2048]{1,0:T(8,128)S(1)} %get-tuple-element.11), channel_id=1, source_target_pairs={{0,2},{1,3},{2,0},{3,1},{4,6},{5,7},{6,4},{7,5},{8,10},{9,11},{10,... | collective-permute-start | bytes 786440 | tf_op jit(solution)/shard_map/ppermute | solution.py:245
  82.5 21.1 %collective-permute-start.14 = (f32[32,2048]{1,0:T(8,128)}, f32[32,2048]{1,0:T(8,128)S(1)}, u32[]{:S(2)}, u32[]{:S(2)}) collective-permute-start(f32[32,2048]{1,0:T(8,128)} %collective-permute-done.13), channel_id=1, source_target_pairs={{0,3},{1,0},{2,1},{3,2},{4,7},{5,4},{6,5},{7,6},{8,11},{9,8},{10,9... | collective-permute-start | bytes 786440 | tf_op jit(solution)/shard_map/ppermute | solution.py:246
  106.6 5.1 %collective-permute-start.17 = (f32[128,128]{1,0:T(8,128)S(1)}, f32[128,128]{1,0:T(8,128)S(1)}, u32[]{:S(2)}, u32[]{:S(2)}) collective-permute-start(f32[128,128]{1,0:T(8,128)S(1)} %broadcast_select_fusion.1), channel_id=1, source_target_pairs={{0,8},{4,12},{8,0},{12,4},{16,24},{20,28},{24,16},{28,20},{32,40},... | collective-permute-start | bytes 196616 | tf_op jit(solution)/shard_map/ppermute | solution.py:111
  106.7 5.2 %collective-permute-start.18 = (f32[128,128]{1,0:T(8,128)S(1)}, f32[128,128]{1,0:T(8,128)S(1)}, u32[]{:S(2)}, u32[]{:S(2)}) collective-permute-start(f32[128,128]{1,0:T(8,128)S(1)} %broadcast_select_fusion.1), channel_id=1, source_target_pairs={{0,12},{4,8},{8,4},{12,0},{16,28},{20,24},{24,20},{28,16},{32,44},... | collective-permute-start | bytes 196616 | tf_op jit(solution)/shard_map/ppermute | solution.py:111
  111.9 6.6 %collective-permute-start.19 = (f32[128,128]{1,0:T(8,128)S(1)}, f32[128,128]{1,0:T(8,128)S(1)}, u32[]{:S(2)}, u32[]{:S(2)}) collective-permute-start(f32[128,128]{1,0:T(8,128)S(1)} %add_add_fusion.2), channel_id=1, source_target_pairs={{0,16},{4,20},{8,24},{12,28},{16,0},{20,4},{24,8},{28,12},{32,48},... | collective-permute-start | bytes 196616 | tf_op jit(solution)/shard_map/ppermute | solution.py:111
  113.5 10.4 %collective-permute-start.20 = (f32[128,128]{1,0:T(8,128)S(1)}, f32[128,128]{1,0:T(8,128)S(1)}, u32[]{:S(2)}, u32[]{:S(2)}) collective-permute-start(f32[128,128]{1,0:T(8,128)S(1)} %add_add_fusion.2), channel_id=1, source_target_pairs={{0,32},{4,36},{8,40},{12,44},{16,48},{20,52},{24,56},{28,60},{32,0... | collective-permute-start | bytes 196616 | tf_op jit(solution)/shard_map/ppermute | solution.py:111
  116.2 9.2 %collective-permute-start.21 = (f32[128,128]{1,0:T(8,128)S(1)}, f32[128,128]{1,0:T(8,128)S(1)}, u32[]{:S(2)}, u32[]{:S(2)}) collective-permute-start(f32[128,128]{1,0:T(8,128)S(1)} %add_add_fusion.2), channel_id=1, source_target_pairs={{0,48},{4,52},{8,56},{12,60},{16,32},{20,36},{24,40},{28,44},{32,1... | collective-permute-start | bytes 196616 | tf_op jit(solution)/shard_map/ppermute | solution.py:111
  125.4 4.9 %collective-permute-start.22 = (f32[128,128]{1,0:T(8,128)S(1)}, f32[128,128]{1,0:T(8,128)S(1)}, u32[]{:S(2)}, u32[]{:S(2)}) collective-permute-start(f32[128,128]{1,0:T(8,128)S(1)} %add_add_fusion.1), channel_id=1, source_target_pairs={{0,64},{4,68},{8,72},{12,76},{16,80},{20,84},{24,88},{28,92},{32,9... | collective-permute-start | bytes 196616 | tf_op jit(solution)/shard_map/ppermute | solution.py:111
  126.8 5.9 %collective-permute-start.23 = (f32[128,128]{1,0:T(8,128)S(1)}, f32[128,128]{1,0:T(8,128)S(1)}, u32[]{:S(2)}, u32[]{:S(2)}) collective-permute-start(f32[128,128]{1,0:T(8,128)S(1)} %add_add_fusion.1), channel_id=1, source_target_pairs={{0,128},{4,132},{8,136},{12,140},{16,144},{20,148},{24,152},{28,15... | collective-permute-start | bytes 196616 | tf_op jit(solution)/shard_map/ppermute | solution.py:111
  128.5 5.5 %collective-permute-start.24 = (f32[128,128]{1,0:T(8,128)S(1)}, f32[128,128]{1,0:T(8,128)S(1)}, u32[]{:S(2)}, u32[]{:S(2)}) collective-permute-start(f32[128,128]{1,0:T(8,128)S(1)} %add_add_fusion.1), channel_id=1, source_target_pairs={{0,192},{4,196},{8,200},{12,204},{16,208},{20,212},{24,216},{28,22... | collective-permute-start | bytes 196616 | tf_op jit(solution)/shard_map/ppermute | solution.py:111
  135.5 6.0 %collective-permute-start.26 = (f32[128,128]{1,0:T(8,128)S(1)}, f32[128,128]{1,0:T(8,128)S(1)}, u32[]{:S(2)}, u32[]{:S(2)}) collective-permute-start(f32[128,128]{1,0:T(8,128)S(1)} %add_add_fusion), channel_id=1, source_target_pairs={{0,2},{1,3},{2,0},{3,1},{4,6},{5,7},{6,4},{7,5},{8,10},{9,11},{10,... | collective-permute-start | bytes 196616 | tf_op jit(solution)/shard_map/ppermute | solution.py:111
  138.4 5.5 %collective-permute-start.27 = (f32[128,128]{1,0:T(8,128)S(1)}, f32[128,128]{1,0:T(8,128)S(1)}, u32[]{:S(2)}, u32[]{:S(2)}) collective-permute-start(f32[128,128]{1,0:T(8,128)S(1)} %add_add_fusion), channel_id=1, source_target_pairs={{0,3},{1,2},{2,1},{3,0},{4,7},{5,6},{6,5},{7,4},{8,11},{9,10},{10,... | collective-permute-start | bytes 196616 | tf_op jit(solution)/shard_map/ppermute | solution.py:111
  (8 other events, 59.7 us)

commit v6 on v4

--- a/solution.py
+++ b/solution.py
@@ -43,7 +43,7 @@
 
     for row in range(rows_here):
         block = step * rows_here + row
-        total = jnp.zeros((size, out_ref.shape[1]), jnp.float32)
+        tiles = []
         for k in range(kb):
             tile_id = index_ref[block * kb + k]
             own_at = jnp.clip(tile_id - halo, 0, own_tiles - 1)
@@ -55,8 +55,12 @@
             tile = jnp.where(
                 tile_id < halo, low_tile, jnp.where(tile_id >= halo + own_tiles, high_tile, own_tile)
             )
-            total = total + jnp.dot(mass_ref[row, k], tile, preferred_element_type=jnp.float32)
-        out_ref[row * size : (row + 1) * size, :] = total
+            tiles.append(tile)
+        joined_mass = jnp.concatenate([mass_ref[row, k] for k in range(kb)], axis=1)
+        joined_tiles = jnp.concatenate(tiles, axis=0)
+        out_ref[row * size : (row + 1) * size, :] = jnp.dot(
+            joined_mass, joined_tiles, preferred_element_type=jnp.float32
+        )
 
     chunk = out_ref[...]
     high_part = chunk.astype(jnp.bfloat16)

time: 165 us -> 166 us (level)
  no operation moved by 1% of the time
where the time goes in v6:
time: 166 us; the launch traced here: 165 us
  waiting for transfers between devices  48.4 us (29%)
  starting transfers between devices  47.5 us (29%)
  Pallas kernels  41.2 us (25%)
  matrix products  17.8 us (11%)
  local copies, waits for them, and re-layouts  6.66 us (4%)
  other arithmetic  3.21 us (2%)
    ppermute x21, starting transfers between devices, butterfly_sum(): parts.append(lax.ppermute(x, axis, pairs))  35.9 us
    ppermute x21, waiting for transfers between devices, butterfly_sum(): parts.append(lax.ppermute(x, axis, pairs))  34.2 us
    pallas_call x3, Pallas kernels, subspace_batch(): pl.pallas_call(subspace_kernel, out_shape=jax.ShapeDtypeStruct((batch, ra...  26 us
    pallas_call x1, Pallas kernels, apply_mass(): pl.pallas_call(mass_kernel, grid_spec=grid_spec, out_shape=[jax.ShapeDtyp...  15.2 us
    ppermute x3, waiting for transfers between devices, shards(): received[shift] = lax.ppermute(piece, 'freq', pairs)  14 us
    dot_general x4, matrix products, modes_of(): lax.dot_general(weights, rows_part, (((0,), (1,)), ((), ())), precision=H...  10.9 us
    ppermute x3, starting transfers between devices, shards(): received[shift] = lax.ppermute(piece, 'freq', pairs)  6.06 us
    ppermute x1, starting transfers between devices, shards(): high = lax.ppermute(snapshots[:width], 'rows', backward)  3.64 us
  transfers between devices with their start and end apart: 26, of which 20 were waited for; matrix products, arithmetic and copies ran while one was open for 6% of the time, Pallas kernels for 0%

profile of v6, /device:TPU:32, one launch (start us, length us, event | category | flops | bytes accessed | tf_op | source)
XLA Modules:
  0.0 165.1 jit_solution(9468642787281533664)
XLA Ops:
  2.8 3.6 %collective-permute-start.1 = (bf16[256,128]{1,0:T(8,128)(2,1)S(1)}, bf16[256,128]{1,0:T(8,128)(2,1)S(1)}, u32[]{:S(2)}, u32[]{:S(2)}) collective-permute-start(bf16[256,128]{1,0:T(8,128)(2,1)S(1)} %get-tuple-element.9), channel_id=1, source_target_pairs={{4,0},{8,4},{12,8},{16,12},{20,16},{24,20},{28,24},{32,28},{36,32}... | collective-permute-start | bytes 196616 | tf_op jit(solution)/shard_map/ppermute | solution.py:228
  9.3 15.2 %shard_map.55 = (f32[16384,128]{1,0:T(8,128)}, f32[128,128]{1,0:T(8,128)}) custom-call(s32[384]{0:T(512)} %reshape.69.index_ref, bf16[256,128]{1,0:T(8,128)(2,1)} %copy-done.1, bf16[16384,128]{1,0:T(8,128)(2,1)} %own_ref.1, bf16[256,128]{1,0:T(8,128)(2,1)} %copy-done.2, bf16[128,3,128,128]{3,2,1,0:T(8,128)(2,1)} %mass_ref.1), custom_call_target="tpu_custom_call" | custom-call | tf_op jit(solution)/shard_map/pallas_call | solution.py:92
  27.7 3.6 %collective-permute-done.3 = f32[128,128]{1,0:T(8,128)S(1)} collective-permute-done((f32[128,128]{1,0:T(8,128)}, f32[128,128]{1,0:T(8,128)S(1)}, u32[]{:S(2)}, u32[]{:S(2)}) %collective-permute-start.3) | collective-permute-done | bytes 65568 | tf_op jit(solution)/shard_map/ppermute | solution.py:115
  32.1 5.8 %collective-permute-start.5 = (f32[128,128]{1,0:T(8,128)S(1)}, f32[128,128]{1,0:T(8,128)S(1)}, u32[]{:S(2)}, u32[]{:S(2)}) collective-permute-start(f32[128,128]{1,0:T(8,128)S(1)} %add_add_fusion.4), channel_id=1, source_target_pairs={{0,16},{4,20},{8,24},{12,28},{16,0},{20,4},{24,8},{28,12},{32,48},... | collective-permute-start | bytes 196616 | tf_op jit(solution)/shard_map/ppermute | solution.py:115
  42.1 5.3 %collective-permute-done.6 = f32[128,128]{1,0:T(8,128)S(1)} collective-permute-done((f32[128,128]{1,0:T(8,128)S(1)}, f32[128,128]{1,0:T(8,128)S(1)}, u32[]{:S(2)}, u32[]{:S(2)}) %collective-permute-start.6) | collective-permute-done | bytes 65568 | tf_op jit(solution)/shard_map/ppermute | solution.py:115
  49.4 2.6 %collective-permute-start.10 = (f32[128,128]{1,0:T(8,128)S(1)}, f32[128,128]{1,0:T(8,128)S(1)}, u32[]{:S(2)}, u32[]{:S(2)}) collective-permute-start(f32[128,128]{1,0:T(8,128)S(1)} %add_add_fusion.3), channel_id=1, source_target_pairs={{0,192},{4,196},{8,200},{12,204},{16,208},{20,212},{24,216},{28,22... | collective-permute-start | bytes 196616 | tf_op jit(solution)/shard_map/ppermute | solution.py:115
  59.1 8.6 %shard_map.56 = f32[1,32,128]{2,1,0:T(8,128)} custom-call(f32[1,128,128]{2,1,0:T(8,128)} %multiply_bitcast_fusion.g_ref, f32[1,32,128]{2,1,0:T(8,128)} %bitcast.47), custom_call_target="tpu_custom_call" | custom-call | tf_op jit(solution)/shard_map/pallas_call | solution.py:167
  67.7 2.7 %fusion.4 = f32[32,4096]{1,0:T(8,128)S(1)} fusion(f32[16384,128]{1,0:T(8,128)} %get-tuple-element.8, s32[]{:T(128)S(6)} %select_n.82, f32[1,32,128]{2,1,0:T(8,128)} %shard_map.56), kind=kOutput, calls=%fused_computation.8 | convolution fusion | flops 100663296 | bytes 2637828 | tf_op jit(solution)/shard_map/dot_general | solution.py:240
  72.0 2.7 %fusion.2 = f32[32,4096]{1,0:T(8,128)S(1)} fusion(f32[16384,128]{1,0:T(8,128)} %get-tuple-element.8, s32[]{:T(128)S(6)} %select_n.84, f32[1,32,128]{2,1,0:T(8,128)S(1)} %copy-done), kind=kOutput, calls=%fused_computation.6 | convolution fusion | flops 100663296 | bytes 2637828 | tf_op jit(solution)/shard_map/dot_general | solution.py:240
  74.8 2.8 %collective-permute-start.12 = (f32[32,4096]{1,0:T(8,128)S(1)}, f32[32,4096]{1,0:T(8,128)S(1)}, u32[]{:S(2)}, u32[]{:S(2)}) collective-permute-start(f32[32,4096]{1,0:T(8,128)S(1)} %fusion.2), channel_id=1, source_target_pairs={{0,2},{1,3},{2,0},{3,1},{4,6},{5,7},{6,4},{7,5},{8,10},{9,11},{10,... | collective-permute-start | bytes 1572872 | tf_op jit(solution)/shard_map/ppermute | solution.py:246
  77.6 2.7 %fusion = f32[32,4096]{1,0:T(8,128)S(1)} fusion(f32[16384,128]{1,0:T(8,128)} %get-tuple-element.8, s32[]{:T(128)S(6)} %select_n.86, f32[1,32,128]{2,1,0:T(8,128)S(1)} %copy-done), kind=kOutput, calls=%fused_computation.4 | convolution fusion | flops 100663296 | bytes 2637828 | tf_op jit(solution)/shard_map/dot_general | solution.py:240
  82.2 2.7 %fusion.6 = f32[32,4096]{1,0:T(8,128)S(1)} fusion(f32[16384,128]{1,0:T(8,128)} %get-tuple-element.8, s32[]{:T(128)S(6)} %select_n.80, f32[1,32,128]{2,1,0:T(8,128)S(1)} %copy-done), kind=kOutput, calls=%fused_computation.10 | convolution fusion | flops 100663296 | bytes 2637828 | tf_op jit(solution)/shard_map/dot_general | solution.py:240
  85.6 10.8 %collective-permute-done.12 = f32[32,4096]{1,0:T(8,128)S(1)} collective-permute-done((f32[32,4096]{1,0:T(8,128)S(1)}, f32[32,4096]{1,0:T(8,128)S(1)}, u32[]{:S(2)}, u32[]{:S(2)}) %collective-permute-start.12) | collective-permute-done | bytes 524320 | tf_op jit(solution)/shard_map/ppermute | solution.py:246
  96.3 2.6 %collective-permute-done.13 = f32[32,4096]{1,0:T(8,128)} collective-permute-done((f32[32,4096]{1,0:T(8,128)S(1)}, f32[32,4096]{1,0:T(8,128)}, u32[]{:S(2)}, u32[]{:S(2)}) %collective-permute-start.13) | collective-permute-done | bytes 524320 | tf_op jit(solution)/shard_map/ppermute | solution.py:246
  98.9 2.3 %fusion.9 = f32[128,128]{1,0:T(8,128)S(1)} fusion(f32[32,4096]{1,0:T(8,128)} %collective-permute-done.13, f32[32,4096]{1,0:T(8,128)S(1)} %collective-permute-done.12, f32[32,4096]{1,0:T(8,128)S(1)} %collective-permute-done.11, f32[32,4096]{1,0:T(8,128)S(1)} %fusion.6), kind=kOutput, calls=%fused_computation.13 | convolution fusion | flops 404226048 | bytes 2162688 | tf_op jit(solution)/shard_map/dot_general | solution.py:250
  105.0 3.2 %collective-permute-done.15 = f32[128,128]{1,0:T(8,128)S(1)} collective-permute-done((f32[128,128]{1,0:T(8,128)S(1)}, f32[128,128]{1,0:T(8,128)S(1)}, u32[]{:S(2)}, u32[]{:S(2)}) %collective-permute-start.15) | collective-permute-done | bytes 65568 | tf_op jit(solution)/shard_map/ppermute | solution.py:115
  110.1 2.7 %collective-permute-start.18 = (f32[128,128]{1,0:T(8,128)S(1)}, f32[128,128]{1,0:T(8,128)S(1)}, u32[]{:S(2)}, u32[]{:S(2)}) collective-permute-start(f32[128,128]{1,0:T(8,128)S(1)} %add_add_fusion.2), channel_id=1, source_target_pairs={{0,32},{4,36},{8,40},{12,44},{16,48},{20,52},{24,56},{28,60},{32,0... | collective-permute-start | bytes 196616 | tf_op jit(solution)/shard_map/ppermute | solution.py:115
  112.8 2.3 %collective-permute-start.19 = (f32[128,128]{1,0:T(8,128)S(1)}, f32[128,128]{1,0:T(8,128)S(1)}, u32[]{:S(2)}, u32[]{:S(2)}) collective-permute-start(f32[128,128]{1,0:T(8,128)S(1)} %add_add_fusion.2), channel_id=1, source_target_pairs={{0,48},{4,52},{8,56},{12,60},{16,32},{20,36},{24,40},{28,44},{32,1... | collective-permute-start | bytes 196616 | tf_op jit(solution)/shard_map/ppermute | solution.py:115
  115.1 5.4 %collective-permute-done.18 = f32[128,128]{1,0:T(8,128)S(1)} collective-permute-done((f32[128,128]{1,0:T(8,128)S(1)}, f32[128,128]{1,0:T(8,128)S(1)}, u32[]{:S(2)}, u32[]{:S(2)}) %collective-permute-start.18) | collective-permute-done | bytes 65568 | tf_op jit(solution)/shard_map/ppermute | solution.py:115
  130.5 2.5 %collective-permute-start.23 = (f32[128,128]{1,0:T(8,128)S(1)}, f32[128,128]{1,0:T(8,128)S(1)}, u32[]{:S(2)}, u32[]{:S(2)}) collective-permute-start(f32[128,128]{1,0:T(8,128)S(1)} %add_add_fusion), channel_id=1, source_target_pairs={{0,1},{1,0},{2,3},{3,2},{4,5},{5,4},{6,7},{7,6},{8,9},{9,8},{10,11... | collective-permute-start | bytes 196616 | tf_op jit(solution)/shard_map/ppermute | solution.py:115
  135.8 3.0 %collective-permute-done.24 = f32[128,128]{1,0:T(8,128)S(1)} collective-permute-done((f32[128,128]{1,0:T(8,128)S(1)}, f32[128,128]{1,0:T(8,128)S(1)}, u32[]{:S(2)}, u32[]{:S(2)}) %collective-permute-start.24) | collective-permute-done | bytes 65568 | tf_op jit(solution)/shard_map/ppermute | solution.py:115
  141.5 9.0 %shard_map.57 = f32[2,32,64]{2,1,0:T(8,128)} custom-call(f32[2,64,64]{2,1,0:T(8,128)} %pad_maximum_fusion.3.g_ref, f32[2,32,64]{2,1,0:T(8,128)} %broadcast_in_dim.62.v_ref), custom_call_target="tpu_custom_call" | custom-call | tf_op jit(solution)/shard_map/pallas_call | solution.py:167
  152.5 8.4 %shard_map.58 = f32[1,32,64]{2,1,0:T(8,128)} custom-call(f32[1,64,64]{2,1,0:T(8,128)} %convolution_bitcast_fusion.g_ref, f32[1,32,64]{2,1,0:T(8,128)} %bitcast.45), custom_call_target="tpu_custom_call" | custom-call | tf_op jit(solution)/shard_map/pallas_call | solution.py:167
  162.5 2.6 %fusion.8 = f32[32,4096]{1,0:T(8,128)} fusion(f32[128,32]{1,0:T(8,128)S(1)} %bitcast_select_fusion, f32[32,4096]{1,0:T(8,128)} %collective-permute-done.13, f32[32,4096]{1,0:T(8,128)S(1)} %collective-permute-done.12, f32[32,4096]{1,0:T(8,128)S(1)} %collective-permute-done.11, f32[32,4096]{1,0:T(8,128)S(1)} %fusion.6), kind=kOutput, calls=%fused_computation.12 | convolution fusion | flops 102236160 | bytes 2637824 | tf_op jit(solution)/shard_map/dot_general | solution.py:258
  (81 shorter events, 51.8 us)
Async XLA Ops:
  0.9 7.2 %collective-permute-start = (bf16[256,128]{1,0:T(8,128)(2,1)S(1)}, bf16[256,128]{1,0:T(8,128)(2,1)S(1)}, u32[]{:S(2)}, u32[]{:S(2)}) collective-permute-start(bf16[256,128]{1,0:T(8,128)(2,1)S(1)} %get-tuple-element.10), channel_id=1, source_target_pairs={{0,4},{4,8},{8,12},{12,16},{16,20},{20,24},{24,28},{28,32},{32,36}... | collective-permute-start | bytes 196616 | tf_op jit(solution)/shard_map/ppermute | solution.py:227
  2.8 5.5 %collective-permute-start.1 = (bf16[256,128]{1,0:T(8,128)(2,1)S(1)}, bf16[256,128]{1,0:T(8,128)(2,1)S(1)}, u32[]{:S(2)}, u32[]{:S(2)}) collective-permute-start(bf16[256,128]{1,0:T(8,128)(2,1)S(1)} %get-tuple-element.9), channel_id=1, source_target_pairs={{4,0},{8,4},{12,8},{16,12},{20,16},{24,20},{28,24},{32,28},{36,32}... | collective-permute-start | bytes 196616 | tf_op jit(solution)/shard_map/ppermute | solution.py:228
  26.3 5.0 %collective-permute-start.3 = (f32[128,128]{1,0:T(8,128)}, f32[128,128]{1,0:T(8,128)S(1)}, u32[]{:S(2)}, u32[]{:S(2)}) collective-permute-start(f32[128,128]{1,0:T(8,128)} %get-tuple-element.7), channel_id=1, source_target_pairs={{0,8},{4,12},{8,0},{12,4},{16,24},{20,28},{24,16},{28,20},{32,40},... | collective-permute-start | bytes 196616 | tf_op jit(solution)/shard_map/ppermute | solution.py:115
  26.4 4.9 %collective-permute-start.4 = (f32[128,128]{1,0:T(8,128)}, f32[128,128]{1,0:T(8,128)S(1)}, u32[]{:S(2)}, u32[]{:S(2)}) collective-permute-start(f32[128,128]{1,0:T(8,128)} %get-tuple-element.7), channel_id=1, source_target_pairs={{0,12},{4,8},{8,4},{12,0},{16,28},{20,24},{24,20},{28,16},{32,44},... | collective-permute-start | bytes 196616 | tf_op jit(solution)/shard_map/ppermute | solution.py:115
  32.1 10.0 %collective-permute-start.5 = (f32[128,128]{1,0:T(8,128)S(1)}, f32[128,128]{1,0:T(8,128)S(1)}, u32[]{:S(2)}, u32[]{:S(2)}) collective-permute-start(f32[128,128]{1,0:T(8,128)S(1)} %add_add_fusion.4), channel_id=1, source_target_pairs={{0,16},{4,20},{8,24},{12,28},{16,0},{20,4},{24,8},{28,12},{32,48},... | collective-permute-start | bytes 196616 | tf_op jit(solution)/shard_map/ppermute | solution.py:115
  37.9 9.5 %collective-permute-start.6 = (f32[128,128]{1,0:T(8,128)S(1)}, f32[128,128]{1,0:T(8,128)S(1)}, u32[]{:S(2)}, u32[]{:S(2)}) collective-permute-start(f32[128,128]{1,0:T(8,128)S(1)} %add_add_fusion.4), channel_id=1, source_target_pairs={{0,32},{4,36},{8,40},{12,44},{16,48},{20,52},{24,56},{28,60},{32,0... | collective-permute-start | bytes 196616 | tf_op jit(solution)/shard_map/ppermute | solution.py:115
  39.9 9.5 %collective-permute-start.7 = (f32[128,128]{1,0:T(8,128)S(1)}, f32[128,128]{1,0:T(8,128)S(1)}, u32[]{:S(2)}, u32[]{:S(2)}) collective-permute-start(f32[128,128]{1,0:T(8,128)S(1)} %add_add_fusion.4), channel_id=1, source_target_pairs={{0,48},{4,52},{8,56},{12,60},{16,32},{20,36},{24,40},{28,44},{32,1... | collective-permute-start | bytes 196616 | tf_op jit(solution)/shard_map/ppermute | solution.py:115
  49.4 5.6 %collective-permute-start.10 = (f32[128,128]{1,0:T(8,128)S(1)}, f32[128,128]{1,0:T(8,128)S(1)}, u32[]{:S(2)}, u32[]{:S(2)}) collective-permute-start(f32[128,128]{1,0:T(8,128)S(1)} %add_add_fusion.3), channel_id=1, source_target_pairs={{0,192},{4,196},{8,200},{12,204},{16,208},{20,212},{24,216},{28,22... | collective-permute-start | bytes 196616 | tf_op jit(solution)/shard_map/ppermute | solution.py:115
  52.0 4.4 %collective-permute-start.8 = (f32[128,128]{1,0:T(8,128)S(1)}, f32[128,128]{1,0:T(8,128)S(1)}, u32[]{:S(2)}, u32[]{:S(2)}) collective-permute-start(f32[128,128]{1,0:T(8,128)S(1)} %add_add_fusion.3), channel_id=1, source_target_pairs={{0,64},{4,68},{8,72},{12,76},{16,80},{20,84},{24,88},{28,92},{32,9... | collective-permute-start | bytes 196616 | tf_op jit(solution)/shard_map/ppermute | solution.py:115
  52.7 5.8 %collective-permute-start.9 = (f32[128,128]{1,0:T(8,128)S(1)}, f32[128,128]{1,0:T(8,128)S(1)}, u32[]{:S(2)}, u32[]{:S(2)}) collective-permute-start(f32[128,128]{1,0:T(8,128)S(1)} %add_add_fusion.3), channel_id=1, source_target_pairs={{0,128},{4,132},{8,136},{12,140},{16,144},{20,148},{24,152},{28,15... | collective-permute-start | bytes 196616 | tf_op jit(solution)/shard_map/ppermute | solution.py:115
  70.5 15.1 %collective-permute-start.11 = (f32[32,4096]{1,0:T(8,128)S(1)}, f32[32,4096]{1,0:T(8,128)S(1)}, u32[]{:S(2)}, u32[]{:S(2)}) collective-permute-start(f32[32,4096]{1,0:T(8,128)S(1)} %fusion.4), channel_id=1, source_target_pairs={{0,1},{1,2},{2,3},{3,0},{4,5},{5,6},{6,7},{7,4},{8,9},{9,10},{10,1... | collective-permute-start | bytes 1572872 | tf_op jit(solution)/shard_map/ppermute | solution.py:246
  74.8 21.6 %collective-permute-start.12 = (f32[32,4096]{1,0:T(8,128)S(1)}, f32[32,4096]{1,0:T(8,128)S(1)}, u32[]{:S(2)}, u32[]{:S(2)}) collective-permute-start(f32[32,4096]{1,0:T(8,128)S(1)} %fusion.2), channel_id=1, source_target_pairs={{0,2},{1,3},{2,0},{3,1},{4,6},{5,7},{6,4},{7,5},{8,10},{9,11},{10,... | collective-permute-start | bytes 1572872 | tf_op jit(solution)/shard_map/ppermute | solution.py:246
  80.3 18.6 %collective-permute-start.13 = (f32[32,4096]{1,0:T(8,128)S(1)}, f32[32,4096]{1,0:T(8,128)}, u32[]{:S(2)}, u32[]{:S(2)}) collective-permute-start(f32[32,4096]{1,0:T(8,128)S(1)} %fusion), channel_id=1, source_target_pairs={{0,3},{1,0},{2,1},{3,2},{4,7},{5,4},{6,5},{7,6},{8,11},{9,8},{10,9... | collective-permute-start | bytes 1572872 | tf_op jit(solution)/shard_map/ppermute | solution.py:246
  103.1 5.1 %collective-permute-start.15 = (f32[128,128]{1,0:T(8,128)S(1)}, f32[128,128]{1,0:T(8,128)S(1)}, u32[]{:S(2)}, u32[]{:S(2)}) collective-permute-start(f32[128,128]{1,0:T(8,128)S(1)} %broadcast_select_fusion.1), channel_id=1, source_target_pairs={{0,8},{4,12},{8,0},{12,4},{16,24},{20,28},{24,16},{28,20},{32,40},... | collective-permute-start | bytes 196616 | tf_op jit(solution)/shard_map/ppermute | solution.py:115
  103.2 5.2 %collective-permute-start.16 = (f32[128,128]{1,0:T(8,128)S(1)}, f32[128,128]{1,0:T(8,128)S(1)}, u32[]{:S(2)}, u32[]{:S(2)}) collective-permute-start(f32[128,128]{1,0:T(8,128)S(1)} %broadcast_select_fusion.1), channel_id=1, source_target_pairs={{0,12},{4,8},{8,4},{12,0},{16,28},{20,24},{24,20},{28,16},{32,44},... | collective-permute-start | bytes 196616 | tf_op jit(solution)/shard_map/ppermute | solution.py:115
  108.5 6.6 %collective-permute-start.17 = (f32[128,128]{1,0:T(8,128)S(1)}, f32[128,128]{1,0:T(8,128)S(1)}, u32[]{:S(2)}, u32[]{:S(2)}) collective-permute-start(f32[128,128]{1,0:T(8,128)S(1)} %add_add_fusion.2), channel_id=1, source_target_pairs={{0,16},{4,20},{8,24},{12,28},{16,0},{20,4},{24,8},{28,12},{32,48},... | collective-permute-start | bytes 196616 | tf_op jit(solution)/shard_map/ppermute | solution.py:115
  110.1 10.4 %collective-permute-start.18 = (f32[128,128]{1,0:T(8,128)S(1)}, f32[128,128]{1,0:T(8,128)S(1)}, u32[]{:S(2)}, u32[]{:S(2)}) collective-permute-start(f32[128,128]{1,0:T(8,128)S(1)} %add_add_fusion.2), channel_id=1, source_target_pairs={{0,32},{4,36},{8,40},{12,44},{16,48},{20,52},{24,56},{28,60},{32,0... | collective-permute-start | bytes 196616 | tf_op jit(solution)/shard_map/ppermute | solution.py:115
  112.8 9.2 %collective-permute-start.19 = (f32[128,128]{1,0:T(8,128)S(1)}, f32[128,128]{1,0:T(8,128)S(1)}, u32[]{:S(2)}, u32[]{:S(2)}) collective-permute-start(f32[128,128]{1,0:T(8,128)S(1)} %add_add_fusion.2), channel_id=1, source_target_pairs={{0,48},{4,52},{8,56},{12,60},{16,32},{20,36},{24,40},{28,44},{32,1... | collective-permute-start | bytes 196616 | tf_op jit(solution)/shard_map/ppermute | solution.py:115
  122.0 4.9 %collective-permute-start.20 = (f32[128,128]{1,0:T(8,128)S(1)}, f32[128,128]{1,0:T(8,128)S(1)}, u32[]{:S(2)}, u32[]{:S(2)}) collective-permute-start(f32[128,128]{1,0:T(8,128)S(1)} %add_add_fusion.1), channel_id=1, source_target_pairs={{0,64},{4,68},{8,72},{12,76},{16,80},{20,84},{24,88},{28,92},{32,9... | collective-permute-start | bytes 196616 | tf_op jit(solution)/shard_map/ppermute | solution.py:115
  123.3 5.9 %collective-permute-start.21 = (f32[128,128]{1,0:T(8,128)S(1)}, f32[128,128]{1,0:T(8,128)S(1)}, u32[]{:S(2)}, u32[]{:S(2)}) collective-permute-start(f32[128,128]{1,0:T(8,128)S(1)} %add_add_fusion.1), channel_id=1, source_target_pairs={{0,128},{4,132},{8,136},{12,140},{16,144},{20,148},{24,152},{28,15... | collective-permute-start | bytes 196616 | tf_op jit(solution)/shard_map/ppermute | solution.py:115
  125.0 5.5 %collective-permute-start.22 = (f32[128,128]{1,0:T(8,128)S(1)}, f32[128,128]{1,0:T(8,128)S(1)}, u32[]{:S(2)}, u32[]{:S(2)}) collective-permute-start(f32[128,128]{1,0:T(8,128)S(1)} %add_add_fusion.1), channel_id=1, source_target_pairs={{0,192},{4,196},{8,200},{12,204},{16,208},{20,212},{24,216},{28,22... | collective-permute-start | bytes 196616 | tf_op jit(solution)/shard_map/ppermute | solution.py:115
  130.5 5.2 %collective-permute-start.23 = (f32[128,128]{1,0:T(8,128)S(1)}, f32[128,128]{1,0:T(8,128)S(1)}, u32[]{:S(2)}, u32[]{:S(2)}) collective-permute-start(f32[128,128]{1,0:T(8,128)S(1)} %add_add_fusion), channel_id=1, source_target_pairs={{0,1},{1,0},{2,3},{3,2},{4,5},{5,4},{6,7},{7,6},{8,9},{9,8},{10,11... | collective-permute-start | bytes 196616 | tf_op jit(solution)/shard_map/ppermute | solution.py:115
  133.0 5.8 %collective-permute-start.24 = (f32[128,128]{1,0:T(8,128)S(1)}, f32[128,128]{1,0:T(8,128)S(1)}, u32[]{:S(2)}, u32[]{:S(2)}) collective-permute-start(f32[128,128]{1,0:T(8,128)S(1)} %add_add_fusion), channel_id=1, source_target_pairs={{0,2},{1,3},{2,0},{3,1},{4,6},{5,7},{6,4},{7,5},{8,10},{9,11},{10,... | collective-permute-start | bytes 196616 | tf_op jit(solution)/shard_map/ppermute | solution.py:115
  134.7 5.5 %collective-permute-start.25 = (f32[128,128]{1,0:T(8,128)S(1)}, f32[128,128]{1,0:T(8,128)S(1)}, u32[]{:S(2)}, u32[]{:S(2)}) collective-permute-start(f32[128,128]{1,0:T(8,128)S(1)} %add_add_fusion), channel_id=1, source_target_pairs={{0,3},{1,2},{2,1},{3,0},{4,7},{5,6},{6,5},{7,4},{8,11},{9,10},{10,... | collective-permute-start | bytes 196616 | tf_op jit(solution)/shard_map/ppermute | solution.py:115
  (6 other events, 50.2 us)

commit v7 on v6

--- a/solution.py
+++ b/solution.py
@@ -65,9 +65,9 @@
     chunk = out_ref[...]
     high_part = chunk.astype(jnp.bfloat16)
     low_part = (chunk - high_part.astype(jnp.float32)).astype(jnp.bfloat16)
-    dims = (((0,), (0,)), ((), ()))
-    main = lax.dot_general(high_part, high_part, dims, preferred_element_type=jnp.float32)
-    cross = lax.dot_general(high_part, low_part, dims, preferred_element_type=jnp.float32)
+    high_t = high_part.T
+    main = jnp.dot(high_t, high_part, preferred_element_type=jnp.float32)
+    cross = jnp.dot(high_t, low_part, preferred_element_type=jnp.float32)
     gram_ref[...] += main + (cross + cross.T)
 
 

time: 166 us -> 166 us (level)
  no operation moved by 1% of the time
where the time goes in v7:
time: 166 us; the launch traced here: 165 us
  waiting for transfers between devices  48.4 us (29%)
  starting transfers between devices  47.5 us (29%)
  Pallas kernels  41.2 us (25%)
  matrix products  17.8 us (11%)
  local copies, waits for them, and re-layouts  6.66 us (4%)
  other arithmetic  3.21 us (2%)
    ppermute x21, starting transfers between devices, butterfly_sum(): parts.append(lax.ppermute(x, axis, pairs))  35.9 us
    ppermute x21, waiting for transfers between devices, butterfly_sum(): parts.append(lax.ppermute(x, axis, pairs))  34.2 us
    pallas_call x3, Pallas kernels, subspace_batch(): pl.pallas_call(subspace_kernel, out_shape=jax.ShapeDtypeStruct((batch, ra...  26 us
    pallas_call x1, Pallas kernels, apply_mass(): pl.pallas_call(mass_kernel, grid_spec=grid_spec, out_shape=[jax.ShapeDtyp...  15.2 us
    ppermute x3, waiting for transfers between devices, shards(): received[shift] = lax.ppermute(piece, 'freq', pairs)  14 us
    dot_general x4, matrix products, modes_of(): lax.dot_general(weights, rows_part, (((0,), (1,)), ((), ())), precision=H...  10.9 us
    ppermute x3, starting transfers between devices, shards(): received[shift] = lax.ppermute(piece, 'freq', pairs)  6.06 us
    ppermute x1, starting transfers between devices, shards(): high = lax.ppermute(snapshots[:width], 'rows', backward)  3.64 us
  transfers between devices with their start and end apart: 26, of which 20 were waited for; matrix products, arithmetic and copies ran while one was open for 6% of the time, Pallas kernels for 0%

profile of v7, /device:TPU:32, one launch (start us, length us, event | category | flops | bytes accessed | tf_op | source)
XLA Modules:
  0.0 165.1 jit_solution(9468642787281533664)
XLA Ops:
  2.8 3.6 %collective-permute-start.1 = (bf16[256,128]{1,0:T(8,128)(2,1)S(1)}, bf16[256,128]{1,0:T(8,128)(2,1)S(1)}, u32[]{:S(2)}, u32[]{:S(2)}) collective-permute-start(bf16[256,128]{1,0:T(8,128)(2,1)S(1)} %get-tuple-element.9), channel_id=1, source_target_pairs={{4,0},{8,4},{12,8},{16,12},{20,16},{24,20},{28,24},{32,28},{36,32}... | collective-permute-start | bytes 196616 | tf_op jit(solution)/shard_map/ppermute | solution.py:228
  9.3 15.2 %shard_map.55 = (f32[16384,128]{1,0:T(8,128)}, f32[128,128]{1,0:T(8,128)}) custom-call(s32[384]{0:T(512)} %reshape.69.index_ref, bf16[256,128]{1,0:T(8,128)(2,1)} %copy-done.1, bf16[16384,128]{1,0:T(8,128)(2,1)} %own_ref.1, bf16[256,128]{1,0:T(8,128)(2,1)} %copy-done.2, bf16[128,3,128,128]{3,2,1,0:T(8,128)(2,1)} %mass_ref.1), custom_call_target="tpu_custom_call" | custom-call | tf_op jit(solution)/shard_map/pallas_call | solution.py:92
  27.7 3.6 %collective-permute-done.3 = f32[128,128]{1,0:T(8,128)S(1)} collective-permute-done((f32[128,128]{1,0:T(8,128)}, f32[128,128]{1,0:T(8,128)S(1)}, u32[]{:S(2)}, u32[]{:S(2)}) %collective-permute-start.3) | collective-permute-done | bytes 65568 | tf_op jit(solution)/shard_map/ppermute | solution.py:115
  32.1 5.8 %collective-permute-start.5 = (f32[128,128]{1,0:T(8,128)S(1)}, f32[128,128]{1,0:T(8,128)S(1)}, u32[]{:S(2)}, u32[]{:S(2)}) collective-permute-start(f32[128,128]{1,0:T(8,128)S(1)} %add_add_fusion.4), channel_id=1, source_target_pairs={{0,16},{4,20},{8,24},{12,28},{16,0},{20,4},{24,8},{28,12},{32,48},... | collective-permute-start | bytes 196616 | tf_op jit(solution)/shard_map/ppermute | solution.py:115
  42.1 5.3 %collective-permute-done.6 = f32[128,128]{1,0:T(8,128)S(1)} collective-permute-done((f32[128,128]{1,0:T(8,128)S(1)}, f32[128,128]{1,0:T(8,128)S(1)}, u32[]{:S(2)}, u32[]{:S(2)}) %collective-permute-start.6) | collective-permute-done | bytes 65568 | tf_op jit(solution)/shard_map/ppermute | solution.py:115
  49.4 2.6 %collective-permute-start.10 = (f32[128,128]{1,0:T(8,128)S(1)}, f32[128,128]{1,0:T(8,128)S(1)}, u32[]{:S(2)}, u32[]{:S(2)}) collective-permute-start(f32[128,128]{1,0:T(8,128)S(1)} %add_add_fusion.3), channel_id=1, source_target_pairs={{0,192},{4,196},{8,200},{12,204},{16,208},{20,212},{24,216},{28,22... | collective-permute-start | bytes 196616 | tf_op jit(solution)/shard_map/ppermute | solution.py:115
  59.1 8.6 %shard_map.56 = f32[1,32,128]{2,1,0:T(8,128)} custom-call(f32[1,128,128]{2,1,0:T(8,128)} %multiply_bitcast_fusion.g_ref, f32[1,32,128]{2,1,0:T(8,128)} %bitcast.47), custom_call_target="tpu_custom_call" | custom-call | tf_op jit(solution)/shard_map/pallas_call | solution.py:167
  67.7 2.7 %fusion.4 = f32[32,4096]{1,0:T(8,128)S(1)} fusion(f32[16384,128]{1,0:T(8,128)} %get-tuple-element.8, s32[]{:T(128)S(6)} %select_n.82, f32[1,32,128]{2,1,0:T(8,128)} %shard_map.56), kind=kOutput, calls=%fused_computation.8 | convolution fusion | flops 100663296 | bytes 2637828 | tf_op jit(solution)/shard_map/dot_general | solution.py:240
  72.0 2.7 %fusion.2 = f32[32,4096]{1,0:T(8,128)S(1)} fusion(f32[16384,128]{1,0:T(8,128)} %get-tuple-element.8, s32[]{:T(128)S(6)} %select_n.84, f32[1,32,128]{2,1,0:T(8,128)S(1)} %copy-done), kind=kOutput, calls=%fused_computation.6 | convolution fusion | flops 100663296 | bytes 2637828 | tf_op jit(solution)/shard_map/dot_general | solution.py:240
  74.8 2.8 %collective-permute-start.12 = (f32[32,4096]{1,0:T(8,128)S(1)}, f32[32,4096]{1,0:T(8,128)S(1)}, u32[]{:S(2)}, u32[]{:S(2)}) collective-permute-start(f32[32,4096]{1,0:T(8,128)S(1)} %fusion.2), channel_id=1, source_target_pairs={{0,2},{1,3},{2,0},{3,1},{4,6},{5,7},{6,4},{7,5},{8,10},{9,11},{10,... | collective-permute-start | bytes 1572872 | tf_op jit(solution)/shard_map/ppermute | solution.py:246
  77.6 2.7 %fusion = f32[32,4096]{1,0:T(8,128)S(1)} fusion(f32[16384,128]{1,0:T(8,128)} %get-tuple-element.8, s32[]{:T(128)S(6)} %select_n.86, f32[1,32,128]{2,1,0:T(8,128)S(1)} %copy-done), kind=kOutput, calls=%fused_computation.4 | convolution fusion | flops 100663296 | bytes 2637828 | tf_op jit(solution)/shard_map/dot_general | solution.py:240
  82.2 2.7 %fusion.6 = f32[32,4096]{1,0:T(8,128)S(1)} fusion(f32[16384,128]{1,0:T(8,128)} %get-tuple-element.8, s32[]{:T(128)S(6)} %select_n.80, f32[1,32,128]{2,1,0:T(8,128)S(1)} %copy-done), kind=kOutput, calls=%fused_computation.10 | convolution fusion | flops 100663296 | bytes 2637828 | tf_op jit(solution)/shard_map/dot_general | solution.py:240
  85.6 10.8 %collective-permute-done.12 = f32[32,4096]{1,0:T(8,128)S(1)} collective-permute-done((f32[32,4096]{1,0:T(8,128)S(1)}, f32[32,4096]{1,0:T(8,128)S(1)}, u32[]{:S(2)}, u32[]{:S(2)}) %collective-permute-start.12) | collective-permute-done | bytes 524320 | tf_op jit(solution)/shard_map/ppermute | solution.py:246
  96.3 2.6 %collective-permute-done.13 = f32[32,4096]{1,0:T(8,128)} collective-permute-done((f32[32,4096]{1,0:T(8,128)S(1)}, f32[32,4096]{1,0:T(8,128)}, u32[]{:S(2)}, u32[]{:S(2)}) %collective-permute-start.13) | collective-permute-done | bytes 524320 | tf_op jit(solution)/shard_map/ppermute | solution.py:246
  98.9 2.3 %fusion.9 = f32[128,128]{1,0:T(8,128)S(1)} fusion(f32[32,4096]{1,0:T(8,128)} %collective-permute-done.13, f32[32,4096]{1,0:T(8,128)S(1)} %collective-permute-done.12, f32[32,4096]{1,0:T(8,128)S(1)} %collective-permute-done.11, f32[32,4096]{1,0:T(8,128)S(1)} %fusion.6), kind=kOutput, calls=%fused_computation.13 | convolution fusion | flops 404226048 | bytes 2162688 | tf_op jit(solution)/shard_map/dot_general | solution.py:250
  105.0 3.2 %collective-permute-done.15 = f32[128,128]{1,0:T(8,128)S(1)} collective-permute-done((f32[128,128]{1,0:T(8,128)S(1)}, f32[128,128]{1,0:T(8,128)S(1)}, u32[]{:S(2)}, u32[]{:S(2)}) %collective-permute-start.15) | collective-permute-done | bytes 65568 | tf_op jit(solution)/shard_map/ppermute | solution.py:115
  110.1 2.7 %collective-permute-start.18 = (f32[128,128]{1,0:T(8,128)S(1)}, f32[128,128]{1,0:T(8,128)S(1)}, u32[]{:S(2)}, u32[]{:S(2)}) collective-permute-start(f32[128,128]{1,0:T(8,128)S(1)} %add_add_fusion.2), channel_id=1, source_target_pairs={{0,32},{4,36},{8,40},{12,44},{16,48},{20,52},{24,56},{28,60},{32,0... | collective-permute-start | bytes 196616 | tf_op jit(solution)/shard_map/ppermute | solution.py:115
  112.8 2.3 %collective-permute-start.19 = (f32[128,128]{1,0:T(8,128)S(1)}, f32[128,128]{1,0:T(8,128)S(1)}, u32[]{:S(2)}, u32[]{:S(2)}) collective-permute-start(f32[128,128]{1,0:T(8,128)S(1)} %add_add_fusion.2), channel_id=1, source_target_pairs={{0,48},{4,52},{8,56},{12,60},{16,32},{20,36},{24,40},{28,44},{32,1... | collective-permute-start | bytes 196616 | tf_op jit(solution)/shard_map/ppermute | solution.py:115
  115.1 5.4 %collective-permute-done.18 = f32[128,128]{1,0:T(8,128)S(1)} collective-permute-done((f32[128,128]{1,0:T(8,128)S(1)}, f32[128,128]{1,0:T(8,128)S(1)}, u32[]{:S(2)}, u32[]{:S(2)}) %collective-permute-start.18) | collective-permute-done | bytes 65568 | tf_op jit(solution)/shard_map/ppermute | solution.py:115
  130.5 2.5 %collective-permute-start.23 = (f32[128,128]{1,0:T(8,128)S(1)}, f32[128,128]{1,0:T(8,128)S(1)}, u32[]{:S(2)}, u32[]{:S(2)}) collective-permute-start(f32[128,128]{1,0:T(8,128)S(1)} %add_add_fusion), channel_id=1, source_target_pairs={{0,1},{1,0},{2,3},{3,2},{4,5},{5,4},{6,7},{7,6},{8,9},{9,8},{10,11... | collective-permute-start | bytes 196616 | tf_op jit(solution)/shard_map/ppermute | solution.py:115
  135.8 3.0 %collective-permute-done.24 = f32[128,128]{1,0:T(8,128)S(1)} collective-permute-done((f32[128,128]{1,0:T(8,128)S(1)}, f32[128,128]{1,0:T(8,128)S(1)}, u32[]{:S(2)}, u32[]{:S(2)}) %collective-permute-start.24) | collective-permute-done | bytes 65568 | tf_op jit(solution)/shard_map/ppermute | solution.py:115
  141.5 9.0 %shard_map.57 = f32[2,32,64]{2,1,0:T(8,128)} custom-call(f32[2,64,64]{2,1,0:T(8,128)} %pad_maximum_fusion.3.g_ref, f32[2,32,64]{2,1,0:T(8,128)} %broadcast_in_dim.62.v_ref), custom_call_target="tpu_custom_call" | custom-call | tf_op jit(solution)/shard_map/pallas_call | solution.py:167
  152.5 8.4 %shard_map.58 = f32[1,32,64]{2,1,0:T(8,128)} custom-call(f32[1,64,64]{2,1,0:T(8,128)} %convolution_bitcast_fusion.g_ref, f32[1,32,64]{2,1,0:T(8,128)} %bitcast.45), custom_call_target="tpu_custom_call" | custom-call | tf_op jit(solution)/shard_map/pallas_call | solution.py:167
  162.5 2.6 %fusion.8 = f32[32,4096]{1,0:T(8,128)} fusion(f32[128,32]{1,0:T(8,128)S(1)} %bitcast_select_fusion, f32[32,4096]{1,0:T(8,128)} %collective-permute-done.13, f32[32,4096]{1,0:T(8,128)S(1)} %collective-permute-done.12, f32[32,4096]{1,0:T(8,128)S(1)} %collective-permute-done.11, f32[32,4096]{1,0:T(8,128)S(1)} %fusion.6), kind=kOutput, calls=%fused_computation.12 | convolution fusion | flops 102236160 | bytes 2637824 | tf_op jit(solution)/shard_map/dot_general | solution.py:258
  (81 shorter events, 51.8 us)
Async XLA Ops:
  0.9 7.2 %collective-permute-start = (bf16[256,128]{1,0:T(8,128)(2,1)S(1)}, bf16[256,128]{1,0:T(8,128)(2,1)S(1)}, u32[]{:S(2)}, u32[]{:S(2)}) collective-permute-start(bf16[256,128]{1,0:T(8,128)(2,1)S(1)} %get-tuple-element.10), channel_id=1, source_target_pairs={{0,4},{4,8},{8,12},{12,16},{16,20},{20,24},{24,28},{28,32},{32,36}... | collective-permute-start | bytes 196616 | tf_op jit(solution)/shard_map/ppermute | solution.py:227
  2.8 5.5 %collective-permute-start.1 = (bf16[256,128]{1,0:T(8,128)(2,1)S(1)}, bf16[256,128]{1,0:T(8,128)(2,1)S(1)}, u32[]{:S(2)}, u32[]{:S(2)}) collective-permute-start(bf16[256,128]{1,0:T(8,128)(2,1)S(1)} %get-tuple-element.9), channel_id=1, source_target_pairs={{4,0},{8,4},{12,8},{16,12},{20,16},{24,20},{28,24},{32,28},{36,32}... | collective-permute-start | bytes 196616 | tf_op jit(solution)/shard_map/ppermute | solution.py:228
  26.3 5.0 %collective-permute-start.3 = (f32[128,128]{1,0:T(8,128)}, f32[128,128]{1,0:T(8,128)S(1)}, u32[]{:S(2)}, u32[]{:S(2)}) collective-permute-start(f32[128,128]{1,0:T(8,128)} %get-tuple-element.7), channel_id=1, source_target_pairs={{0,8},{4,12},{8,0},{12,4},{16,24},{20,28},{24,16},{28,20},{32,40},... | collective-permute-start | bytes 196616 | tf_op jit(solution)/shard_map/ppermute | solution.py:115
  26.4 4.9 %collective-permute-start.4 = (f32[128,128]{1,0:T(8,128)}, f32[128,128]{1,0:T(8,128)S(1)}, u32[]{:S(2)}, u32[]{:S(2)}) collective-permute-start(f32[128,128]{1,0:T(8,128)} %get-tuple-element.7), channel_id=1, source_target_pairs={{0,12},{4,8},{8,4},{12,0},{16,28},{20,24},{24,20},{28,16},{32,44},... | collective-permute-start | bytes 196616 | tf_op jit(solution)/shard_map/ppermute | solution.py:115
  32.1 10.0 %collective-permute-start.5 = (f32[128,128]{1,0:T(8,128)S(1)}, f32[128,128]{1,0:T(8,128)S(1)}, u32[]{:S(2)}, u32[]{:S(2)}) collective-permute-start(f32[128,128]{1,0:T(8,128)S(1)} %add_add_fusion.4), channel_id=1, source_target_pairs={{0,16},{4,20},{8,24},{12,28},{16,0},{20,4},{24,8},{28,12},{32,48},... | collective-permute-start | bytes 196616 | tf_op jit(solution)/shard_map/ppermute | solution.py:115
  37.9 9.5 %collective-permute-start.6 = (f32[128,128]{1,0:T(8,128)S(1)}, f32[128,128]{1,0:T(8,128)S(1)}, u32[]{:S(2)}, u32[]{:S(2)}) collective-permute-start(f32[128,128]{1,0:T(8,128)S(1)} %add_add_fusion.4), channel_id=1, source_target_pairs={{0,32},{4,36},{8,40},{12,44},{16,48},{20,52},{24,56},{28,60},{32,0... | collective-permute-start | bytes 196616 | tf_op jit(solution)/shard_map/ppermute | solution.py:115
  39.9 9.5 %collective-permute-start.7 = (f32[128,128]{1,0:T(8,128)S(1)}, f32[128,128]{1,0:T(8,128)S(1)}, u32[]{:S(2)}, u32[]{:S(2)}) collective-permute-start(f32[128,128]{1,0:T(8,128)S(1)} %add_add_fusion.4), channel_id=1, source_target_pairs={{0,48},{4,52},{8,56},{12,60},{16,32},{20,36},{24,40},{28,44},{32,1... | collective-permute-start | bytes 196616 | tf_op jit(solution)/shard_map/ppermute | solution.py:115
  49.4 5.6 %collective-permute-start.10 = (f32[128,128]{1,0:T(8,128)S(1)}, f32[128,128]{1,0:T(8,128)S(1)}, u32[]{:S(2)}, u32[]{:S(2)}) collective-permute-start(f32[128,128]{1,0:T(8,128)S(1)} %add_add_fusion.3), channel_id=1, source_target_pairs={{0,192},{4,196},{8,200},{12,204},{16,208},{20,212},{24,216},{28,22... | collective-permute-start | bytes 196616 | tf_op jit(solution)/shard_map/ppermute | solution.py:115
  52.0 4.4 %collective-permute-start.8 = (f32[128,128]{1,0:T(8,128)S(1)}, f32[128,128]{1,0:T(8,128)S(1)}, u32[]{:S(2)}, u32[]{:S(2)}) collective-permute-start(f32[128,128]{1,0:T(8,128)S(1)} %add_add_fusion.3), channel_id=1, source_target_pairs={{0,64},{4,68},{8,72},{12,76},{16,80},{20,84},{24,88},{28,92},{32,9... | collective-permute-start | bytes 196616 | tf_op jit(solution)/shard_map/ppermute | solution.py:115
  52.7 5.8 %collective-permute-start.9 = (f32[128,128]{1,0:T(8,128)S(1)}, f32[128,128]{1,0:T(8,128)S(1)}, u32[]{:S(2)}, u32[]{:S(2)}) collective-permute-start(f32[128,128]{1,0:T(8,128)S(1)} %add_add_fusion.3), channel_id=1, source_target_pairs={{0,128},{4,132},{8,136},{12,140},{16,144},{20,148},{24,152},{28,15... | collective-permute-start | bytes 196616 | tf_op jit(solution)/shard_map/ppermute | solution.py:115
  70.5 15.1 %collective-permute-start.11 = (f32[32,4096]{1,0:T(8,128)S(1)}, f32[32,4096]{1,0:T(8,128)S(1)}, u32[]{:S(2)}, u32[]{:S(2)}) collective-permute-start(f32[32,4096]{1,0:T(8,128)S(1)} %fusion.4), channel_id=1, source_target_pairs={{0,1},{1,2},{2,3},{3,0},{4,5},{5,6},{6,7},{7,4},{8,9},{9,10},{10,1... | collective-permute-start | bytes 1572872 | tf_op jit(solution)/shard_map/ppermute | solution.py:246
  74.8 21.6 %collective-permute-start.12 = (f32[32,4096]{1,0:T(8,128)S(1)}, f32[32,4096]{1,0:T(8,128)S(1)}, u32[]{:S(2)}, u32[]{:S(2)}) collective-permute-start(f32[32,4096]{1,0:T(8,128)S(1)} %fusion.2), channel_id=1, source_target_pairs={{0,2},{1,3},{2,0},{3,1},{4,6},{5,7},{6,4},{7,5},{8,10},{9,11},{10,... | collective-permute-start | bytes 1572872 | tf_op jit(solution)/shard_map/ppermute | solution.py:246
  80.3 18.6 %collective-permute-start.13 = (f32[32,4096]{1,0:T(8,128)S(1)}, f32[32,4096]{1,0:T(8,128)}, u32[]{:S(2)}, u32[]{:S(2)}) collective-permute-start(f32[32,4096]{1,0:T(8,128)S(1)} %fusion), channel_id=1, source_target_pairs={{0,3},{1,0},{2,1},{3,2},{4,7},{5,4},{6,5},{7,6},{8,11},{9,8},{10,9... | collective-permute-start | bytes 1572872 | tf_op jit(solution)/shard_map/ppermute | solution.py:246
  103.1 5.1 %collective-permute-start.15 = (f32[128,128]{1,0:T(8,128)S(1)}, f32[128,128]{1,0:T(8,128)S(1)}, u32[]{:S(2)}, u32[]{:S(2)}) collective-permute-start(f32[128,128]{1,0:T(8,128)S(1)} %broadcast_select_fusion.1), channel_id=1, source_target_pairs={{0,8},{4,12},{8,0},{12,4},{16,24},{20,28},{24,16},{28,20},{32,40},... | collective-permute-start | bytes 196616 | tf_op jit(solution)/shard_map/ppermute | solution.py:115
  103.2 5.2 %collective-permute-start.16 = (f32[128,128]{1,0:T(8,128)S(1)}, f32[128,128]{1,0:T(8,128)S(1)}, u32[]{:S(2)}, u32[]{:S(2)}) collective-permute-start(f32[128,128]{1,0:T(8,128)S(1)} %broadcast_select_fusion.1), channel_id=1, source_target_pairs={{0,12},{4,8},{8,4},{12,0},{16,28},{20,24},{24,20},{28,16},{32,44},... | collective-permute-start | bytes 196616 | tf_op jit(solution)/shard_map/ppermute | solution.py:115
  108.5 6.6 %collective-permute-start.17 = (f32[128,128]{1,0:T(8,128)S(1)}, f32[128,128]{1,0:T(8,128)S(1)}, u32[]{:S(2)}, u32[]{:S(2)}) collective-permute-start(f32[128,128]{1,0:T(8,128)S(1)} %add_add_fusion.2), channel_id=1, source_target_pairs={{0,16},{4,20},{8,24},{12,28},{16,0},{20,4},{24,8},{28,12},{32,48},... | collective-permute-start | bytes 196616 | tf_op jit(solution)/shard_map/ppermute | solution.py:115
  110.1 10.4 %collective-permute-start.18 = (f32[128,128]{1,0:T(8,128)S(1)}, f32[128,128]{1,0:T(8,128)S(1)}, u32[]{:S(2)}, u32[]{:S(2)}) collective-permute-start(f32[128,128]{1,0:T(8,128)S(1)} %add_add_fusion.2), channel_id=1, source_target_pairs={{0,32},{4,36},{8,40},{12,44},{16,48},{20,52},{24,56},{28,60},{32,0... | collective-permute-start | bytes 196616 | tf_op jit(solution)/shard_map/ppermute | solution.py:115
  112.8 9.2 %collective-permute-start.19 = (f32[128,128]{1,0:T(8,128)S(1)}, f32[128,128]{1,0:T(8,128)S(1)}, u32[]{:S(2)}, u32[]{:S(2)}) collective-permute-start(f32[128,128]{1,0:T(8,128)S(1)} %add_add_fusion.2), channel_id=1, source_target_pairs={{0,48},{4,52},{8,56},{12,60},{16,32},{20,36},{24,40},{28,44},{32,1... | collective-permute-start | bytes 196616 | tf_op jit(solution)/shard_map/ppermute | solution.py:115
  122.0 4.9 %collective-permute-start.20 = (f32[128,128]{1,0:T(8,128)S(1)}, f32[128,128]{1,0:T(8,128)S(1)}, u32[]{:S(2)}, u32[]{:S(2)}) collective-permute-start(f32[128,128]{1,0:T(8,128)S(1)} %add_add_fusion.1), channel_id=1, source_target_pairs={{0,64},{4,68},{8,72},{12,76},{16,80},{20,84},{24,88},{28,92},{32,9... | collective-permute-start | bytes 196616 | tf_op jit(solution)/shard_map/ppermute | solution.py:115
  123.3 5.9 %collective-permute-start.21 = (f32[128,128]{1,0:T(8,128)S(1)}, f32[128,128]{1,0:T(8,128)S(1)}, u32[]{:S(2)}, u32[]{:S(2)}) collective-permute-start(f32[128,128]{1,0:T(8,128)S(1)} %add_add_fusion.1), channel_id=1, source_target_pairs={{0,128},{4,132},{8,136},{12,140},{16,144},{20,148},{24,152},{28,15... | collective-permute-start | bytes 196616 | tf_op jit(solution)/shard_map/ppermute | solution.py:115
  125.0 5.5 %collective-permute-start.22 = (f32[128,128]{1,0:T(8,128)S(1)}, f32[128,128]{1,0:T(8,128)S(1)}, u32[]{:S(2)}, u32[]{:S(2)}) collective-permute-start(f32[128,128]{1,0:T(8,128)S(1)} %add_add_fusion.1), channel_id=1, source_target_pairs={{0,192},{4,196},{8,200},{12,204},{16,208},{20,212},{24,216},{28,22... | collective-permute-start | bytes 196616 | tf_op jit(solution)/shard_map/ppermute | solution.py:115
  130.5 5.2 %collective-permute-start.23 = (f32[128,128]{1,0:T(8,128)S(1)}, f32[128,128]{1,0:T(8,128)S(1)}, u32[]{:S(2)}, u32[]{:S(2)}) collective-permute-start(f32[128,128]{1,0:T(8,128)S(1)} %add_add_fusion), channel_id=1, source_target_pairs={{0,1},{1,0},{2,3},{3,2},{4,5},{5,4},{6,7},{7,6},{8,9},{9,8},{10,11... | collective-permute-start | bytes 196616 | tf_op jit(solution)/shard_map/ppermute | solution.py:115
  133.0 5.8 %collective-permute-start.24 = (f32[128,128]{1,0:T(8,128)S(1)}, f32[128,128]{1,0:T(8,128)S(1)}, u32[]{:S(2)}, u32[]{:S(2)}) collective-permute-start(f32[128,128]{1,0:T(8,128)S(1)} %add_add_fusion), channel_id=1, source_target_pairs={{0,2},{1,3},{2,0},{3,1},{4,6},{5,7},{6,4},{7,5},{8,10},{9,11},{10,... | collective-permute-start | bytes 196616 | tf_op jit(solution)/shard_map/ppermute | solution.py:115
  134.7 5.5 %collective-permute-start.25 = (f32[128,128]{1,0:T(8,128)S(1)}, f32[128,128]{1,0:T(8,128)S(1)}, u32[]{:S(2)}, u32[]{:S(2)}) collective-permute-start(f32[128,128]{1,0:T(8,128)S(1)} %add_add_fusion), channel_id=1, source_target_pairs={{0,3},{1,2},{2,1},{3,0},{4,7},{5,6},{6,5},{7,4},{8,11},{9,10},{10,... | collective-permute-start | bytes 196616 | tf_op jit(solution)/shard_map/ppermute | solution.py:115
  (6 other events, 50.2 us)

commit v8 on v4

--- a/solution.py
+++ b/solution.py
@@ -130,9 +130,9 @@
         carry = []
         for b in range(batch):
             product = lax.dot_general(
-                currents[b], grams[b], nt, precision=HIGHEST, preferred_element_type=jnp.float32
+                currents[b], grams[b], nt, precision=HIGH, preferred_element_type=jnp.float32
             )
-            inner = lax.dot_general(product, product, nt, precision=HIGHEST, preferred_element_type=jnp.float32)
+            inner = lax.dot_general(product, product, nt, precision=HIGH, preferred_element_type=jnp.float32)
             carry.append((inner, product, jnp.zeros_like(product)))
 
         def one_column(j, carry):

time: 165 us -> 165 us (level)
  no operation moved by 1% of the time
where the time goes in v8:
time: 165 us; the launch traced here: 164 us
  waiting for transfers between devices  48.4 us (29%)
  starting transfers between devices  47.6 us (29%)
  Pallas kernels  40 us (24%)
  matrix products  17.8 us (11%)
  local copies, waits for them, and re-layouts  6.66 us (4%)
  other arithmetic  3.21 us (2%)
    ppermute x21, starting transfers between devices, butterfly_sum(): parts.append(lax.ppermute(x, axis, pairs))  35.9 us
    ppermute x21, waiting for transfers between devices, butterfly_sum(): parts.append(lax.ppermute(x, axis, pairs))  34.2 us
    pallas_call x3, Pallas kernels, subspace_batch(): pl.pallas_call(subspace_kernel, out_shape=jax.ShapeDtypeStruct((batch, ra...  25.3 us
    pallas_call x1, Pallas kernels, apply_mass(): pl.pallas_call(mass_kernel, grid_spec=grid_spec, out_shape=[jax.ShapeDtyp...  14.7 us
    ppermute x3, waiting for transfers between devices, shards(): received[shift] = lax.ppermute(piece, 'freq', pairs)  14 us
    dot_general x4, matrix products, modes_of(): lax.dot_general(weights, rows_part, (((0,), (1,)), ((), ())), precision=H...  10.9 us
    ppermute x3, starting transfers between devices, shards(): received[shift] = lax.ppermute(piece, 'freq', pairs)  6.08 us
    ppermute x1, starting transfers between devices, shards(): high = lax.ppermute(snapshots[:width], 'rows', backward)  3.64 us
  transfers between devices with their start and end apart: 26, of which 20 were waited for; matrix products, arithmetic and copies ran while one was open for 6% of the time, Pallas kernels for 0%

profile of v8, /device:TPU:32, one launch (start us, length us, event | category | flops | bytes accessed | tf_op | source)
XLA Modules:
  0.0 163.9 jit_solution(4490308876490516310)
XLA Ops:
  2.8 3.6 %collective-permute-start.1 = (bf16[256,128]{1,0:T(8,128)(2,1)S(1)}, bf16[256,128]{1,0:T(8,128)(2,1)S(1)}, u32[]{:S(2)}, u32[]{:S(2)}) collective-permute-start(bf16[256,128]{1,0:T(8,128)(2,1)S(1)} %get-tuple-element.9), channel_id=1, source_target_pairs={{4,0},{8,4},{12,8},{16,12},{20,16},{24,20},{28,24},{32,28},{36,32}... | collective-permute-start | bytes 196616 | tf_op jit(solution)/shard_map/ppermute | solution.py:224
  9.3 14.7 %shard_map.55 = (f32[16384,128]{1,0:T(8,128)}, f32[128,128]{1,0:T(8,128)}) custom-call(s32[384]{0:T(512)} %reshape.69.index_ref, bf16[256,128]{1,0:T(8,128)(2,1)} %copy-done.1, bf16[16384,128]{1,0:T(8,128)(2,1)} %own_ref.1, bf16[256,128]{1,0:T(8,128)(2,1)} %copy-done.2, bf16[128,3,128,128]{3,2,1,0:T(8,128)(2,1)} %mass_ref.1), custom_call_target="tpu_custom_call" | custom-call | tf_op jit(solution)/shard_map/pallas_call | solution.py:88
  27.2 3.6 %collective-permute-done.3 = f32[128,128]{1,0:T(8,128)S(1)} collective-permute-done((f32[128,128]{1,0:T(8,128)}, f32[128,128]{1,0:T(8,128)S(1)}, u32[]{:S(2)}, u32[]{:S(2)}) %collective-permute-start.3) | collective-permute-done | bytes 65568 | tf_op jit(solution)/shard_map/ppermute | solution.py:111
  31.6 5.8 %collective-permute-start.5 = (f32[128,128]{1,0:T(8,128)S(1)}, f32[128,128]{1,0:T(8,128)S(1)}, u32[]{:S(2)}, u32[]{:S(2)}) collective-permute-start(f32[128,128]{1,0:T(8,128)S(1)} %add_add_fusion.4), channel_id=1, source_target_pairs={{0,16},{4,20},{8,24},{12,28},{16,0},{20,4},{24,8},{28,12},{32,48},... | collective-permute-start | bytes 196616 | tf_op jit(solution)/shard_map/ppermute | solution.py:111
  41.6 5.3 %collective-permute-done.6 = f32[128,128]{1,0:T(8,128)S(1)} collective-permute-done((f32[128,128]{1,0:T(8,128)S(1)}, f32[128,128]{1,0:T(8,128)S(1)}, u32[]{:S(2)}, u32[]{:S(2)}) %collective-permute-start.6) | collective-permute-done | bytes 65568 | tf_op jit(solution)/shard_map/ppermute | solution.py:111
  48.9 2.6 %collective-permute-start.10 = (f32[128,128]{1,0:T(8,128)S(1)}, f32[128,128]{1,0:T(8,128)S(1)}, u32[]{:S(2)}, u32[]{:S(2)}) collective-permute-start(f32[128,128]{1,0:T(8,128)S(1)} %add_add_fusion.3), channel_id=1, source_target_pairs={{0,192},{4,196},{8,200},{12,204},{16,208},{20,212},{24,216},{28,22... | collective-permute-start | bytes 196616 | tf_op jit(solution)/shard_map/ppermute | solution.py:111
  58.6 8.4 %shard_map.56 = f32[1,32,128]{2,1,0:T(8,128)} custom-call(f32[1,128,128]{2,1,0:T(8,128)} %multiply_bitcast_fusion.g_ref, f32[1,32,128]{2,1,0:T(8,128)} %bitcast.47), custom_call_target="tpu_custom_call" | custom-call | tf_op jit(solution)/shard_map/pallas_call | solution.py:163
  66.9 2.7 %fusion.4 = f32[32,4096]{1,0:T(8,128)S(1)} fusion(f32[16384,128]{1,0:T(8,128)} %get-tuple-element.8, s32[]{:T(128)S(6)} %select_n.82, f32[1,32,128]{2,1,0:T(8,128)} %shard_map.56), kind=kOutput, calls=%fused_computation.8 | convolution fusion | flops 100663296 | bytes 2637828 | tf_op jit(solution)/shard_map/dot_general | solution.py:236
  71.3 2.7 %fusion.2 = f32[32,4096]{1,0:T(8,128)S(1)} fusion(f32[16384,128]{1,0:T(8,128)} %get-tuple-element.8, s32[]{:T(128)S(6)} %select_n.84, f32[1,32,128]{2,1,0:T(8,128)S(1)} %copy-done), kind=kOutput, calls=%fused_computation.6 | convolution fusion | flops 100663296 | bytes 2637828 | tf_op jit(solution)/shard_map/dot_general | solution.py:236
  74.0 2.8 %collective-permute-start.12 = (f32[32,4096]{1,0:T(8,128)S(1)}, f32[32,4096]{1,0:T(8,128)S(1)}, u32[]{:S(2)}, u32[]{:S(2)}) collective-permute-start(f32[32,4096]{1,0:T(8,128)S(1)} %fusion.2), channel_id=1, source_target_pairs={{0,2},{1,3},{2,0},{3,1},{4,6},{5,7},{6,4},{7,5},{8,10},{9,11},{10,... | collective-permute-start | bytes 1572872 | tf_op jit(solution)/shard_map/ppermute | solution.py:242
  76.8 2.7 %fusion = f32[32,4096]{1,0:T(8,128)S(1)} fusion(f32[16384,128]{1,0:T(8,128)} %get-tuple-element.8, s32[]{:T(128)S(6)} %select_n.86, f32[1,32,128]{2,1,0:T(8,128)S(1)} %copy-done), kind=kOutput, calls=%fused_computation.4 | convolution fusion | flops 100663296 | bytes 2637828 | tf_op jit(solution)/shard_map/dot_general | solution.py:236
  81.4 2.7 %fusion.6 = f32[32,4096]{1,0:T(8,128)S(1)} fusion(f32[16384,128]{1,0:T(8,128)} %get-tuple-element.8, s32[]{:T(128)S(6)} %select_n.80, f32[1,32,128]{2,1,0:T(8,128)S(1)} %copy-done), kind=kOutput, calls=%fused_computation.10 | convolution fusion | flops 100663296 | bytes 2637828 | tf_op jit(solution)/shard_map/dot_general | solution.py:236
  84.8 10.8 %collective-permute-done.12 = f32[32,4096]{1,0:T(8,128)S(1)} collective-permute-done((f32[32,4096]{1,0:T(8,128)S(1)}, f32[32,4096]{1,0:T(8,128)S(1)}, u32[]{:S(2)}, u32[]{:S(2)}) %collective-permute-start.12) | collective-permute-done | bytes 524320 | tf_op jit(solution)/shard_map/ppermute | solution.py:242
  95.6 2.6 %collective-permute-done.13 = f32[32,4096]{1,0:T(8,128)} collective-permute-done((f32[32,4096]{1,0:T(8,128)S(1)}, f32[32,4096]{1,0:T(8,128)}, u32[]{:S(2)}, u32[]{:S(2)}) %collective-permute-start.13) | collective-permute-done | bytes 524320 | tf_op jit(solution)/shard_map/ppermute | solution.py:242
  98.1 2.3 %fusion.9 = f32[128,128]{1,0:T(8,128)S(1)} fusion(f32[32,4096]{1,0:T(8,128)} %collective-permute-done.13, f32[32,4096]{1,0:T(8,128)S(1)} %collective-permute-done.12, f32[32,4096]{1,0:T(8,128)S(1)} %collective-permute-done.11, f32[32,4096]{1,0:T(8,128)S(1)} %fusion.6), kind=kOutput, calls=%fused_computation.13 | convolution fusion | flops 404226048 | bytes 2162688 | tf_op jit(solution)/shard_map/dot_general | solution.py:246
  104.2 3.2 %collective-permute-done.15 = f32[128,128]{1,0:T(8,128)S(1)} collective-permute-done((f32[128,128]{1,0:T(8,128)S(1)}, f32[128,128]{1,0:T(8,128)S(1)}, u32[]{:S(2)}, u32[]{:S(2)}) %collective-permute-start.15) | collective-permute-done | bytes 65568 | tf_op jit(solution)/shard_map/ppermute | solution.py:111
  109.3 2.7 %collective-permute-start.18 = (f32[128,128]{1,0:T(8,128)S(1)}, f32[128,128]{1,0:T(8,128)S(1)}, u32[]{:S(2)}, u32[]{:S(2)}) collective-permute-start(f32[128,128]{1,0:T(8,128)S(1)} %add_add_fusion.2), channel_id=1, source_target_pairs={{0,32},{4,36},{8,40},{12,44},{16,48},{20,52},{24,56},{28,60},{32,0... | collective-permute-start | bytes 196616 | tf_op jit(solution)/shard_map/ppermute | solution.py:111
  114.3 5.4 %collective-permute-done.18 = f32[128,128]{1,0:T(8,128)S(1)} collective-permute-done((f32[128,128]{1,0:T(8,128)S(1)}, f32[128,128]{1,0:T(8,128)S(1)}, u32[]{:S(2)}, u32[]{:S(2)}) %collective-permute-start.18) | collective-permute-done | bytes 65568 | tf_op jit(solution)/shard_map/ppermute | solution.py:111
  126.1 2.2 %collective-permute-done.21 = f32[128,128]{1,0:T(8,128)S(1)} collective-permute-done((f32[128,128]{1,0:T(8,128)S(1)}, f32[128,128]{1,0:T(8,128)S(1)}, u32[]{:S(2)}, u32[]{:S(2)}) %collective-permute-start.21) | collective-permute-done | bytes 65568 | tf_op jit(solution)/shard_map/ppermute | solution.py:111
  129.8 2.5 %collective-permute-start.23 = (f32[128,128]{1,0:T(8,128)S(1)}, f32[128,128]{1,0:T(8,128)S(1)}, u32[]{:S(2)}, u32[]{:S(2)}) collective-permute-start(f32[128,128]{1,0:T(8,128)S(1)} %add_add_fusion), channel_id=1, source_target_pairs={{0,1},{1,0},{2,3},{3,2},{4,5},{5,4},{6,7},{7,6},{8,9},{9,8},{10,11... | collective-permute-start | bytes 196616 | tf_op jit(solution)/shard_map/ppermute | solution.py:111
  135.0 3.0 %collective-permute-done.24 = f32[128,128]{1,0:T(8,128)S(1)} collective-permute-done((f32[128,128]{1,0:T(8,128)S(1)}, f32[128,128]{1,0:T(8,128)S(1)}, u32[]{:S(2)}, u32[]{:S(2)}) %collective-permute-start.24) | collective-permute-done | bytes 65568 | tf_op jit(solution)/shard_map/ppermute | solution.py:111
  140.8 8.7 %shard_map.57 = f32[2,32,64]{2,1,0:T(8,128)} custom-call(f32[2,64,64]{2,1,0:T(8,128)} %pad_maximum_fusion.3.g_ref, f32[2,32,64]{2,1,0:T(8,128)} %broadcast_in_dim.62.v_ref), custom_call_target="tpu_custom_call" | custom-call | tf_op jit(solution)/shard_map/pallas_call | solution.py:163
  151.5 8.2 %shard_map.58 = f32[1,32,64]{2,1,0:T(8,128)} custom-call(f32[1,64,64]{2,1,0:T(8,128)} %convolution_bitcast_fusion.g_ref, f32[1,32,64]{2,1,0:T(8,128)} %bitcast.45), custom_call_target="tpu_custom_call" | custom-call | tf_op jit(solution)/shard_map/pallas_call | solution.py:163
  161.3 2.6 %fusion.8 = f32[32,4096]{1,0:T(8,128)} fusion(f32[128,32]{1,0:T(8,128)S(1)} %bitcast_select_fusion, f32[32,4096]{1,0:T(8,128)} %collective-permute-done.13, f32[32,4096]{1,0:T(8,128)S(1)} %collective-permute-done.12, f32[32,4096]{1,0:T(8,128)S(1)} %collective-permute-done.11, f32[32,4096]{1,0:T(8,128)S(1)} %fusion.6), kind=kOutput, calls=%fused_computation.12 | convolution fusion | flops 102236160 | bytes 2637824 | tf_op jit(solution)/shard_map/dot_general | solution.py:254
  (81 shorter events, 51.8 us)
Async XLA Ops:
  0.9 7.2 %collective-permute-start = (bf16[256,128]{1,0:T(8,128)(2,1)S(1)}, bf16[256,128]{1,0:T(8,128)(2,1)S(1)}, u32[]{:S(2)}, u32[]{:S(2)}) collective-permute-start(bf16[256,128]{1,0:T(8,128)(2,1)S(1)} %get-tuple-element.10), channel_id=1, source_target_pairs={{0,4},{4,8},{8,12},{12,16},{16,20},{20,24},{24,28},{28,32},{32,36}... | collective-permute-start | bytes 196616 | tf_op jit(solution)/shard_map/ppermute | solution.py:223
  2.8 5.5 %collective-permute-start.1 = (bf16[256,128]{1,0:T(8,128)(2,1)S(1)}, bf16[256,128]{1,0:T(8,128)(2,1)S(1)}, u32[]{:S(2)}, u32[]{:S(2)}) collective-permute-start(bf16[256,128]{1,0:T(8,128)(2,1)S(1)} %get-tuple-element.9), channel_id=1, source_target_pairs={{4,0},{8,4},{12,8},{16,12},{20,16},{24,20},{28,24},{32,28},{36,32}... | collective-permute-start | bytes 196616 | tf_op jit(solution)/shard_map/ppermute | solution.py:224
  25.8 5.0 %collective-permute-start.3 = (f32[128,128]{1,0:T(8,128)}, f32[128,128]{1,0:T(8,128)S(1)}, u32[]{:S(2)}, u32[]{:S(2)}) collective-permute-start(f32[128,128]{1,0:T(8,128)} %get-tuple-element.7), channel_id=1, source_target_pairs={{0,8},{4,12},{8,0},{12,4},{16,24},{20,28},{24,16},{28,20},{32,40},... | collective-permute-start | bytes 196616 | tf_op jit(solution)/shard_map/ppermute | solution.py:111
  25.9 4.9 %collective-permute-start.4 = (f32[128,128]{1,0:T(8,128)}, f32[128,128]{1,0:T(8,128)S(1)}, u32[]{:S(2)}, u32[]{:S(2)}) collective-permute-start(f32[128,128]{1,0:T(8,128)} %get-tuple-element.7), channel_id=1, source_target_pairs={{0,12},{4,8},{8,4},{12,0},{16,28},{20,24},{24,20},{28,16},{32,44},... | collective-permute-start | bytes 196616 | tf_op jit(solution)/shard_map/ppermute | solution.py:111
  31.6 10.0 %collective-permute-start.5 = (f32[128,128]{1,0:T(8,128)S(1)}, f32[128,128]{1,0:T(8,128)S(1)}, u32[]{:S(2)}, u32[]{:S(2)}) collective-permute-start(f32[128,128]{1,0:T(8,128)S(1)} %add_add_fusion.4), channel_id=1, source_target_pairs={{0,16},{4,20},{8,24},{12,28},{16,0},{20,4},{24,8},{28,12},{32,48},... | collective-permute-start | bytes 196616 | tf_op jit(solution)/shard_map/ppermute | solution.py:111
  37.4 9.5 %collective-permute-start.6 = (f32[128,128]{1,0:T(8,128)S(1)}, f32[128,128]{1,0:T(8,128)S(1)}, u32[]{:S(2)}, u32[]{:S(2)}) collective-permute-start(f32[128,128]{1,0:T(8,128)S(1)} %add_add_fusion.4), channel_id=1, source_target_pairs={{0,32},{4,36},{8,40},{12,44},{16,48},{20,52},{24,56},{28,60},{32,0... | collective-permute-start | bytes 196616 | tf_op jit(solution)/shard_map/ppermute | solution.py:111
  39.4 9.5 %collective-permute-start.7 = (f32[128,128]{1,0:T(8,128)S(1)}, f32[128,128]{1,0:T(8,128)S(1)}, u32[]{:S(2)}, u32[]{:S(2)}) collective-permute-start(f32[128,128]{1,0:T(8,128)S(1)} %add_add_fusion.4), channel_id=1, source_target_pairs={{0,48},{4,52},{8,56},{12,60},{16,32},{20,36},{24,40},{28,44},{32,1... | collective-permute-start | bytes 196616 | tf_op jit(solution)/shard_map/ppermute | solution.py:111
  48.9 5.6 %collective-permute-start.10 = (f32[128,128]{1,0:T(8,128)S(1)}, f32[128,128]{1,0:T(8,128)S(1)}, u32[]{:S(2)}, u32[]{:S(2)}) collective-permute-start(f32[128,128]{1,0:T(8,128)S(1)} %add_add_fusion.3), channel_id=1, source_target_pairs={{0,192},{4,196},{8,200},{12,204},{16,208},{20,212},{24,216},{28,22... | collective-permute-start | bytes 196616 | tf_op jit(solution)/shard_map/ppermute | solution.py:111
  51.5 4.4 %collective-permute-start.8 = (f32[128,128]{1,0:T(8,128)S(1)}, f32[128,128]{1,0:T(8,128)S(1)}, u32[]{:S(2)}, u32[]{:S(2)}) collective-permute-start(f32[128,128]{1,0:T(8,128)S(1)} %add_add_fusion.3), channel_id=1, source_target_pairs={{0,64},{4,68},{8,72},{12,76},{16,80},{20,84},{24,88},{28,92},{32,9... | collective-permute-start | bytes 196616 | tf_op jit(solution)/shard_map/ppermute | solution.py:111
  52.2 5.8 %collective-permute-start.9 = (f32[128,128]{1,0:T(8,128)S(1)}, f32[128,128]{1,0:T(8,128)S(1)}, u32[]{:S(2)}, u32[]{:S(2)}) collective-permute-start(f32[128,128]{1,0:T(8,128)S(1)} %add_add_fusion.3), channel_id=1, source_target_pairs={{0,128},{4,132},{8,136},{12,140},{16,144},{20,148},{24,152},{28,15... | collective-permute-start | bytes 196616 | tf_op jit(solution)/shard_map/ppermute | solution.py:111
  69.7 15.1 %collective-permute-start.11 = (f32[32,4096]{1,0:T(8,128)S(1)}, f32[32,4096]{1,0:T(8,128)S(1)}, u32[]{:S(2)}, u32[]{:S(2)}) collective-permute-start(f32[32,4096]{1,0:T(8,128)S(1)} %fusion.4), channel_id=1, source_target_pairs={{0,1},{1,2},{2,3},{3,0},{4,5},{5,6},{6,7},{7,4},{8,9},{9,10},{10,1... | collective-permute-start | bytes 1572872 | tf_op jit(solution)/shard_map/ppermute | solution.py:242
  74.0 21.6 %collective-permute-start.12 = (f32[32,4096]{1,0:T(8,128)S(1)}, f32[32,4096]{1,0:T(8,128)S(1)}, u32[]{:S(2)}, u32[]{:S(2)}) collective-permute-start(f32[32,4096]{1,0:T(8,128)S(1)} %fusion.2), channel_id=1, source_target_pairs={{0,2},{1,3},{2,0},{3,1},{4,6},{5,7},{6,4},{7,5},{8,10},{9,11},{10,... | collective-permute-start | bytes 1572872 | tf_op jit(solution)/shard_map/ppermute | solution.py:242
  79.5 18.6 %collective-permute-start.13 = (f32[32,4096]{1,0:T(8,128)S(1)}, f32[32,4096]{1,0:T(8,128)}, u32[]{:S(2)}, u32[]{:S(2)}) collective-permute-start(f32[32,4096]{1,0:T(8,128)S(1)} %fusion), channel_id=1, source_target_pairs={{0,3},{1,0},{2,1},{3,2},{4,7},{5,4},{6,5},{7,6},{8,11},{9,8},{10,9... | collective-permute-start | bytes 1572872 | tf_op jit(solution)/shard_map/ppermute | solution.py:242
  102.3 5.1 %collective-permute-start.15 = (f32[128,128]{1,0:T(8,128)S(1)}, f32[128,128]{1,0:T(8,128)S(1)}, u32[]{:S(2)}, u32[]{:S(2)}) collective-permute-start(f32[128,128]{1,0:T(8,128)S(1)} %broadcast_select_fusion.1), channel_id=1, source_target_pairs={{0,8},{4,12},{8,0},{12,4},{16,24},{20,28},{24,16},{28,20},{32,40},... | collective-permute-start | bytes 196616 | tf_op jit(solution)/shard_map/ppermute | solution.py:111
  102.4 5.2 %collective-permute-start.16 = (f32[128,128]{1,0:T(8,128)S(1)}, f32[128,128]{1,0:T(8,128)S(1)}, u32[]{:S(2)}, u32[]{:S(2)}) collective-permute-start(f32[128,128]{1,0:T(8,128)S(1)} %broadcast_select_fusion.1), channel_id=1, source_target_pairs={{0,12},{4,8},{8,4},{12,0},{16,28},{20,24},{24,20},{28,16},{32,44},... | collective-permute-start | bytes 196616 | tf_op jit(solution)/shard_map/ppermute | solution.py:111
  107.7 6.6 %collective-permute-start.17 = (f32[128,128]{1,0:T(8,128)S(1)}, f32[128,128]{1,0:T(8,128)S(1)}, u32[]{:S(2)}, u32[]{:S(2)}) collective-permute-start(f32[128,128]{1,0:T(8,128)S(1)} %add_add_fusion.2), channel_id=1, source_target_pairs={{0,16},{4,20},{8,24},{12,28},{16,0},{20,4},{24,8},{28,12},{32,48},... | collective-permute-start | bytes 196616 | tf_op jit(solution)/shard_map/ppermute | solution.py:111
  109.3 10.4 %collective-permute-start.18 = (f32[128,128]{1,0:T(8,128)S(1)}, f32[128,128]{1,0:T(8,128)S(1)}, u32[]{:S(2)}, u32[]{:S(2)}) collective-permute-start(f32[128,128]{1,0:T(8,128)S(1)} %add_add_fusion.2), channel_id=1, source_target_pairs={{0,32},{4,36},{8,40},{12,44},{16,48},{20,52},{24,56},{28,60},{32,0... | collective-permute-start | bytes 196616 | tf_op jit(solution)/shard_map/ppermute | solution.py:111
  112.0 9.2 %collective-permute-start.19 = (f32[128,128]{1,0:T(8,128)S(1)}, f32[128,128]{1,0:T(8,128)S(1)}, u32[]{:S(2)}, u32[]{:S(2)}) collective-permute-start(f32[128,128]{1,0:T(8,128)S(1)} %add_add_fusion.2), channel_id=1, source_target_pairs={{0,48},{4,52},{8,56},{12,60},{16,32},{20,36},{24,40},{28,44},{32,1... | collective-permute-start | bytes 196616 | tf_op jit(solution)/shard_map/ppermute | solution.py:111
  121.2 4.9 %collective-permute-start.20 = (f32[128,128]{1,0:T(8,128)S(1)}, f32[128,128]{1,0:T(8,128)S(1)}, u32[]{:S(2)}, u32[]{:S(2)}) collective-permute-start(f32[128,128]{1,0:T(8,128)S(1)} %add_add_fusion.1), channel_id=1, source_target_pairs={{0,64},{4,68},{8,72},{12,76},{16,80},{20,84},{24,88},{28,92},{32,9... | collective-permute-start | bytes 196616 | tf_op jit(solution)/shard_map/ppermute | solution.py:111
  122.5 5.9 %collective-permute-start.21 = (f32[128,128]{1,0:T(8,128)S(1)}, f32[128,128]{1,0:T(8,128)S(1)}, u32[]{:S(2)}, u32[]{:S(2)}) collective-permute-start(f32[128,128]{1,0:T(8,128)S(1)} %add_add_fusion.1), channel_id=1, source_target_pairs={{0,128},{4,132},{8,136},{12,140},{16,144},{20,148},{24,152},{28,15... | collective-permute-start | bytes 196616 | tf_op jit(solution)/shard_map/ppermute | solution.py:111
  124.3 5.5 %collective-permute-start.22 = (f32[128,128]{1,0:T(8,128)S(1)}, f32[128,128]{1,0:T(8,128)S(1)}, u32[]{:S(2)}, u32[]{:S(2)}) collective-permute-start(f32[128,128]{1,0:T(8,128)S(1)} %add_add_fusion.1), channel_id=1, source_target_pairs={{0,192},{4,196},{8,200},{12,204},{16,208},{20,212},{24,216},{28,22... | collective-permute-start | bytes 196616 | tf_op jit(solution)/shard_map/ppermute | solution.py:111
  129.8 5.2 %collective-permute-start.23 = (f32[128,128]{1,0:T(8,128)S(1)}, f32[128,128]{1,0:T(8,128)S(1)}, u32[]{:S(2)}, u32[]{:S(2)}) collective-permute-start(f32[128,128]{1,0:T(8,128)S(1)} %add_add_fusion), channel_id=1, source_target_pairs={{0,1},{1,0},{2,3},{3,2},{4,5},{5,4},{6,7},{7,6},{8,9},{9,8},{10,11... | collective-permute-start | bytes 196616 | tf_op jit(solution)/shard_map/ppermute | solution.py:111
  132.2 5.8 %collective-permute-start.24 = (f32[128,128]{1,0:T(8,128)S(1)}, f32[128,128]{1,0:T(8,128)S(1)}, u32[]{:S(2)}, u32[]{:S(2)}) collective-permute-start(f32[128,128]{1,0:T(8,128)S(1)} %add_add_fusion), channel_id=1, source_target_pairs={{0,2},{1,3},{2,0},{3,1},{4,6},{5,7},{6,4},{7,5},{8,10},{9,11},{10,... | collective-permute-start | bytes 196616 | tf_op jit(solution)/shard_map/ppermute | solution.py:111
  133.9 5.5 %collective-permute-start.25 = (f32[128,128]{1,0:T(8,128)S(1)}, f32[128,128]{1,0:T(8,128)S(1)}, u32[]{:S(2)}, u32[]{:S(2)}) collective-permute-start(f32[128,128]{1,0:T(8,128)S(1)} %add_add_fusion), channel_id=1, source_target_pairs={{0,3},{1,2},{2,1},{3,0},{4,7},{5,6},{6,5},{7,4},{8,11},{9,10},{10,... | collective-permute-start | bytes 196616 | tf_op jit(solution)/shard_map/ppermute | solution.py:111
  (6 other events, 50.2 us)

commit v9 on v4

--- a/solution.py
+++ b/solution.py
@@ -26,7 +26,7 @@
     return block
 
 
-ROWS_PER_STEP = 16
+ROWS_PER_STEP = 32
 
 
 def mass_kernel(index_ref, low_ref, own_ref, high_ref, mass_ref, out_ref, gram_ref):

time: 165 us -> 165 us (level)
  no operation moved by 1% of the time
where the time goes in v9:
time: 165 us; the launch traced here: 164 us
  waiting for transfers between devices  48.6 us (29%)
  starting transfers between devices  47.6 us (29%)
  Pallas kernels  39.7 us (24%)
  matrix products  17.8 us (11%)
  local copies, waits for them, and re-layouts  6.66 us (4%)
  other arithmetic  3.21 us (2%)
    ppermute x21, starting transfers between devices, butterfly_sum(): parts.append(lax.ppermute(x, axis, pairs))  35.9 us
    ppermute x21, waiting for transfers between devices, butterfly_sum(): parts.append(lax.ppermute(x, axis, pairs))  34.2 us
    pallas_call x3, Pallas kernels, subspace_batch(): pl.pallas_call(subspace_kernel, out_shape=jax.ShapeDtypeStruct((batch, ra...  26 us
    ppermute x3, waiting for transfers between devices, shards(): received[shift] = lax.ppermute(piece, 'freq', pairs)  14.1 us
    pallas_call x1, Pallas kernels, apply_mass(): pl.pallas_call(mass_kernel, grid_spec=grid_spec, out_shape=[jax.ShapeDtyp...  13.7 us
    dot_general x4, matrix products, modes_of(): lax.dot_general(weights, rows_part, (((0,), (1,)), ((), ())), precision=H...  10.9 us
    ppermute x3, starting transfers between devices, shards(): received[shift] = lax.ppermute(piece, 'freq', pairs)  6.07 us
    ppermute x1, starting transfers between devices, shards(): high = lax.ppermute(snapshots[:width], 'rows', backward)  3.64 us
  transfers between devices with their start and end apart: 26, of which 20 were waited for; matrix products, arithmetic and copies ran while one was open for 6% of the time, Pallas kernels for 0%

profile of v9, /device:TPU:32, one launch (start us, length us, event | category | flops | bytes accessed | tf_op | source)
XLA Modules:
  0.0 163.8 jit_solution(11359698718742193882)
XLA Ops:
  2.8 3.6 %collective-permute-start.1 = (bf16[256,128]{1,0:T(8,128)(2,1)S(1)}, bf16[256,128]{1,0:T(8,128)(2,1)S(1)}, u32[]{:S(2)}, u32[]{:S(2)}) collective-permute-start(bf16[256,128]{1,0:T(8,128)(2,1)S(1)} %get-tuple-element.9), channel_id=1, source_target_pairs={{4,0},{8,4},{12,8},{16,12},{20,16},{24,20},{28,24},{32,28},{36,32}... | collective-permute-start | bytes 196616 | tf_op jit(solution)/shard_map/ppermute | solution.py:224
  9.3 13.7 %shard_map.55 = (f32[16384,128]{1,0:T(8,128)}, f32[128,128]{1,0:T(8,128)}) custom-call(s32[384]{0:T(512)} %reshape.69.index_ref, bf16[256,128]{1,0:T(8,128)(2,1)} %copy-done.1, bf16[16384,128]{1,0:T(8,128)(2,1)} %own_ref.1, bf16[256,128]{1,0:T(8,128)(2,1)} %copy-done.2, bf16[128,3,128,128]{3,2,1,0:T(8,128)(2,1)} %mass_ref.1), custom_call_target="tpu_custom_call" | custom-call | tf_op jit(solution)/shard_map/pallas_call | solution.py:88
  26.2 3.6 %collective-permute-done.3 = f32[128,128]{1,0:T(8,128)S(1)} collective-permute-done((f32[128,128]{1,0:T(8,128)}, f32[128,128]{1,0:T(8,128)S(1)}, u32[]{:S(2)}, u32[]{:S(2)}) %collective-permute-start.3) | collective-permute-done | bytes 65568 | tf_op jit(solution)/shard_map/ppermute | solution.py:111
  30.7 5.8 %collective-permute-start.5 = (f32[128,128]{1,0:T(8,128)S(1)}, f32[128,128]{1,0:T(8,128)S(1)}, u32[]{:S(2)}, u32[]{:S(2)}) collective-permute-start(f32[128,128]{1,0:T(8,128)S(1)} %add_add_fusion.4), channel_id=1, source_target_pairs={{0,16},{4,20},{8,24},{12,28},{16,0},{20,4},{24,8},{28,12},{32,48},... | collective-permute-start | bytes 196616 | tf_op jit(solution)/shard_map/ppermute | solution.py:111
  40.7 5.3 %collective-permute-done.6 = f32[128,128]{1,0:T(8,128)S(1)} collective-permute-done((f32[128,128]{1,0:T(8,128)S(1)}, f32[128,128]{1,0:T(8,128)S(1)}, u32[]{:S(2)}, u32[]{:S(2)}) %collective-permute-start.6) | collective-permute-done | bytes 65568 | tf_op jit(solution)/shard_map/ppermute | solution.py:111
  48.0 2.6 %collective-permute-start.10 = (f32[128,128]{1,0:T(8,128)S(1)}, f32[128,128]{1,0:T(8,128)S(1)}, u32[]{:S(2)}, u32[]{:S(2)}) collective-permute-start(f32[128,128]{1,0:T(8,128)S(1)} %add_add_fusion.3), channel_id=1, source_target_pairs={{0,192},{4,196},{8,200},{12,204},{16,208},{20,212},{24,216},{28,22... | collective-permute-start | bytes 196616 | tf_op jit(solution)/shard_map/ppermute | solution.py:111
  57.6 8.6 %shard_map.56 = f32[1,32,128]{2,1,0:T(8,128)} custom-call(f32[1,128,128]{2,1,0:T(8,128)} %multiply_bitcast_fusion.g_ref, f32[1,32,128]{2,1,0:T(8,128)} %bitcast.47), custom_call_target="tpu_custom_call" | custom-call | tf_op jit(solution)/shard_map/pallas_call | solution.py:163
  66.2 2.7 %fusion.4 = f32[32,4096]{1,0:T(8,128)S(1)} fusion(f32[16384,128]{1,0:T(8,128)} %get-tuple-element.8, s32[]{:T(128)S(6)} %select_n.82, f32[1,32,128]{2,1,0:T(8,128)} %shard_map.56), kind=kOutput, calls=%fused_computation.8 | convolution fusion | flops 100663296 | bytes 2637828 | tf_op jit(solution)/shard_map/dot_general | solution.py:236
  70.6 2.7 %fusion.2 = f32[32,4096]{1,0:T(8,128)S(1)} fusion(f32[16384,128]{1,0:T(8,128)} %get-tuple-element.8, s32[]{:T(128)S(6)} %select_n.84, f32[1,32,128]{2,1,0:T(8,128)S(1)} %copy-done), kind=kOutput, calls=%fused_computation.6 | convolution fusion | flops 100663296 | bytes 2637828 | tf_op jit(solution)/shard_map/dot_general | solution.py:236
  73.3 3.0 %collective-permute-start.12 = (f32[32,4096]{1,0:T(8,128)S(1)}, f32[32,4096]{1,0:T(8,128)S(1)}, u32[]{:S(2)}, u32[]{:S(2)}) collective-permute-start(f32[32,4096]{1,0:T(8,128)S(1)} %fusion.2), channel_id=1, source_target_pairs={{0,2},{1,3},{2,0},{3,1},{4,6},{5,7},{6,4},{7,5},{8,10},{9,11},{10,... | collective-permute-start | bytes 1572872 | tf_op jit(solution)/shard_map/ppermute | solution.py:242
  76.3 2.7 %fusion = f32[32,4096]{1,0:T(8,128)S(1)} fusion(f32[16384,128]{1,0:T(8,128)} %get-tuple-element.8, s32[]{:T(128)S(6)} %select_n.86, f32[1,32,128]{2,1,0:T(8,128)S(1)} %copy-done), kind=kOutput, calls=%fused_computation.4 | convolution fusion | flops 100663296 | bytes 2637828 | tf_op jit(solution)/shard_map/dot_general | solution.py:236
  80.7 2.7 %fusion.6 = f32[32,4096]{1,0:T(8,128)S(1)} fusion(f32[16384,128]{1,0:T(8,128)} %get-tuple-element.8, s32[]{:T(128)S(6)} %select_n.80, f32[1,32,128]{2,1,0:T(8,128)S(1)} %copy-done), kind=kOutput, calls=%fused_computation.10 | convolution fusion | flops 100663296 | bytes 2637828 | tf_op jit(solution)/shard_map/dot_general | solution.py:236
  84.1 10.8 %collective-permute-done.12 = f32[32,4096]{1,0:T(8,128)S(1)} collective-permute-done((f32[32,4096]{1,0:T(8,128)S(1)}, f32[32,4096]{1,0:T(8,128)S(1)}, u32[]{:S(2)}, u32[]{:S(2)}) %collective-permute-start.12) | collective-permute-done | bytes 524320 | tf_op jit(solution)/shard_map/ppermute | solution.py:242
  94.9 2.7 %collective-permute-done.13 = f32[32,4096]{1,0:T(8,128)} collective-permute-done((f32[32,4096]{1,0:T(8,128)S(1)}, f32[32,4096]{1,0:T(8,128)}, u32[]{:S(2)}, u32[]{:S(2)}) %collective-permute-start.13) | collective-permute-done | bytes 524320 | tf_op jit(solution)/shard_map/ppermute | solution.py:242
  97.6 2.3 %fusion.9 = f32[128,128]{1,0:T(8,128)S(1)} fusion(f32[32,4096]{1,0:T(8,128)} %collective-permute-done.13, f32[32,4096]{1,0:T(8,128)S(1)} %collective-permute-done.12, f32[32,4096]{1,0:T(8,128)S(1)} %collective-permute-done.11, f32[32,4096]{1,0:T(8,128)S(1)} %fusion.6), kind=kOutput, calls=%fused_computation.13 | convolution fusion | flops 404226048 | bytes 2162688 | tf_op jit(solution)/shard_map/dot_general | solution.py:246
  103.7 3.2 %collective-permute-done.15 = f32[128,128]{1,0:T(8,128)S(1)} collective-permute-done((f32[128,128]{1,0:T(8,128)S(1)}, f32[128,128]{1,0:T(8,128)S(1)}, u32[]{:S(2)}, u32[]{:S(2)}) %collective-permute-start.15) | collective-permute-done | bytes 65568 | tf_op jit(solution)/shard_map/ppermute | solution.py:111
  108.8 2.7 %collective-permute-start.18 = (f32[128,128]{1,0:T(8,128)S(1)}, f32[128,128]{1,0:T(8,128)S(1)}, u32[]{:S(2)}, u32[]{:S(2)}) collective-permute-start(f32[128,128]{1,0:T(8,128)S(1)} %add_add_fusion.2), channel_id=1, source_target_pairs={{0,32},{4,36},{8,40},{12,44},{16,48},{20,52},{24,56},{28,60},{32,0... | collective-permute-start | bytes 196616 | tf_op jit(solution)/shard_map/ppermute | solution.py:111
  113.8 5.4 %collective-permute-done.18 = f32[128,128]{1,0:T(8,128)S(1)} collective-permute-done((f32[128,128]{1,0:T(8,128)S(1)}, f32[128,128]{1,0:T(8,128)S(1)}, u32[]{:S(2)}, u32[]{:S(2)}) %collective-permute-start.18) | collective-permute-done | bytes 65568 | tf_op jit(solution)/shard_map/ppermute | solution.py:111
  125.6 2.3 %collective-permute-done.21 = f32[128,128]{1,0:T(8,128)S(1)} collective-permute-done((f32[128,128]{1,0:T(8,128)S(1)}, f32[128,128]{1,0:T(8,128)S(1)}, u32[]{:S(2)}, u32[]{:S(2)}) %collective-permute-start.21) | collective-permute-done | bytes 65568 | tf_op jit(solution)/shard_map/ppermute | solution.py:111
  129.2 2.5 %collective-permute-start.23 = (f32[128,128]{1,0:T(8,128)S(1)}, f32[128,128]{1,0:T(8,128)S(1)}, u32[]{:S(2)}, u32[]{:S(2)}) collective-permute-start(f32[128,128]{1,0:T(8,128)S(1)} %add_add_fusion), channel_id=1, source_target_pairs={{0,1},{1,0},{2,3},{3,2},{4,5},{5,4},{6,7},{7,6},{8,9},{9,8},{10,11... | collective-permute-start | bytes 196616 | tf_op jit(solution)/shard_map/ppermute | solution.py:111
  134.5 3.0 %collective-permute-done.24 = f32[128,128]{1,0:T(8,128)S(1)} collective-permute-done((f32[128,128]{1,0:T(8,128)S(1)}, f32[128,128]{1,0:T(8,128)S(1)}, u32[]{:S(2)}, u32[]{:S(2)}) %collective-permute-start.24) | collective-permute-done | bytes 65568 | tf_op jit(solution)/shard_map/ppermute | solution.py:111
  140.2 9.0 %shard_map.57 = f32[2,32,64]{2,1,0:T(8,128)} custom-call(f32[2,64,64]{2,1,0:T(8,128)} %pad_maximum_fusion.3.g_ref, f32[2,32,64]{2,1,0:T(8,128)} %broadcast_in_dim.62.v_ref), custom_call_target="tpu_custom_call" | custom-call | tf_op jit(solution)/shard_map/pallas_call | solution.py:163
  151.2 8.4 %shard_map.58 = f32[1,32,64]{2,1,0:T(8,128)} custom-call(f32[1,64,64]{2,1,0:T(8,128)} %convolution_bitcast_fusion.g_ref, f32[1,32,64]{2,1,0:T(8,128)} %bitcast.45), custom_call_target="tpu_custom_call" | custom-call | tf_op jit(solution)/shard_map/pallas_call | solution.py:163
  161.2 2.6 %fusion.8 = f32[32,4096]{1,0:T(8,128)} fusion(f32[128,32]{1,0:T(8,128)S(1)} %bitcast_select_fusion, f32[32,4096]{1,0:T(8,128)} %collective-permute-done.13, f32[32,4096]{1,0:T(8,128)S(1)} %collective-permute-done.12, f32[32,4096]{1,0:T(8,128)S(1)} %collective-permute-done.11, f32[32,4096]{1,0:T(8,128)S(1)} %fusion.6), kind=kOutput, calls=%fused_computation.12 | convolution fusion | flops 102236160 | bytes 2637824 | tf_op jit(solution)/shard_map/dot_general | solution.py:254
  (81 shorter events, 51.6 us)
Async XLA Ops:
  0.9 7.2 %collective-permute-start = (bf16[256,128]{1,0:T(8,128)(2,1)S(1)}, bf16[256,128]{1,0:T(8,128)(2,1)S(1)}, u32[]{:S(2)}, u32[]{:S(2)}) collective-permute-start(bf16[256,128]{1,0:T(8,128)(2,1)S(1)} %get-tuple-element.10), channel_id=1, source_target_pairs={{0,4},{4,8},{8,12},{12,16},{16,20},{20,24},{24,28},{28,32},{32,36}... | collective-permute-start | bytes 196616 | tf_op jit(solution)/shard_map/ppermute | solution.py:223
  2.8 5.5 %collective-permute-start.1 = (bf16[256,128]{1,0:T(8,128)(2,1)S(1)}, bf16[256,128]{1,0:T(8,128)(2,1)S(1)}, u32[]{:S(2)}, u32[]{:S(2)}) collective-permute-start(bf16[256,128]{1,0:T(8,128)(2,1)S(1)} %get-tuple-element.9), channel_id=1, source_target_pairs={{4,0},{8,4},{12,8},{16,12},{20,16},{24,20},{28,24},{32,28},{36,32}... | collective-permute-start | bytes 196616 | tf_op jit(solution)/shard_map/ppermute | solution.py:224
  24.8 5.0 %collective-permute-start.3 = (f32[128,128]{1,0:T(8,128)}, f32[128,128]{1,0:T(8,128)S(1)}, u32[]{:S(2)}, u32[]{:S(2)}) collective-permute-start(f32[128,128]{1,0:T(8,128)} %get-tuple-element.7), channel_id=1, source_target_pairs={{0,8},{4,12},{8,0},{12,4},{16,24},{20,28},{24,16},{28,20},{32,40},... | collective-permute-start | bytes 196616 | tf_op jit(solution)/shard_map/ppermute | solution.py:111
  24.9 4.9 %collective-permute-start.4 = (f32[128,128]{1,0:T(8,128)}, f32[128,128]{1,0:T(8,128)S(1)}, u32[]{:S(2)}, u32[]{:S(2)}) collective-permute-start(f32[128,128]{1,0:T(8,128)} %get-tuple-element.7), channel_id=1, source_target_pairs={{0,12},{4,8},{8,4},{12,0},{16,28},{20,24},{24,20},{28,16},{32,44},... | collective-permute-start | bytes 196616 | tf_op jit(solution)/shard_map/ppermute | solution.py:111
  30.7 10.0 %collective-permute-start.5 = (f32[128,128]{1,0:T(8,128)S(1)}, f32[128,128]{1,0:T(8,128)S(1)}, u32[]{:S(2)}, u32[]{:S(2)}) collective-permute-start(f32[128,128]{1,0:T(8,128)S(1)} %add_add_fusion.4), channel_id=1, source_target_pairs={{0,16},{4,20},{8,24},{12,28},{16,0},{20,4},{24,8},{28,12},{32,48},... | collective-permute-start | bytes 196616 | tf_op jit(solution)/shard_map/ppermute | solution.py:111
  36.4 9.5 %collective-permute-start.6 = (f32[128,128]{1,0:T(8,128)S(1)}, f32[128,128]{1,0:T(8,128)S(1)}, u32[]{:S(2)}, u32[]{:S(2)}) collective-permute-start(f32[128,128]{1,0:T(8,128)S(1)} %add_add_fusion.4), channel_id=1, source_target_pairs={{0,32},{4,36},{8,40},{12,44},{16,48},{20,52},{24,56},{28,60},{32,0... | collective-permute-start | bytes 196616 | tf_op jit(solution)/shard_map/ppermute | solution.py:111
  38.4 9.5 %collective-permute-start.7 = (f32[128,128]{1,0:T(8,128)S(1)}, f32[128,128]{1,0:T(8,128)S(1)}, u32[]{:S(2)}, u32[]{:S(2)}) collective-permute-start(f32[128,128]{1,0:T(8,128)S(1)} %add_add_fusion.4), channel_id=1, source_target_pairs={{0,48},{4,52},{8,56},{12,60},{16,32},{20,36},{24,40},{28,44},{32,1... | collective-permute-start | bytes 196616 | tf_op jit(solution)/shard_map/ppermute | solution.py:111
  48.0 5.6 %collective-permute-start.10 = (f32[128,128]{1,0:T(8,128)S(1)}, f32[128,128]{1,0:T(8,128)S(1)}, u32[]{:S(2)}, u32[]{:S(2)}) collective-permute-start(f32[128,128]{1,0:T(8,128)S(1)} %add_add_fusion.3), channel_id=1, source_target_pairs={{0,192},{4,196},{8,200},{12,204},{16,208},{20,212},{24,216},{28,22... | collective-permute-start | bytes 196616 | tf_op jit(solution)/shard_map/ppermute | solution.py:111
  50.6 4.4 %collective-permute-start.8 = (f32[128,128]{1,0:T(8,128)S(1)}, f32[128,128]{1,0:T(8,128)S(1)}, u32[]{:S(2)}, u32[]{:S(2)}) collective-permute-start(f32[128,128]{1,0:T(8,128)S(1)} %add_add_fusion.3), channel_id=1, source_target_pairs={{0,64},{4,68},{8,72},{12,76},{16,80},{20,84},{24,88},{28,92},{32,9... | collective-permute-start | bytes 196616 | tf_op jit(solution)/shard_map/ppermute | solution.py:111
  51.2 5.8 %collective-permute-start.9 = (f32[128,128]{1,0:T(8,128)S(1)}, f32[128,128]{1,0:T(8,128)S(1)}, u32[]{:S(2)}, u32[]{:S(2)}) collective-permute-start(f32[128,128]{1,0:T(8,128)S(1)} %add_add_fusion.3), channel_id=1, source_target_pairs={{0,128},{4,132},{8,136},{12,140},{16,144},{20,148},{24,152},{28,15... | collective-permute-start | bytes 196616 | tf_op jit(solution)/shard_map/ppermute | solution.py:111
  69.0 15.1 %collective-permute-start.11 = (f32[32,4096]{1,0:T(8,128)S(1)}, f32[32,4096]{1,0:T(8,128)S(1)}, u32[]{:S(2)}, u32[]{:S(2)}) collective-permute-start(f32[32,4096]{1,0:T(8,128)S(1)} %fusion.4), channel_id=1, source_target_pairs={{0,1},{1,2},{2,3},{3,0},{4,5},{5,6},{6,7},{7,4},{8,9},{9,10},{10,1... | collective-permute-start | bytes 1572872 | tf_op jit(solution)/shard_map/ppermute | solution.py:242
  73.3 21.6 %collective-permute-start.12 = (f32[32,4096]{1,0:T(8,128)S(1)}, f32[32,4096]{1,0:T(8,128)S(1)}, u32[]{:S(2)}, u32[]{:S(2)}) collective-permute-start(f32[32,4096]{1,0:T(8,128)S(1)} %fusion.2), channel_id=1, source_target_pairs={{0,2},{1,3},{2,0},{3,1},{4,6},{5,7},{6,4},{7,5},{8,10},{9,11},{10,... | collective-permute-start | bytes 1572872 | tf_op jit(solution)/shard_map/ppermute | solution.py:242
  79.0 18.6 %collective-permute-start.13 = (f32[32,4096]{1,0:T(8,128)S(1)}, f32[32,4096]{1,0:T(8,128)}, u32[]{:S(2)}, u32[]{:S(2)}) collective-permute-start(f32[32,4096]{1,0:T(8,128)S(1)} %fusion), channel_id=1, source_target_pairs={{0,3},{1,0},{2,1},{3,2},{4,7},{5,4},{6,5},{7,6},{8,11},{9,8},{10,9... | collective-permute-start | bytes 1572872 | tf_op jit(solution)/shard_map/ppermute | solution.py:242
  101.8 5.1 %collective-permute-start.15 = (f32[128,128]{1,0:T(8,128)S(1)}, f32[128,128]{1,0:T(8,128)S(1)}, u32[]{:S(2)}, u32[]{:S(2)}) collective-permute-start(f32[128,128]{1,0:T(8,128)S(1)} %broadcast_select_fusion.1), channel_id=1, source_target_pairs={{0,8},{4,12},{8,0},{12,4},{16,24},{20,28},{24,16},{28,20},{32,40},... | collective-permute-start | bytes 196616 | tf_op jit(solution)/shard_map/ppermute | solution.py:111
  101.9 5.2 %collective-permute-start.16 = (f32[128,128]{1,0:T(8,128)S(1)}, f32[128,128]{1,0:T(8,128)S(1)}, u32[]{:S(2)}, u32[]{:S(2)}) collective-permute-start(f32[128,128]{1,0:T(8,128)S(1)} %broadcast_select_fusion.1), channel_id=1, source_target_pairs={{0,12},{4,8},{8,4},{12,0},{16,28},{20,24},{24,20},{28,16},{32,44},... | collective-permute-start | bytes 196616 | tf_op jit(solution)/shard_map/ppermute | solution.py:111
  107.2 6.6 %collective-permute-start.17 = (f32[128,128]{1,0:T(8,128)S(1)}, f32[128,128]{1,0:T(8,128)S(1)}, u32[]{:S(2)}, u32[]{:S(2)}) collective-permute-start(f32[128,128]{1,0:T(8,128)S(1)} %add_add_fusion.2), channel_id=1, source_target_pairs={{0,16},{4,20},{8,24},{12,28},{16,0},{20,4},{24,8},{28,12},{32,48},... | collective-permute-start | bytes 196616 | tf_op jit(solution)/shard_map/ppermute | solution.py:111
  108.8 10.3 %collective-permute-start.18 = (f32[128,128]{1,0:T(8,128)S(1)}, f32[128,128]{1,0:T(8,128)S(1)}, u32[]{:S(2)}, u32[]{:S(2)}) collective-permute-start(f32[128,128]{1,0:T(8,128)S(1)} %add_add_fusion.2), channel_id=1, source_target_pairs={{0,32},{4,36},{8,40},{12,44},{16,48},{20,52},{24,56},{28,60},{32,0... | collective-permute-start | bytes 196616 | tf_op jit(solution)/shard_map/ppermute | solution.py:111
  111.5 9.2 %collective-permute-start.19 = (f32[128,128]{1,0:T(8,128)S(1)}, f32[128,128]{1,0:T(8,128)S(1)}, u32[]{:S(2)}, u32[]{:S(2)}) collective-permute-start(f32[128,128]{1,0:T(8,128)S(1)} %add_add_fusion.2), channel_id=1, source_target_pairs={{0,48},{4,52},{8,56},{12,60},{16,32},{20,36},{24,40},{28,44},{32,1... | collective-permute-start | bytes 196616 | tf_op jit(solution)/shard_map/ppermute | solution.py:111
  120.7 4.9 %collective-permute-start.20 = (f32[128,128]{1,0:T(8,128)S(1)}, f32[128,128]{1,0:T(8,128)S(1)}, u32[]{:S(2)}, u32[]{:S(2)}) collective-permute-start(f32[128,128]{1,0:T(8,128)S(1)} %add_add_fusion.1), channel_id=1, source_target_pairs={{0,64},{4,68},{8,72},{12,76},{16,80},{20,84},{24,88},{28,92},{32,9... | collective-permute-start | bytes 196616 | tf_op jit(solution)/shard_map/ppermute | solution.py:111
  122.0 5.9 %collective-permute-start.21 = (f32[128,128]{1,0:T(8,128)S(1)}, f32[128,128]{1,0:T(8,128)S(1)}, u32[]{:S(2)}, u32[]{:S(2)}) collective-permute-start(f32[128,128]{1,0:T(8,128)S(1)} %add_add_fusion.1), channel_id=1, source_target_pairs={{0,128},{4,132},{8,136},{12,140},{16,144},{20,148},{24,152},{28,15... | collective-permute-start | bytes 196616 | tf_op jit(solution)/shard_map/ppermute | solution.py:111
  123.7 5.5 %collective-permute-start.22 = (f32[128,128]{1,0:T(8,128)S(1)}, f32[128,128]{1,0:T(8,128)S(1)}, u32[]{:S(2)}, u32[]{:S(2)}) collective-permute-start(f32[128,128]{1,0:T(8,128)S(1)} %add_add_fusion.1), channel_id=1, source_target_pairs={{0,192},{4,196},{8,200},{12,204},{16,208},{20,212},{24,216},{28,22... | collective-permute-start | bytes 196616 | tf_op jit(solution)/shard_map/ppermute | solution.py:111
  129.2 5.2 %collective-permute-start.23 = (f32[128,128]{1,0:T(8,128)S(1)}, f32[128,128]{1,0:T(8,128)S(1)}, u32[]{:S(2)}, u32[]{:S(2)}) collective-permute-start(f32[128,128]{1,0:T(8,128)S(1)} %add_add_fusion), channel_id=1, source_target_pairs={{0,1},{1,0},{2,3},{3,2},{4,5},{5,4},{6,7},{7,6},{8,9},{9,8},{10,11... | collective-permute-start | bytes 196616 | tf_op jit(solution)/shard_map/ppermute | solution.py:111
  131.7 5.8 %collective-permute-start.24 = (f32[128,128]{1,0:T(8,128)S(1)}, f32[128,128]{1,0:T(8,128)S(1)}, u32[]{:S(2)}, u32[]{:S(2)}) collective-permute-start(f32[128,128]{1,0:T(8,128)S(1)} %add_add_fusion), channel_id=1, source_target_pairs={{0,2},{1,3},{2,0},{3,1},{4,6},{5,7},{6,4},{7,5},{8,10},{9,11},{10,... | collective-permute-start | bytes 196616 | tf_op jit(solution)/shard_map/ppermute | solution.py:111
  133.4 5.5 %collective-permute-start.25 = (f32[128,128]{1,0:T(8,128)S(1)}, f32[128,128]{1,0:T(8,128)S(1)}, u32[]{:S(2)}, u32[]{:S(2)}) collective-permute-start(f32[128,128]{1,0:T(8,128)S(1)} %add_add_fusion), channel_id=1, source_target_pairs={{0,3},{1,2},{2,1},{3,0},{4,7},{5,6},{6,5},{7,4},{8,11},{9,10},{10,... | collective-permute-start | bytes 196616 | tf_op jit(solution)/shard_map/ppermute | solution.py:111
  (6 other events, 50.2 us)
